TPU v7x, 128 devices: a whole 4x4x4 slice. The times are simulated.
128 devices in a mesh: row: 16 (over y_lo, x, core), col: 8 (over z, y_hi).
Axes of the slice: x: 4, y: 4 (y_hi: 2, y_lo: 2; y = y_hi * 2 + y_lo), z: 4, core: 2. Of those that a mesh axis runs over, the one named last changes fastest.
Arguments:
- gate_feats: bfloat16 [16, 8, 1024, 256], P('row', 'col'), may hold values from -6 to 6
- adjacency: int32 [16, 8, 8, 5, 128, 128], P('row', 'col'), may hold values 0 or 1
- gate_count: int32 [16, 8], P('row', 'col'), may hold values from 128 to 1024, as said below
- membership: int32 [16, 8, 512, 1024], P('row', 'col'), may hold values 0 or 1
- tok_count: int32 [16, 8], P('row', 'col'), may hold values from 64 to 512, as said below
- w_msg: bfloat16 [256, 256], replicated, may hold values from -0.375 to 0.375
- w_query: bfloat16 [256, 256], replicated, may hold values from -0.375 to 0.375
- w_key: bfloat16 [256, 256], replicated, may hold values from -0.375 to 0.375
- w_value: bfloat16 [256, 256], replicated, may hold values from -0.375 to 0.375
- w_out: bfloat16 [256, 256], replicated, may hold values from -0.375 to 0.375
- w_score: bfloat16 [256], replicated, may hold values from -0.375 to 0.375
- cotangent: float32 [16, 8, 512], P('row', 'col'), may hold values from -6 to 6
Outputs:
- value_out: float32 [16, 8, 512], P('row', 'col')
- g_msg: float32 [256, 256], replicated
- g_query: float32 [256, 256], replicated
- g_key: float32 [256, 256], replicated
- g_value: float32 [256, 256], replicated
- g_out: float32 [256, 256], replicated
- g_score: float32 [256], replicated
Inputs may be any that keep to these rules, and one draw needn't show every extreme that they name: `gate_count`: some tile is full in every draw. `tok_count`: some tile is full in every draw.
All inputs are finite; a program needn't handle non-finite values. No bound on the sum of `adjacency` or of `membership` on one device may be relied on, other than what follows from the above.
Results may differ from a plain program's by a relative error of at most 0.017.
Values may be sent and summed in bfloat16 or wider, within the bound.
No kernel may reach another device: no remote copies, remote signals or barrier semaphores. Data moves between devices by JAX's collectives and lax.ppermute only.
A program may use at most 128 MiB of HBM per device.

v0:
```python
import math

import jax
import jax.numpy as jnp
from jax import lax
from jax.experimental import pallas as pl
from jax.experimental.pallas import tpu as pltpu
from jax.sharding import PartitionSpec as P

H = 256
HEADS = 2
HD = 128
BLK = 128
NB = 8
NT = 512


EPS = 1e-06
SHIFT = math.log(NT)

def _nt(a, b):
    return lax.dot_general(a, b, (((1,), (1,)), ((), ())), preferred_element_type=jnp.float32)

def _nn(a, b):
    return jnp.dot(a, b, preferred_element_type=jnp.float32)

def _probs(q, k):
    return jax.nn.sigmoid(_nt(q, k) / math.sqrt(HD) - SHIFT)

def _fwd_kernel(q_ref, k_ref, v_ref, o_ref, acc_ref):
    blocks = k_ref.shape[0] // NT
    acc_ref[...] = jnp.zeros_like(acc_ref)
    def step(j, carry):
        rows = pl.ds(pl.multiple_of(j * NT, NT), NT)
        for h in range(HEADS):
            cols = slice(h * HD, (h + 1) * HD)
            w = _probs(q_ref[:, cols], k_ref[rows, cols]).astype(jnp.bfloat16)
            acc_ref[:, cols] += _nn(w, v_ref[rows, cols])
        return carry
    lax.fori_loop(0, blocks, step, 0)
    o_ref[...] = acc_ref[...].astype(o_ref.dtype)

def _gq_kernel(q_ref, g_ref, k_ref, v_ref, o_ref, acc_ref):
    blocks = k_ref.shape[0] // NT
    acc_ref[...] = jnp.zeros_like(acc_ref)
    def step(j, carry):
        rows = pl.ds(pl.multiple_of(j * NT, NT), NT)
        for h in range(HEADS):
            cols = slice(h * HD, (h + 1) * HD)
            k = k_ref[rows, cols]
            p = _probs(q_ref[:, cols], k)
            dp = _nt(g_ref[:, cols], v_ref[rows, cols])
            ds = (dp * p * (1.0 - p) / math.sqrt(HD)).astype(jnp.bfloat16)
            acc_ref[:, cols] += _nn(ds, k)
        return carry
    lax.fori_loop(0, blocks, step, 0)
    o_ref[...] = acc_ref[...].astype(o_ref.dtype)

def _gkv_kernel(q_ref, g_ref, k_ref, v_ref, dk_ref, dv_ref, acck_ref, accv_ref):
    blocks = q_ref.shape[0] // NT
    acck_ref[...] = jnp.zeros_like(acck_ref)
    accv_ref[...] = jnp.zeros_like(accv_ref)
    def step(i, carry):
        rows = pl.ds(pl.multiple_of(i * NT, NT), NT)
        for h in range(HEADS):
            cols = slice(h * HD, (h + 1) * HD)
            q = q_ref[rows, cols]
            g = g_ref[rows, cols]
            p = _probs(k_ref[:, cols], q)
            w = p.astype(jnp.bfloat16)
            dp = _nt(v_ref[:, cols], g)
            ds = (dp * p * (1.0 - p) / math.sqrt(HD)).astype(jnp.bfloat16)
            acck_ref[:, cols] += _nn(ds, q)
            accv_ref[:, cols] += _nn(w, g)
        return carry
    lax.fori_loop(0, blocks, step, 0)
    dk_ref[...] = acck_ref[...].astype(dk_ref.dtype)
    dv_ref[...] = accv_ref[...].astype(dv_ref.dtype)

def attend_fwd(q, k_all, v_all):
    return pl.pallas_call(_fwd_kernel, out_shape=jax.ShapeDtypeStruct(q.shape, jnp.bfloat16),
        scratch_shapes=[pltpu.VMEM(q.shape, jnp.float32)])(q, k_all, v_all)

def attend_gq(q, g, k_all, v_all):
    return pl.pallas_call(_gq_kernel, out_shape=jax.ShapeDtypeStruct(q.shape, jnp.bfloat16),
        scratch_shapes=[pltpu.VMEM(q.shape, jnp.float32)])(q, g, k_all, v_all)

def attend_gkv(q_all, g_all, k, v):
    sh = jax.ShapeDtypeStruct(k.shape, jnp.bfloat16)
    return pl.pallas_call(_gkv_kernel, out_shape=(sh, sh),
        scratch_shapes=[pltpu.VMEM(k.shape, jnp.float32), pltpu.VMEM(k.shape, jnp.float32)],)(q_all, g_all, k, v)


def with_halo(array, sides, width):
    for axis, dim in sides:
        size, length = (lax.axis_size(axis), array.shape[dim])
        up = [(i, (i + 1) % size) for i in range(size - 1)]
        down = [(j, i) for i, j in up]
        last = lax.slice_in_dim(array, length - width, length, axis=dim)
        first = lax.slice_in_dim(array, 0, width, axis=dim)
        before = lax.ppermute(last, axis, up)
        after = lax.ppermute(first, axis, down)
        array = jnp.concatenate([before, array, after], axis=dim)
    return array


def gather_tiles(rows_in, axis):
    size = lax.axis_size(axis)
    copies = jnp.broadcast_to(rows_in[None], (size,) + rows_in.shape)
    return lax.all_to_all(copies, axis, 0, 0, tiled=True)


def all_reduce_a2a(flat, axes):
    size = 1
    for axis in axes:
        size *= lax.axis_size(axis)
    chunks = lax.all_to_all(flat.reshape(size, -1), axes, 0, 0, tiled=True)
    total = jnp.sum(chunks, axis=0, keepdims=True)
    copies = jnp.broadcast_to(total, chunks.shape)
    return lax.all_to_all(copies, axes, 0, 0, tiled=True).reshape(-1)


def silu_grad(preact):
    sigmoid_val = jax.nn.sigmoid(preact)
    return sigmoid_val * (1.0 + preact * (1.0 - sigmoid_val))


def rms_forward(values_in):
    rscale = lax.rsqrt(jnp.mean(values_in * values_in, axis=-1, keepdims=True) + EPS)
    return (values_in * rscale, rscale)


def rms_backward(grad_in, normed, rscale):
    return rscale * (grad_in - normed * jnp.mean(grad_in * normed, axis=-1, keepdims=True))


def split_heads(rows_in):
    return rows_in.reshape(rows_in.shape[0], HEADS, HD)


def score_probs(query_rows, key_rows):
    scores = jnp.einsum(
        "qhd,khd->hqk",
        split_heads(query_rows),
        split_heads(key_rows),
        preferred_element_type=jnp.float32,
    )
    return jax.nn.sigmoid(scores / math.sqrt(HD) - math.log(NT))


def project(rows_in, weight_mat):
    return jnp.dot(rows_in, weight_mat, preferred_element_type=jnp.float32).astype(jnp.bfloat16)


def body(
    gate_feats,
    adjacency,
    gate_count,
    membership,
    tok_count,
    w_msg,
    w_query,
    w_key,
    w_value,
    w_out,
    w_score,
    cotangent,
):
    gate_total = gate_feats.shape[2]
    gate_live = (jnp.arange(gate_total) < gate_count[0, 0]).astype(jnp.float32)
    live_feats = (gate_feats[0, 0].astype(jnp.float32) * gate_live[:, None]).astype(jnp.bfloat16)
    by_row = with_halo(live_feats[None], (("row", 0),), 1)
    by_col = with_halo(live_feats[None], (("col", 0),), 1)
    sources = jnp.stack([live_feats, by_row[0], by_row[2], by_col[0], by_col[2]], axis=0)
    sources = sources.reshape(5, NB, BLK, H)
    adj_tiles = adjacency[0, 0]
    aggregate = jnp.einsum(
        "bkij,kbjh->bih",
        adj_tiles.astype(jnp.bfloat16),
        sources,
        preferred_element_type=jnp.float32,
    )
    degree = jnp.sum(adj_tiles, axis=(1, 3)).astype(jnp.float32)
    message = (aggregate / (degree[:, :, None] + 1.0)).astype(jnp.bfloat16).reshape(gate_total, H)
    preact = jnp.dot(message, w_msg, preferred_element_type=jnp.float32)
    hidden = (gate_live[:, None] * (live_feats.astype(jnp.float32) + jax.nn.silu(preact))).astype(
        jnp.bfloat16
    )
    member_rows = membership[0, 0].astype(jnp.bfloat16)
    member_count = jnp.sum(membership[0, 0], axis=1).astype(jnp.float32)[:, None]
    pooled = jnp.dot(member_rows, hidden, preferred_element_type=jnp.float32) / (member_count + 1.0)
    normed, rscale = rms_forward(pooled)
    token_live = (jnp.arange(NT) < tok_count[0, 0]).astype(jnp.float32)[:, None]
    tokens = (token_live * normed).astype(jnp.bfloat16)

    tokens_all = gather_tiles(tokens, "col").reshape(-1, H)
    query_all = project(tokens_all, w_query)
    key_all = project(tokens_all, w_key)
    value_all = project(tokens_all, w_value)
    query_own = project(tokens, w_query)
    key_own = project(tokens, w_key)
    value_own = project(tokens, w_value)

    attended = attend_fwd(query_own, key_all, value_all)
    proj = jnp.dot(attended, w_out, preferred_element_type=jnp.float32)
    pnormed, pscale = rms_forward(proj)
    mixed = tokens.astype(jnp.float32) + pnormed
    score_w = w_score.astype(jnp.float32)
    value_out = token_live[:, 0] * jnp.sum(mixed * score_w, axis=1)
    loss_weight = 1.0 / math.sqrt(lax.axis_size("row") * lax.axis_size("col") * NT)
    grad_value = token_live[:, 0] * cotangent[0, 0] * loss_weight
    g_score = jnp.sum(mixed * grad_value[:, None], axis=0)
    grad_mixed = grad_value[:, None] * score_w
    grad_proj = rms_backward(grad_mixed, pnormed, pscale).astype(jnp.bfloat16)
    g_out = jnp.einsum("nh,ne->he", attended, grad_proj, preferred_element_type=jnp.float32)
    grad_attn = jnp.dot(grad_proj, w_out.T, preferred_element_type=jnp.float32).astype(jnp.bfloat16)

    grad_attn_all = gather_tiles(grad_attn, "col").reshape(-1, H)

    grad_query = attend_gq(query_own, grad_attn, key_all, value_all)
    grad_key, grad_val = attend_gkv(query_all, grad_attn_all, key_own, value_own)

    g_query = jnp.einsum("nh,ne->he", tokens, grad_query, preferred_element_type=jnp.float32)
    g_key = jnp.einsum("nh,ne->he", tokens, grad_key, preferred_element_type=jnp.float32)
    g_value = jnp.einsum("nh,ne->he", tokens, grad_val, preferred_element_type=jnp.float32)
    grad_tokens = grad_mixed + jnp.dot(grad_query, w_query.T, preferred_element_type=jnp.float32)
    grad_tokens = grad_tokens + jnp.dot(grad_key, w_key.T, preferred_element_type=jnp.float32)
    grad_tokens = grad_tokens + jnp.dot(grad_val, w_value.T, preferred_element_type=jnp.float32)
    grad_pooled = rms_backward(token_live * grad_tokens, normed, rscale)
    grad_scaled = (grad_pooled / (member_count + 1.0)).astype(jnp.bfloat16)
    grad_hidden = jnp.einsum(
        "ng,nh->gh", member_rows, grad_scaled, preferred_element_type=jnp.float32
    )
    grad_pre = (gate_live[:, None] * grad_hidden * silu_grad(preact)).astype(jnp.bfloat16)
    g_msg = jnp.einsum("gh,ge->he", message, grad_pre, preferred_element_type=jnp.float32)

    flat = jnp.concatenate(
        [g.reshape(-1) for g in (g_msg, g_query, g_key, g_value, g_out, g_score)]
    )
    devices = lax.axis_size("row") * lax.axis_size("col")
    pad = (-flat.shape[0]) % devices
    summed = all_reduce_a2a(jnp.pad(flat, (0, pad)), ("row", "col"))
    sq = H * H
    outs = [summed[i * sq:(i + 1) * sq].reshape(H, H) for i in range(5)]
    g_score_sum = summed[5 * sq:5 * sq + H]
    return (value_out[None, None], *outs, g_score_sum)


def solution(mesh):
    placed = (
        P("row", "col", None, None),
        P("row", "col", None, None, None, None),
        P("row", "col"),
        P("row", "col", None, None),
        P("row", "col"),
        P(),
        P(),
        P(),
        P(),
        P(),
        P(),
        P("row", "col", None),
    )
    return jax.shard_map(
        body,
        mesh=mesh,
        in_specs=placed,
        out_specs=(P("row", "col", None), P(), P(), P(), P(), P(), P()),
        check_vma=False,
    )
```

profile of v0, /device:TPU:0, one launch (start us, length us, event | category | flops | bytes accessed | tf_op | source)
XLA Modules:
  0.0 233.0 jit_solution(14956810910716209380)
XLA Ops:
  2.6 2.2 collective-permute-start
  6.1 6.4 %collective-permute-start.2 = (bf16[1,1024,256]{2,1,0:T(8,128)(2,1)S(1)}, bf16[1,1024,256]{2,1,0:T(8,128)(2,1)}, u32[]{:S(2)}, u32[]{:S(2)}) collective-permute-start(bf16[1,1024,256]{2,1,0:T(8,128)(2,1)S(1)} %fusion.11), channel_id=1, source_target_pairs={{0,1},{1,2},{2,3},{3,4},{4,5},{5,6},{6,7},{8,9},{9,10},{10,11},{11... | collective-permute-start | bytes 1572872 | tf_op jit(solution)/shard_map/ppermute | solution.py:101
  13.9 2.1 fusion.22
  15.9 2.0 reduce_sum.83
  18.8 2.0 constant_dynamic-update-slice_fusion.3
  20.8 1.9 constant_dynamic-update-slice_fusion.2
  22.7 3.0 %collective-permute-done.2 = bf16[1,1024,256]{2,1,0:T(8,128)(2,1)} collective-permute-done((bf16[1,1024,256]{2,1,0:T(8,128)(2,1)S(1)}, bf16[1,1024,256]{2,1,0:T(8,128)(2,1)}, u32[]{:S(2)}, u32[]{:S(2)}) %collective-permute-start.2) | collective-permute-done | bytes 524320 | tf_op jit(solution)/shard_map/ppermute | solution.py:101
  25.7 1.9 constant_dynamic-update-slice_fusion.1
  27.6 12.7 %collective-permute-done.3 = bf16[1,1024,256]{2,1,0:T(8,128)(2,1)S(1)} collective-permute-done((bf16[1,1024,256]{2,1,0:T(8,128)(2,1)S(1)}, bf16[1,1024,256]{2,1,0:T(8,128)(2,1)S(1)}, u32[]{:S(2)}, u32[]{:S(2)}) %collective-permute-start.3) | collective-permute-done | bytes 524320 | tf_op jit(solution)/shard_map/ppermute | solution.py:102
  41.2 2.5 %divide_convert_fusion = bf16[8,256,128]{1,2,0:T(8,128)(2,1)S(1)} fusion(bf16[5,8,128,256]{3,2,0,1:T(8,128)(2,1)} %constant_dynamic-update-slice_fusion, s32[1,1,8,5,128,128]{5,4,3,2,1,0:T(8,128)S(1)} %copy-done.1, f32[8,128]{1,0:T(8,128)S(1)} %convert_add_fusion.1), kind=kOutput, calls=%fused_computation.37 | convolution fusion | flops 336723968 | bytes 5771264 | tf_op jit(solution)/shard_map/bkij,kbjh->bih/dot_general | solution.py:177
  46.7 6.4 %all-to-all-start = ((bf16[8,512,256]{2,1,0:T(8,128)(2,1)}), bf16[8,512,256]{2,1,0:T(8,128)(2,1)S(1)}, u32[]{:S(2)}, u32[]{:S(2)}) async-start(bf16[8,512,256]{2,1,0:T(8,128)(2,1)} %broadcast_in_dim.6), calls=%async_computation | async-start | bytes 4194304 | tf_op jit(solution)/shard_map/all_to_all | solution.py:110
  54.7 27.2 %all-to-all-done = bf16[8,512,256]{2,1,0:T(8,128)(2,1)S(1)} async-done(((bf16[8,512,256]{2,1,0:T(8,128)(2,1)}), bf16[8,512,256]{2,1,0:T(8,128)(2,1)S(1)}, u32[]{:S(2)}, u32[]{:S(2)}) %all-to-all-start) | async-done | bytes 2097184 | tf_op jit(solution)/shard_map/all_to_all | solution.py:110
  81.9 2.0 convolution_convert_fusion.2.k_ref
  84.0 2.1 convolution_convert_fusion.1.v_ref
  86.0 9.1 %shard_map.171 = bf16[512,256]{1,0:T(8,128)(2,1)} custom-call(bf16[512,256]{1,0:T(8,128)(2,1)} %convolution_convert_fusion.6.q_ref, bf16[4096,256]{1,0:T(8,128)(2,1)} %convolution_convert_fusion.2.k_ref, bf16[4096,256]{1,0:T(8,128)(2,1)} %convolution_convert_fusion.1.v_ref), custom_call_target="tpu_custom_call" | custom-call | tf_op jit(solution)/shard_map/pallas_call | solution.py:81
  102.6 4.5 %all-to-all-start.1 = ((bf16[8,512,256]{2,1,0:T(8,128)(2,1)}), bf16[8,512,256]{2,1,0:T(8,128)(2,1)}, u32[]{:S(2)}, u32[]{:S(2)}) async-start(bf16[8,512,256]{2,1,0:T(8,128)(2,1)} %broadcast_in_dim.7), calls=%async_computation.1 | async-start | bytes 4194304 | tf_op jit(solution)/shard_map/all_to_all | solution.py:110
  107.1 1.9 convolution_convert_fusion.4.k_ref
  110.0 12.4 %shard_map.172 = bf16[512,256]{1,0:T(8,128)(2,1)} custom-call(bf16[512,256]{1,0:T(8,128)(2,1)} %convolution_convert_fusion.6.q_ref, bf16[512,256]{1,0:T(8,128)(2,1)} %copy-done.10, bf16[4096,256]{1,0:T(8,128)(2,1)} %convolution_convert_fusion.2.k_ref, bf16[4096,256]{1,0:T(8,128)(2,1)} %convolution_convert_fusion.1.v_ref), custom_call_target="tpu_custom_call" | custom-call | tf_op jit(solution)/shard_map/pallas_call | solution.py:85
  126.9 2.0 convolution_convert_fusion.q_ref
  128.9 5.9 %all-to-all-done.1 = bf16[8,512,256]{2,1,0:T(8,128)(2,1)} async-done(((bf16[8,512,256]{2,1,0:T(8,128)(2,1)}), bf16[8,512,256]{2,1,0:T(8,128)(2,1)}, u32[]{:S(2)}, u32[]{:S(2)}) %all-to-all-start.1) | async-done | bytes 2097184 | tf_op jit(solution)/shard_map/all_to_all | solution.py:110
  134.8 15.3 %shard_map.173 = (bf16[512,256]{1,0:T(8,128)(2,1)}, bf16[512,256]{1,0:T(8,128)(2,1)}) custom-call(bf16[4096,256]{1,0:T(8,128)(2,1)} %convolution_convert_fusion.q_ref, bf16[4096,256]{1,0:T(8,128)(2,1)} %bitcast.20.g_ref, bf16[512,256]{1,0:T(8,128)(2,1)} %convolution_convert_fusion.4.k_ref, bf16[512,256]{1,0:T(8,128)(2,1)} %convolution_convert_fusion.3.v_ref), custom_call_target="tpu_custom_call" | custom-call | tf_op jit(solution)/shard_map/pallas_call | solution.py:90
  150.1 1.9 convolution_bitcast_fusion.3
  154.7 2.5 %fusion.7 = f32[32,2,8,128]{3,2,1,0:T(8,128)S(1)} fusion(bf16[1024,256]{1,0:T(8,128)(2,1)} %bitcast.138, f32[1024,256]{1,0:T(8,128)} %copy-done.14, f32[1024]{0:T(1024)S(1)} %copy-done.18, s32[1,1,512,1024]{3,2,1,0:T(8,128)S(1)} %copy-done.4, f32[512,256]{0,1:T(8,128)} %get-tuple-element.24, f32[256,512]{1,0:T(8,128)S(1)} %get-tuple-element.20, ...), kind=kOutput, calls=%fused_computation.24 | convolution fusion | flops 406585344 | bytes 4990976 | tf_op jit(solution)/shard_map/gh,ge->he/dot_general | solution.py:235
  158.4 3.0 %all_to_all.21 = f32[128,1,2562]{2,1,0:T(1,128)} reshape(f32[327936]{0:T(1024)S(1)} %constant_dynamic-update-slice_fusion.5) | data formatting | bytes 2623488 | tf_op jit(solution)/shard_map/all_to_all | solution.py:117
  161.3 30.1 %all_to_all.26 = f32[128,1,2562]{2,1,0:T(1,128)S(1)} all-to-all(f32[128,1,2562]{2,1,0:T(1,128)} %all_to_all.21), channel_id=1, replica_groups=mesh['row'=16,'col'=8] {'row','col'}, dimensions={0} | all-to-all | bytes 2623488 | tf_op jit(solution)/shard_map/all_to_all | solution.py:117
  192.3 1.8 broadcast_in_dim.8
  194.0 6.1 %all-to-all-start.3 = ((f32[128,1,2562]{2,1,0:T(1,128)}), f32[128,1,2562]{2,1,0:T(1,128)}, u32[]{:S(2)}, u32[]{:S(2)}) async-start(f32[128,1,2562]{2,1,0:T(1,128)} %broadcast_in_dim.8), calls=%async_computation.3 | async-start | bytes 2752512 | tf_op jit(solution)/shard_map/all_to_all | solution.py:120
  200.8 20.1 %all-to-all-done.3 = f32[128,1,2562]{2,1,0:T(1,128)} async-done(((f32[128,1,2562]{2,1,0:T(1,128)}), f32[128,1,2562]{2,1,0:T(1,128)}, u32[]{:S(2)}, u32[]{:S(2)}) %all-to-all-start.3) | async-done | bytes 1311776 | tf_op jit(solution)/shard_map/all_to_all | solution.py:120
  220.9 4.6 %reduce.4 = f32[128,2562]{1,0:T(8,128)S(1)} reduce(f32[128,1,2562]{2,1,0:T(1,128)} %all-to-all-done.3, f32[]{:T(128)} %constant.29), dimensions={1}, to_apply=%all_to_all.20.reduce_sub_computation | reduce | bytes 2623492 | tf_op jit(solution)/shard_map/all_to_all | solution.py:120
  225.5 2.1 slice.25
  227.6 1.8 reshape.215
  229.4 2.3 fusion.55
  (100 shorter events, 28.7 us)
Async XLA Ops:
  0.6 83.3 %copy-start = (bf16[256,256]{1,0:T(8,128)(2,1)S(1)}, bf16[256,256]{1,0:T(8,128)(2,1)}, u32[]{:S(2)}) copy-start(bf16[256,256]{1,0:T(8,128)(2,1)} %param.20) | copy-start | bytes 393220
  1.3 42.6 %copy-start.17 = (f32[1024]{0:T(1024)}, f32[1024]{0:T(1024)S(1)}, u32[]{:S(2)}) copy-start(f32[1024]{0:T(1024)S(1)} %fusion.49) | copy-start | bytes 12292
  2.6 15.3 %copy-start.3 = (s32[1,1,512,1024]{3,2,1,0:T(8,128)S(1)}, s32[1,1,512,1024]{3,2,1,0:T(8,128)}, u32[]{:S(2)}) copy-start(s32[1,1,512,1024]{3,2,1,0:T(8,128)} %param.15) | copy-start | bytes 6291460
  2.6 16.1 %collective-permute-start = (bf16[1,1024,256]{2,1,0:T(8,128)(2,1)S(1)}, bf16[1,1024,256]{2,1,0:T(8,128)(2,1)}, u32[]{:S(2)}, u32[]{:S(2)}) collective-permute-start(bf16[1,1024,256]{2,1,0:T(8,128)(2,1)S(1)} %fusion.11), channel_id=1, source_target_pairs={{0,8},{8,16},{16,24},{24,32},{32,40},{40,48},{48,56},{56,64},{64,7... | collective-permute-start | bytes 1572872 | tf_op jit(solution)/shard_map/ppermute | solution.py:101
  4.8 16.0 %collective-permute-start.1 = (bf16[1,1024,256]{2,1,0:T(8,128)(2,1)S(1)}, bf16[1,1024,256]{2,1,0:T(8,128)(2,1)}, u32[]{:S(2)}, u32[]{:S(2)}) collective-permute-start(bf16[1,1024,256]{2,1,0:T(8,128)(2,1)S(1)} %fusion.11), channel_id=1, source_target_pairs={{8,0},{16,8},{24,16},{32,24},{40,32},{48,40},{56,48},{64,56},{72,6... | collective-permute-start | bytes 1572872 | tf_op jit(solution)/shard_map/ppermute | solution.py:102
  6.1 19.6 %collective-permute-start.2 = (bf16[1,1024,256]{2,1,0:T(8,128)(2,1)S(1)}, bf16[1,1024,256]{2,1,0:T(8,128)(2,1)}, u32[]{:S(2)}, u32[]{:S(2)}) collective-permute-start(bf16[1,1024,256]{2,1,0:T(8,128)(2,1)S(1)} %fusion.11), channel_id=1, source_target_pairs={{0,1},{1,2},{2,3},{3,4},{4,5},{5,6},{6,7},{8,9},{9,10},{10,11},{11... | collective-permute-start | bytes 1572872 | tf_op jit(solution)/shard_map/ppermute | solution.py:101
  12.6 27.7 %collective-permute-start.3 = (bf16[1,1024,256]{2,1,0:T(8,128)(2,1)S(1)}, bf16[1,1024,256]{2,1,0:T(8,128)(2,1)S(1)}, u32[]{:S(2)}, u32[]{:S(2)}) collective-permute-start(bf16[1,1024,256]{2,1,0:T(8,128)(2,1)S(1)} %fusion.11), channel_id=1, source_target_pairs={{1,0},{2,1},{3,2},{4,3},{5,4},{6,5},{7,6},{9,8},{10,9},{11,10},{12... | collective-permute-start | bytes 1572872 | tf_op jit(solution)/shard_map/ppermute | solution.py:102
  18.1 25.9 %copy-start.23 = (f32[512]{0:T(512)}, f32[512]{0:T(512)S(1)}, u32[]{:S(2)}) copy-start(f32[512]{0:T(512)S(1)} %convert_add_fusion.2) | copy-start | bytes 6148
  18.8 22.4 %copy-start.1 = (s32[1,1,8,5,128,128]{5,4,3,2,1,0:T(8,128)S(1)}, s32[1,1,8,5,128,128]{5,4,3,2,1,0:T(8,128)}, u32[]{:S(2)}) copy-start(s32[1,1,8,5,128,128]{5,4,3,2,1,0:T(8,128)} %param.13) | copy-start | bytes 7864324
  41.1 2.5 %copy-start.16 = (bf16[256,256]{1,0:T(8,128)(2,1)S(1)}, bf16[256,256]{1,0:T(8,128)(2,1)}, u32[]{:S(2)}) copy-start(bf16[256,256]{1,0:T(8,128)(2,1)} %param.17) | copy-start | bytes 393220
  41.1 2.8 %copy-start.5 = (bf16[1,1,1024,256]{3,2,1,0:T(8,128)(2,1)S(1)}, bf16[1,1,1024,256]{3,2,1,0:T(8,128)(2,1)}, u32[]{:S(2)}) copy-start(bf16[1,1,1024,256]{3,2,1,0:T(8,128)(2,1)} %param.12) | copy-start | bytes 1572868
  43.6 1.2 copy-start.15
  44.0 1.1 copy-start.14
  46.7 6.4 %copy-start.25 = (bf16[256]{0:T(256)(128)(2,1)S(1)}, bf16[256]{0:T(256)(128)(2,1)}, u32[]{:S(2)}) copy-start(bf16[256]{0:T(256)(128)(2,1)} %param.22) | copy-start | bytes 1540
  46.7 7.0 %copy-start.6 = (bf16[256,256]{1,0:T(8,128)(2,1)S(1)}, bf16[256,256]{1,0:T(8,128)(2,1)}, u32[]{:S(2)}) copy-start(bf16[256,256]{1,0:T(8,128)(2,1)} %param.18) | copy-start | bytes 393220
  46.7 35.2 %copy-start.8 = (bf16[256,256]{1,0:T(8,128)(2,1)S(1)}, bf16[256,256]{1,0:T(8,128)(2,1)}, u32[]{:S(2)}) copy-start(bf16[256,256]{1,0:T(8,128)(2,1)} %param.19) | copy-start | bytes 393220
  46.7 35.2 %all-to-all-start = ((bf16[8,512,256]{2,1,0:T(8,128)(2,1)}), bf16[8,512,256]{2,1,0:T(8,128)(2,1)S(1)}, u32[]{:S(2)}, u32[]{:S(2)}) async-start(bf16[8,512,256]{2,1,0:T(8,128)(2,1)} %broadcast_in_dim.6), calls=%async_computation | async-start | bytes 4194304 | tf_op jit(solution)/shard_map/all_to_all | solution.py:110
  100.4 0.7 copy-start.10
  102.6 32.2 %all-to-all-start.1 = ((bf16[8,512,256]{2,1,0:T(8,128)(2,1)}), bf16[8,512,256]{2,1,0:T(8,128)(2,1)}, u32[]{:S(2)}, u32[]{:S(2)}) async-start(bf16[8,512,256]{2,1,0:T(8,128)(2,1)} %broadcast_in_dim.7), calls=%async_computation.1 | async-start | bytes 4194304 | tf_op jit(solution)/shard_map/all_to_all | solution.py:110
  122.4 4.2 %copy-start.2 = (bf16[512,256]{1,0:T(8,128)(2,1)S(1)}, bf16[512,256]{1,0:T(8,128)(2,1)}, u32[]{:S(2)}) copy-start(bf16[512,256]{1,0:T(8,128)(2,1)} %shard_map.172) | copy-start | bytes 786436
  122.4 4.2 %copy-start.7 = (bf16[256,256]{1,0:T(8,128)(2,1)S(1)}, bf16[256,256]{1,0:T(8,128)(2,1)}, u32[]{:S(2)}) copy-start(bf16[256,256]{1,0:T(8,128)(2,1)} %param.18) | copy-start | bytes 393220
  122.4 4.2 %copy-start.19 = (f32[256]{0:T(256)S(1)}, f32[256]{0:T(256)}, u32[]{:S(2)}) copy-start(f32[256]{0:T(256)} %convert_element_type.172) | copy-start | bytes 3076
  150.1 3.3 %copy-start.9 = (bf16[512,256]{1,0:T(8,128)(2,1)S(1)}, bf16[512,256]{1,0:T(8,128)(2,1)}, u32[]{:S(2)}) copy-start(bf16[512,256]{1,0:T(8,128)(2,1)} %get-tuple-element.10) | copy-start | bytes 786436
  152.0 2.7 %copy-start.4 = (s32[1,1,512,1024]{3,2,1,0:T(8,128)S(1)}, s32[1,1,512,1024]{3,2,1,0:T(8,128)}, u32[]{:S(2)}) copy-start(s32[1,1,512,1024]{3,2,1,0:T(8,128)} %param.15) | copy-start | bytes 6291460
  152.0 2.7 %copy-start.18 = (f32[1024]{0:T(1024)S(1)}, f32[1024]{0:T(1024)}, u32[]{:S(2)}) copy-start(f32[1024]{0:T(1024)} %copy-done.17) | copy-start | bytes 12292
  152.0 2.7 %copy-start.24 = (f32[512]{0:T(512)S(1)}, f32[512]{0:T(512)}, u32[]{:S(2)}) copy-start(f32[512]{0:T(512)} %copy-done.23) | copy-start | bytes 6148
  154.7 2.8 %copy-start.11 = (f32[32,2,8,128]{3,2,1,0:T(8,128)S(1)}, f32[32,2,8,128]{3,2,1,0:T(8,128)}, u32[]{:S(2)}) copy-start(f32[32,2,8,128]{3,2,1,0:T(8,128)} %convolution_bitcast_fusion.3) | copy-start | bytes 786436
  157.3 1.0 copy-start.13
  157.3 1.0 copy-start.12
  157.3 1.0 copy-start.22
  192.2 7.9 %copy-start.20 = (f32[512]{0:T(512)S(1)}, f32[512]{0:T(512)}, u32[]{:S(2)}) copy-start(f32[512]{0:T(512)} %get-tuple-element.12) | copy-start | bytes 6148
  194.0 26.8 %all-to-all-start.3 = ((f32[128,1,2562]{2,1,0:T(1,128)}), f32[128,1,2562]{2,1,0:T(1,128)}, u32[]{:S(2)}, u32[]{:S(2)}) async-start(f32[128,1,2562]{2,1,0:T(1,128)} %broadcast_in_dim.8), calls=%async_computation.3 | async-start | bytes 2752512 | tf_op jit(solution)/shard_map/all_to_all | solution.py:120
  (1 other events, 0.6 us)
where the time goes:
time: 234 us; the launch traced here: 233 us
  waiting for transfers between devices  68.9 us (29%)
  Pallas kernels  36.7 us (16%)
  blocking collectives  30.1 us (13%)
  starting transfers between devices  28.3 us (12%)
  local copies, waits for them, and re-layouts  26.2 us (11%)
  matrix products  26.1 us (11%)
  other arithmetic  14.3 us (6%)
  between operations  2.43 us (1%)
    all_to_all x2, waiting for transfers between devices, gather_tiles(): return lax.all_to_all(copies, axis, 0, 0, tiled=True)  33.1 us
    all_to_all x1, blocking collectives, all_reduce_a2a(): chunks = lax.all_to_all(flat.reshape(size, -1), axes, 0, 0, tiled=True)  30.1 us
    all_to_all x1, waiting for transfers between devices, all_reduce_a2a(): return lax.all_to_all(copies, axes, 0, 0, tiled=True).reshape(-1)  20.1 us
    pallas_call x1, Pallas kernels, attend_gkv(): pl.pallas_call(_gkv_kernel, out_shape=(sh, sh), scratch_shapes=[pltpu.VME...  15.3 us
    ppermute x2, waiting for transfers between devices, with_halo(): after = lax.ppermute(first, axis, down)  12.7 us
    pallas_call x1, Pallas kernels, attend_gq(): pl.pallas_call(_gq_kernel, out_shape=jax.ShapeDtypeStruct(q.shape, jnp.bf...  12.4 us
    all_to_all x2, starting transfers between devices, gather_tiles(): return lax.all_to_all(copies, axis, 0, 0, tiled=True)  10.9 us
    unnamed x65, local copies, waits for them, and re-layouts  10 us
  transfers between devices with their start and end apart: 7, of which 5 were waited for; matrix products, arithmetic and copies ran while one was open for 9% of the time, Pallas kernels for 5%

commit v1 on v0

--- a/solution.py
+++ b/solution.py
@@ -24,8 +24,8 @@
 def _nn(a, b):
     return jnp.dot(a, b, preferred_element_type=jnp.float32)
 
-def _probs(q, k):
-    return jax.nn.sigmoid(_nt(q, k) / math.sqrt(HD) - SHIFT)
+def _half_tanh(q, k):
+    return jnp.tanh(_nt(q, k) * (0.5 / math.sqrt(HD)) - 0.5 * SHIFT)
 
 def _fwd_kernel(q_ref, k_ref, v_ref, o_ref, acc_ref):
     blocks = k_ref.shape[0] // NT
@@ -34,7 +34,8 @@
         rows = pl.ds(pl.multiple_of(j * NT, NT), NT)
         for h in range(HEADS):
             cols = slice(h * HD, (h + 1) * HD)
-            w = _probs(q_ref[:, cols], k_ref[rows, cols]).astype(jnp.bfloat16)
+            t = _half_tanh(q_ref[:, cols], k_ref[rows, cols])
+            w = (0.5 * t + 0.5).astype(jnp.bfloat16)
             acc_ref[:, cols] += _nn(w, v_ref[rows, cols])
         return carry
     lax.fori_loop(0, blocks, step, 0)
@@ -48,9 +49,9 @@
         for h in range(HEADS):
             cols = slice(h * HD, (h + 1) * HD)
             k = k_ref[rows, cols]
-            p = _probs(q_ref[:, cols], k)
+            t = _half_tanh(q_ref[:, cols], k)
             dp = _nt(g_ref[:, cols], v_ref[rows, cols])
-            ds = (dp * p * (1.0 - p) / math.sqrt(HD)).astype(jnp.bfloat16)
+            ds = (dp * (1.0 - t * t) * (0.25 / math.sqrt(HD))).astype(jnp.bfloat16)
             acc_ref[:, cols] += _nn(ds, k)
         return carry
     lax.fori_loop(0, blocks, step, 0)
@@ -66,10 +67,10 @@
             cols = slice(h * HD, (h + 1) * HD)
             q = q_ref[rows, cols]
             g = g_ref[rows, cols]
-            p = _probs(k_ref[:, cols], q)
-            w = p.astype(jnp.bfloat16)
+            t = _half_tanh(k_ref[:, cols], q)
+            w = (0.5 * t + 0.5).astype(jnp.bfloat16)
             dp = _nt(v_ref[:, cols], g)
-            ds = (dp * p * (1.0 - p) / math.sqrt(HD)).astype(jnp.bfloat16)
+            ds = (dp * (1.0 - t * t) * (0.25 / math.sqrt(HD))).astype(jnp.bfloat16)
             acck_ref[:, cols] += _nn(ds, q)
             accv_ref[:, cols] += _nn(w, g)
         return carry
@@ -91,17 +92,10 @@
         scratch_shapes=[pltpu.VMEM(k.shape, jnp.float32), pltpu.VMEM(k.shape, jnp.float32)],)(q_all, g_all, k, v)
 
 
-def with_halo(array, sides, width):
-    for axis, dim in sides:
-        size, length = (lax.axis_size(axis), array.shape[dim])
-        up = [(i, (i + 1) % size) for i in range(size - 1)]
-        down = [(j, i) for i, j in up]
-        last = lax.slice_in_dim(array, length - width, length, axis=dim)
-        first = lax.slice_in_dim(array, 0, width, axis=dim)
-        before = lax.ppermute(last, axis, up)
-        after = lax.ppermute(first, axis, down)
-        array = jnp.concatenate([before, array, after], axis=dim)
-    return array
+def from_neighbour(array, axis, step):
+    size = lax.axis_size(axis)
+    pairs = [(i, i + step) for i in range(size) if 0 <= i + step < size]
+    return lax.ppermute(array, axis, pairs)
 
 
 def gather_tiles(rows_in, axis):
@@ -110,14 +104,14 @@
     return lax.all_to_all(copies, axis, 0, 0, tiled=True)
 
 
-def all_reduce_a2a(flat, axes):
+def all_reduce_a2a(rows_in, axes):
     size = 1
     for axis in axes:
         size *= lax.axis_size(axis)
-    chunks = lax.all_to_all(flat.reshape(size, -1), axes, 0, 0, tiled=True)
+    chunks = lax.all_to_all(rows_in.reshape(size, -1, rows_in.shape[1]), axes, 0, 0, tiled=True)
     total = jnp.sum(chunks, axis=0, keepdims=True)
     copies = jnp.broadcast_to(total, chunks.shape)
-    return lax.all_to_all(copies, axes, 0, 0, tiled=True).reshape(-1)
+    return lax.all_to_all(copies, axes, 0, 0, tiled=True).reshape(rows_in.shape)
 
 
 def silu_grad(preact):
@@ -169,16 +163,22 @@
     gate_total = gate_feats.shape[2]
     gate_live = (jnp.arange(gate_total) < gate_count[0, 0]).astype(jnp.float32)
     live_feats = (gate_feats[0, 0].astype(jnp.float32) * gate_live[:, None]).astype(jnp.bfloat16)
-    by_row = with_halo(live_feats[None], (("row", 0),), 1)
-    by_col = with_halo(live_feats[None], (("col", 0),), 1)
-    sources = jnp.stack([live_feats, by_row[0], by_row[2], by_col[0], by_col[2]], axis=0)
-    sources = sources.reshape(5, NB, BLK, H)
+    sources = (
+        live_feats,
+        from_neighbour(live_feats, "row", 1),
+        from_neighbour(live_feats, "row", -1),
+        from_neighbour(live_feats, "col", 1),
+        from_neighbour(live_feats, "col", -1),
+    )
     adj_tiles = adjacency[0, 0]
-    aggregate = jnp.einsum(
-        "bkij,kbjh->bih",
-        adj_tiles.astype(jnp.bfloat16),
-        sources,
-        preferred_element_type=jnp.float32,
+    aggregate = sum(
+        jnp.einsum(
+            "bij,bjh->bih",
+            adj_tiles[:, k].astype(jnp.bfloat16),
+            src.reshape(NB, BLK, H),
+            preferred_element_type=jnp.float32,
+        )
+        for k, src in enumerate(sources)
     )
     degree = jnp.sum(adj_tiles, axis=(1, 3)).astype(jnp.float32)
     message = (aggregate / (degree[:, :, None] + 1.0)).astype(jnp.bfloat16).reshape(gate_total, H)
@@ -234,15 +234,15 @@
     grad_pre = (gate_live[:, None] * grad_hidden * silu_grad(preact)).astype(jnp.bfloat16)
     g_msg = jnp.einsum("gh,ge->he", message, grad_pre, preferred_element_type=jnp.float32)
 
-    flat = jnp.concatenate(
-        [g.reshape(-1) for g in (g_msg, g_query, g_key, g_value, g_out, g_score)]
-    )
     devices = lax.axis_size("row") * lax.axis_size("col")
-    pad = (-flat.shape[0]) % devices
-    summed = all_reduce_a2a(jnp.pad(flat, (0, pad)), ("row", "col"))
-    sq = H * H
-    outs = [summed[i * sq:(i + 1) * sq].reshape(H, H) for i in range(5)]
-    g_score_sum = summed[5 * sq:5 * sq + H]
+    grads = [g_msg, g_query, g_key, g_value, g_out, g_score[None]]
+    used = 5 * H + 1
+    per_device = -(-used // devices)
+    per_device = -(-per_device // 8) * 8
+    grads.append(jnp.zeros((per_device * devices - used, H), jnp.float32))
+    summed = all_reduce_a2a(jnp.concatenate(grads, axis=0), ("row", "col"))
+    outs = [summed[i * H:(i + 1) * H] for i in range(5)]
+    g_score_sum = summed[5 * H]
     return (value_out[None, None], *outs, g_score_sum)
 
 

time: 234 us -> 236 us (level)
  local copies, waits for them, and re-layouts: 26.2 us -> 12.8 us
  starting transfers between devices: 28.3 us -> 38.4 us
  matrix products: 26.1 us -> 35.3 us
  blocking collectives: 30.1 us -> 34.2 us
  other arithmetic: 14.3 us -> 10.6 us
  waiting for transfers between devices: 68.9 us -> 65.3 us
    all_to_all x2, starting transfers between devices: 10.9 us -> 21.2 us  [gather_tiles(): return lax.all_to_all(copies, axis, 0, 0, tiled=True)]
    ppermute x4, waiting for transfers between devices: 15.7 us -> 7 us  [from_neighbour(): return lax.ppermute(array, axis, pairs)]
    unnamed x65 -> x50, local copies, waits for them, and re-layouts: 10 us -> 1.68 us
    all_to_all x1, waiting for transfers between devices: 20.1 us -> 28.1 us  [all_reduce_a2a(): return lax.all_to_all(copies, axes, 0, 0, tiled=True).reshape(rows_in.shape)]
    concatenate x1, local copies, waits for them, and re-layouts: 0.01 us -> 4.82 us  [body(): summed = all_reduce_a2a(jnp.concatenate(grads, axis=0), ('row', 'col'))]
    all_to_all x1 -> x0, other arithmetic: 4.62 us -> none  [all_reduce_a2a(): return lax.all_to_all(copies, axes, 0, 0, tiled=True).reshape(-1)]
    dot_general x1 -> x5, matrix products: 2.47 us -> 7.02 us  [body(): jnp.einsum('bij,bjh->bih', adj_tiles[:, k].astype(jnp.bfloat16), src.resh...]
    all_to_all x1, blocking collectives: 30.1 us -> 34.2 us  [all_reduce_a2a(): lax.all_to_all(rows_in.reshape(size, -1, rows_in.shape[1]), axes, 0, 0, t...]
  transfers between devices with their start and end apart: 7 -> 7, of which waited for: 5 -> 4; matrix products, arithmetic and copies ran while one was open for 9% -> 9% of each run, Pallas kernels for 5% -> 5%
where the time goes in v1:
time: 236 us; the launch traced here: 235 us
  waiting for transfers between devices  65.3 us (28%)
  starting transfers between devices  38.4 us (16%)
  Pallas kernels  35.6 us (15%)
  matrix products  35.3 us (15%)
  blocking collectives  34.2 us (14%)
  local copies, waits for them, and re-layouts  12.8 us (5%)
  other arithmetic  10.6 us (4%)
  between operations  2.54 us (1%)
    all_to_all x1, blocking collectives, all_reduce_a2a(): lax.all_to_all(rows_in.reshape(size, -1, rows_in.shape[1]), axes, 0, 0, t...  34.2 us
    all_to_all x2, waiting for transfers between devices, gather_tiles(): return lax.all_to_all(copies, axis, 0, 0, tiled=True)  30.2 us
    all_to_all x1, waiting for transfers between devices, all_reduce_a2a(): return lax.all_to_all(copies, axes, 0, 0, tiled=True).reshape(rows_in.shape)  28.1 us
    all_to_all x2, starting transfers between devices, gather_tiles(): return lax.all_to_all(copies, axis, 0, 0, tiled=True)  21.2 us
    pallas_call x1, Pallas kernels, attend_gkv(): pl.pallas_call(_gkv_kernel, out_shape=(sh, sh), scratch_shapes=[pltpu.VME...  14.2 us
    pallas_call x1, Pallas kernels, attend_gq(): pl.pallas_call(_gq_kernel, out_shape=jax.ShapeDtypeStruct(q.shape, jnp.bf...  11.8 us
    ppermute x4, starting transfers between devices, from_neighbour(): return lax.ppermute(array, axis, pairs)  11.5 us
    dot_general x6, matrix products, project(): jnp.dot(rows_in, weight_mat, preferred_element_type=jnp.float32)  9.98 us
  transfers between devices with their start and end apart: 7, of which 4 were waited for; matrix products, arithmetic and copies ran while one was open for 9% of the time, Pallas kernels for 5%

profile of v1, /device:TPU:0, one launch (start us, length us, event | category | flops | bytes accessed | tf_op | source)
XLA Modules:
  0.0 234.8 jit_solution(10512526581410024640)
XLA Ops:
  1.5 2.1 fusion.13
  4.8 6.9 %collective-permute-start.2 = (bf16[1024,256]{1,0:T(8,128)(2,1)}, bf16[1024,256]{1,0:T(8,128)(2,1)}, u32[]{:S(2)}, u32[]{:S(2)}) collective-permute-start(bf16[1024,256]{1,0:T(8,128)(2,1)} %fusion.13), channel_id=1, source_target_pairs={{0,1},{1,2},{2,3},{3,4},{4,5},{5,6},{6,7},{8,9},{9,10},{10,11},{11... | collective-permute-start | bytes 1572872 | tf_op jit(solution)/shard_map/ppermute | solution.py:98
  11.7 2.1 collective-permute-start
  15.1 1.8 reduce_sum.84
  19.3 1.4 fusion.21
  20.7 7.0 %collective-permute-done.3 = bf16[1024,256]{1,0:T(8,128)(2,1)} collective-permute-done((bf16[1024,256]{1,0:T(8,128)(2,1)}, bf16[1024,256]{1,0:T(8,128)(2,1)}, u32[]{:S(2)}, u32[]{:S(2)}) %collective-permute-start.3) | collective-permute-done | bytes 524320 | tf_op jit(solution)/shard_map/ppermute | solution.py:98
  31.8 1.6 fusion.6
  35.0 1.5 broadcast_in_dim.10
  36.5 16.7 %all-to-all-start = ((bf16[8,512,256]{2,1,0:T(8,128)(2,1)}), bf16[8,512,256]{2,1,0:T(8,128)(2,1)S(1)}, u32[]{:S(2)}, u32[]{:S(2)}) async-start(bf16[8,512,256]{2,1,0:T(8,128)(2,1)} %broadcast_in_dim.10), calls=%async_computation | async-start | bytes 4194304 | tf_op jit(solution)/shard_map/all_to_all | solution.py:104
  54.7 26.1 %all-to-all-done = bf16[8,512,256]{2,1,0:T(8,128)(2,1)S(1)} async-done(((bf16[8,512,256]{2,1,0:T(8,128)(2,1)}), bf16[8,512,256]{2,1,0:T(8,128)(2,1)S(1)}, u32[]{:S(2)}, u32[]{:S(2)}) %all-to-all-start) | async-done | bytes 2097184 | tf_op jit(solution)/shard_map/all_to_all | solution.py:104
  80.7 2.0 convolution_convert_fusion.2.k_ref
  82.8 2.1 convolution_convert_fusion.1.v_ref
  84.8 9.5 %shard_map.171 = bf16[512,256]{1,0:T(8,128)(2,1)} custom-call(bf16[512,256]{1,0:T(8,128)(2,1)} %convolution_convert_fusion.6.q_ref, bf16[4096,256]{1,0:T(8,128)(2,1)} %convolution_convert_fusion.2.k_ref, bf16[4096,256]{1,0:T(8,128)(2,1)} %convolution_convert_fusion.1.v_ref), custom_call_target="tpu_custom_call" | custom-call | tf_op jit(solution)/shard_map/pallas_call | solution.py:82
  96.4 1.5 multiply_reduce_fusion
  100.5 1.5 broadcast_in_dim.11
  101.9 4.5 %all-to-all-start.1 = ((bf16[8,512,256]{2,1,0:T(8,128)(2,1)}), bf16[8,512,256]{2,1,0:T(8,128)(2,1)}, u32[]{:S(2)}, u32[]{:S(2)}) async-start(bf16[8,512,256]{2,1,0:T(8,128)(2,1)} %broadcast_in_dim.11), calls=%async_computation.1 | async-start | bytes 4194304 | tf_op jit(solution)/shard_map/all_to_all | solution.py:104
  106.4 1.9 convolution_convert_fusion.4.k_ref
  109.3 11.8 %shard_map.172 = bf16[512,256]{1,0:T(8,128)(2,1)} custom-call(bf16[512,256]{1,0:T(8,128)(2,1)} %convolution_convert_fusion.6.q_ref, bf16[512,256]{1,0:T(8,128)(2,1)} %copy-done.13, bf16[4096,256]{1,0:T(8,128)(2,1)} %convolution_convert_fusion.2.k_ref, bf16[4096,256]{1,0:T(8,128)(2,1)} %convolution_convert_fusion.1.v_ref), custom_call_target="tpu_custom_call" | custom-call | tf_op jit(solution)/shard_map/pallas_call | solution.py:86
  121.1 1.9 fusion.60
  123.1 2.1 convolution_add_fusion.4
  125.2 2.0 fusion.53
  127.2 2.1 convolution_convert_fusion.q_ref
  129.2 4.1 %all-to-all-done.1 = bf16[8,512,256]{2,1,0:T(8,128)(2,1)} async-done(((bf16[8,512,256]{2,1,0:T(8,128)(2,1)}), bf16[8,512,256]{2,1,0:T(8,128)(2,1)}, u32[]{:S(2)}, u32[]{:S(2)}) %all-to-all-start.1) | async-done | bytes 2097184 | tf_op jit(solution)/shard_map/all_to_all | solution.py:104
  133.3 14.2 %shard_map.173 = (bf16[512,256]{1,0:T(8,128)(2,1)}, bf16[512,256]{1,0:T(8,128)(2,1)}) custom-call(bf16[4096,256]{1,0:T(8,128)(2,1)} %convolution_convert_fusion.q_ref, bf16[4096,256]{1,0:T(8,128)(2,1)} %bitcast.22.g_ref, bf16[512,256]{1,0:T(8,128)(2,1)} %convolution_convert_fusion.4.k_ref, bf16[512,256]{1,0:T(8,128)(2,1)} %convolution_convert_fusion.3.v_ref), custom_call_target="tpu_custom_call" | custom-call | tf_op jit(solution)/shard_map/pallas_call | solution.py:91
  147.6 1.9 fusion.61
  153.0 3.3 %fusion.8 = f32[256,256]{1,0:T(8,128)} fusion(bf16[1024,256]{1,0:T(8,128)(2,1)} %bitcast.133, f32[1024,256]{1,0:T(8,128)} %copy-done.14, f32[1024]{0:T(1024)S(1)} %copy-done.18, s32[1,1,512,1024]{3,2,1,0:T(8,128)S(1)} %copy-done.5, f32[512,256]{0,1:T(8,128)} %get-tuple-element.24, f32[256,512]{1,0:T(8,128)S(1)} %get-tuple-element.20, ...), kind=kOutput, calls=%fused_computation.16 | convolution fusion | flops 406585344 | bytes 4990976 | tf_op jit(solution)/shard_map/gh,ge->he/dot_general | solution.py:235
  156.3 4.8 %concatenate.3 = f32[2048,256]{1,0:T(8,128)S(1)} concatenate(f32[256,256]{1,0:T(8,128)} %fusion.8, f32[256,256]{1,0:T(8,128)S(1)} %copy-done.10, f32[256,256]{1,0:T(8,128)} %fusion.61, f32[256,256]{1,0:T(8,128)} %fusion.62, f32[256,256]{1,0:T(8,128)S(1)} %copy-done.11, f32[1,256]{1,0:T(1,128)S(1)} %bitcast.140, f32[767,256]{1,0:T(8,128)S(1)} %broadcast_in_dim.13), dimensions={0} | concatenate | bytes 4194304 | tf_op jit(solution)/shard_map/concatenate | solution.py:243
  161.1 34.2 %all_to_all.20 = f32[128,16,256]{2,1,0:T(8,128)} all-to-all(f32[128,16,256]{2,1,0:T(8,128)S(1)} %bitcast.129), channel_id=1, replica_groups=mesh['row'=16,'col'=8] {'row','col'}, dimensions={0} | all-to-all | bytes 4194304 | tf_op jit(solution)/shard_map/all_to_all | solution.py:111
  195.3 1.8 reduce_sum.92
  197.1 1.6 broadcast_in_dim.14
  198.7 5.7 %all-to-all-start.3 = ((f32[128,16,256]{2,1,0:T(8,128)}), f32[128,16,256]{2,1,0:T(8,128)S(1)}, u32[]{:S(2)}, u32[]{:S(2)}) async-start(f32[128,16,256]{2,1,0:T(8,128)} %broadcast_in_dim.14), calls=%async_computation.3 | async-start | bytes 4194304 | tf_op jit(solution)/shard_map/all_to_all | solution.py:114
  205.0 28.1 %all-to-all-done.3 = f32[128,16,256]{2,1,0:T(8,128)S(1)} async-done(((f32[128,16,256]{2,1,0:T(8,128)}), f32[128,16,256]{2,1,0:T(8,128)S(1)}, u32[]{:S(2)}, u32[]{:S(2)}) %all-to-all-start.3) | async-done | bytes 2097184 | tf_op jit(solution)/shard_map/all_to_all | solution.py:114
  (85 shorter events, 22.6 us)
Async XLA Ops:
  0.6 82.2 %copy-start = (bf16[256,256]{1,0:T(8,128)(2,1)S(1)}, bf16[256,256]{1,0:T(8,128)(2,1)}, u32[]{:S(2)}) copy-start(bf16[256,256]{1,0:T(8,128)(2,1)} %param.20) | copy-start | bytes 393220
  0.6 16.2 %copy-start.1 = (s32[1,1,8,5,128,128]{5,4,3,2,1,0:T(8,128)S(1)}, s32[1,1,8,5,128,128]{5,4,3,2,1,0:T(8,128)}, u32[]{:S(2)}) copy-start(s32[1,1,8,5,128,128]{5,4,3,2,1,0:T(8,128)} %param.13) | copy-start | bytes 7864324
  1.5 32.2 %copy-start.17 = (f32[1024]{0:T(1024)}, f32[1024]{0:T(1024)S(1)}, u32[]{:S(2)}) copy-start(f32[1024]{0:T(1024)S(1)} %fusion.49) | copy-start | bytes 12292
  3.5 24.1 %collective-permute-start.3 = (bf16[1024,256]{1,0:T(8,128)(2,1)}, bf16[1024,256]{1,0:T(8,128)(2,1)}, u32[]{:S(2)}, u32[]{:S(2)}) collective-permute-start(bf16[1024,256]{1,0:T(8,128)(2,1)} %fusion.13), channel_id=1, source_target_pairs={{1,0},{2,1},{3,2},{4,3},{5,4},{6,5},{7,6},{9,8},{10,9},{11,10},{12... | collective-permute-start | bytes 1572872 | tf_op jit(solution)/shard_map/ppermute | solution.py:98
  4.8 24.2 %collective-permute-start.2 = (bf16[1024,256]{1,0:T(8,128)(2,1)}, bf16[1024,256]{1,0:T(8,128)(2,1)}, u32[]{:S(2)}, u32[]{:S(2)}) collective-permute-start(bf16[1024,256]{1,0:T(8,128)(2,1)} %fusion.13), channel_id=1, source_target_pairs={{0,1},{1,2},{2,3},{3,4},{4,5},{5,6},{6,7},{8,9},{9,10},{10,11},{11... | collective-permute-start | bytes 1572872 | tf_op jit(solution)/shard_map/ppermute | solution.py:98
  11.7 18.7 %collective-permute-start = (bf16[1024,256]{1,0:T(8,128)(2,1)}, bf16[1024,256]{1,0:T(8,128)(2,1)}, u32[]{:S(2)}, u32[]{:S(2)}) collective-permute-start(bf16[1024,256]{1,0:T(8,128)(2,1)} %fusion.13), channel_id=1, source_target_pairs={{0,8},{8,16},{16,24},{24,32},{32,40},{40,48},{48,56},{56,64},{64,7... | collective-permute-start | bytes 1572872 | tf_op jit(solution)/shard_map/ppermute | solution.py:98
  13.8 18.0 %collective-permute-start.1 = (bf16[1024,256]{1,0:T(8,128)(2,1)}, bf16[1024,256]{1,0:T(8,128)(2,1)}, u32[]{:S(2)}, u32[]{:S(2)}) collective-permute-start(bf16[1024,256]{1,0:T(8,128)(2,1)} %fusion.13), channel_id=1, source_target_pairs={{8,0},{16,8},{24,16},{32,24},{40,32},{48,40},{56,48},{64,56},{72,6... | collective-permute-start | bytes 1572872 | tf_op jit(solution)/shard_map/ppermute | solution.py:98
  16.9 16.8 %copy-start.22 = (f32[512]{0:T(512)}, f32[512]{0:T(512)S(1)}, u32[]{:S(2)}) copy-start(f32[512]{0:T(512)S(1)} %convert_add_fusion.2) | copy-start | bytes 6148
  18.2 1.1 copy-start.3
  19.1 9.9 %copy-start.2 = (bf16[8,5,128,128]{3,2,0,1:T(8,128)(2,1)S(1)}, bf16[8,5,128,128]{3,2,0,1:T(8,128)(2,1)}, u32[]{:S(2)}) copy-start(bf16[8,5,128,128]{3,2,0,1:T(8,128)(2,1)} %fusion.5) | copy-start | bytes 3932164
  31.8 1.6 copy-start.16
  31.8 1.9 copy-start.4
  33.4 1.2 copy-start.15
  33.7 1.1 copy-start.14
  36.5 16.7 %copy-start.24 = (bf16[256]{0:T(256)(128)(2,1)S(1)}, bf16[256]{0:T(256)(128)(2,1)}, u32[]{:S(2)}) copy-start(bf16[256]{0:T(256)(128)(2,1)} %param.22) | copy-start | bytes 1540
  36.5 17.2 %copy-start.7 = (bf16[256,256]{1,0:T(8,128)(2,1)S(1)}, bf16[256,256]{1,0:T(8,128)(2,1)}, u32[]{:S(2)}) copy-start(bf16[256,256]{1,0:T(8,128)(2,1)} %param.18) | copy-start | bytes 393220
  36.5 44.3 %copy-start.9 = (bf16[256,256]{1,0:T(8,128)(2,1)S(1)}, bf16[256,256]{1,0:T(8,128)(2,1)}, u32[]{:S(2)}) copy-start(bf16[256,256]{1,0:T(8,128)(2,1)} %param.19) | copy-start | bytes 393220
  36.5 44.3 %all-to-all-start = ((bf16[8,512,256]{2,1,0:T(8,128)(2,1)}), bf16[8,512,256]{2,1,0:T(8,128)(2,1)S(1)}, u32[]{:S(2)}, u32[]{:S(2)}) async-start(bf16[8,512,256]{2,1,0:T(8,128)(2,1)} %broadcast_in_dim.10), calls=%async_computation | async-start | bytes 4194304 | tf_op jit(solution)/shard_map/all_to_all | solution.py:104
  97.9 0.6 copy-start.20
  99.8 0.7 copy-start.13
  101.9 31.4 %all-to-all-start.1 = ((bf16[8,512,256]{2,1,0:T(8,128)(2,1)}), bf16[8,512,256]{2,1,0:T(8,128)(2,1)}, u32[]{:S(2)}, u32[]{:S(2)}) async-start(bf16[8,512,256]{2,1,0:T(8,128)(2,1)} %broadcast_in_dim.11), calls=%async_computation.1 | async-start | bytes 4194304 | tf_op jit(solution)/shard_map/all_to_all | solution.py:104
  121.1 6.0 %copy-start.8 = (bf16[256,256]{1,0:T(8,128)(2,1)S(1)}, bf16[256,256]{1,0:T(8,128)(2,1)}, u32[]{:S(2)}) copy-start(bf16[256,256]{1,0:T(8,128)(2,1)} %param.18) | copy-start | bytes 393220
  133.3 16.2 %copy-start.6 = (f32[512,256]{0,1:T(8,128)S(1)}, f32[512,256]{0,1:T(8,128)}, u32[]{:S(2)}) copy-start(f32[512,256]{0,1:T(8,128)} %convolution_add_fusion.4) | copy-start | bytes 1572868
  147.6 3.3 %copy-start.12 = (bf16[512,256]{1,0:T(8,128)(2,1)S(1)}, bf16[512,256]{1,0:T(8,128)(2,1)}, u32[]{:S(2)}) copy-start(bf16[512,256]{1,0:T(8,128)(2,1)} %get-tuple-element.10) | copy-start | bytes 786436
  149.5 3.4 %copy-start.5 = (s32[1,1,512,1024]{3,2,1,0:T(8,128)S(1)}, s32[1,1,512,1024]{3,2,1,0:T(8,128)}, u32[]{:S(2)}) copy-start(s32[1,1,512,1024]{3,2,1,0:T(8,128)} %param.15) | copy-start | bytes 6291460
  149.5 3.4 %copy-start.18 = (f32[1024]{0:T(1024)S(1)}, f32[1024]{0:T(1024)}, u32[]{:S(2)}) copy-start(f32[1024]{0:T(1024)} %copy-done.17) | copy-start | bytes 12292
  149.5 3.4 %copy-start.23 = (f32[512]{0:T(512)S(1)}, f32[512]{0:T(512)}, u32[]{:S(2)}) copy-start(f32[512]{0:T(512)} %copy-done.22) | copy-start | bytes 6148
  152.9 3.4 %copy-start.10 = (f32[256,256]{1,0:T(8,128)S(1)}, f32[256,256]{1,0:T(8,128)}, u32[]{:S(2)}) copy-start(f32[256,256]{1,0:T(8,128)} %fusion.60) | copy-start | bytes 786436
  152.9 3.4 %copy-start.11 = (f32[256,256]{1,0:T(8,128)S(1)}, f32[256,256]{1,0:T(8,128)}, u32[]{:S(2)}) copy-start(f32[256,256]{1,0:T(8,128)} %fusion.53) | copy-start | bytes 786436
  152.9 3.4 %copy-start.21 = (f32[256]{0:T(256)S(1)}, f32[256]{0:T(256)}, u32[]{:S(2)}) copy-start(f32[256]{0:T(256)} %get-tuple-element.11) | copy-start | bytes 3076
  198.7 5.7 %copy-start.19 = (f32[512]{0:T(512)S(1)}, f32[512]{0:T(512)}, u32[]{:S(2)}) copy-start(f32[512]{0:T(512)} %get-tuple-element.12) | copy-start | bytes 6148
  198.7 34.4 %all-to-all-start.3 = ((f32[128,16,256]{2,1,0:T(8,128)}), f32[128,16,256]{2,1,0:T(8,128)S(1)}, u32[]{:S(2)}, u32[]{:S(2)}) async-start(f32[128,16,256]{2,1,0:T(8,128)} %broadcast_in_dim.14), calls=%async_computation.3 | async-start | bytes 4194304 | tf_op jit(solution)/shard_map/all_to_all | solution.py:114

commit v2 on v1

--- a/solution.py
+++ b/solution.py
@@ -108,10 +108,12 @@
     size = 1
     for axis in axes:
         size *= lax.axis_size(axis)
-    chunks = lax.all_to_all(rows_in.reshape(size, -1, rows_in.shape[1]), axes, 0, 0, tiled=True)
+    if rows_in.shape[0] != size:
+        rows_in = rows_in.reshape(size, -1, rows_in.shape[-1])
+    chunks = lax.all_to_all(rows_in, axes, 0, 0, tiled=True)
     total = jnp.sum(chunks, axis=0, keepdims=True)
     copies = jnp.broadcast_to(total, chunks.shape)
-    return lax.all_to_all(copies, axes, 0, 0, tiled=True).reshape(rows_in.shape)
+    return lax.all_to_all(copies, axes, 0, 0, tiled=True)
 
 
 def silu_grad(preact):
@@ -194,12 +196,15 @@
     tokens = (token_live * normed).astype(jnp.bfloat16)
 
     tokens_all = gather_tiles(tokens, "col").reshape(-1, H)
-    query_all = project(tokens_all, w_query)
-    key_all = project(tokens_all, w_key)
-    value_all = project(tokens_all, w_value)
-    query_own = project(tokens, w_query)
-    key_own = project(tokens, w_key)
-    value_own = project(tokens, w_value)
+    w_qkv = jnp.concatenate([w_query, w_key, w_value], axis=1)
+    qkv_all = project(tokens_all, w_qkv)
+    query_all = qkv_all[:, :H]
+    key_all = qkv_all[:, H:2 * H]
+    value_all = qkv_all[:, 2 * H:]
+    qkv_own = project(tokens, w_qkv)
+    query_own = qkv_own[:, :H]
+    key_own = qkv_own[:, H:2 * H]
+    value_own = qkv_own[:, 2 * H:]
 
     attended = attend_fwd(query_own, key_all, value_all)
     proj = jnp.dot(attended, w_out, preferred_element_type=jnp.float32)
@@ -214,6 +219,9 @@
     grad_proj = rms_backward(grad_mixed, pnormed, pscale).astype(jnp.bfloat16)
     g_out = jnp.einsum("nh,ne->he", attended, grad_proj, preferred_element_type=jnp.float32)
     grad_attn = jnp.dot(grad_proj, w_out.T, preferred_element_type=jnp.float32).astype(jnp.bfloat16)
+    devices = lax.axis_size("row") * lax.axis_size("col")
+    early = jnp.concatenate([g_out, g_score[None], jnp.zeros((3 * devices - H - 1, H), jnp.float32)])
+    early = all_reduce_a2a(early.reshape(devices, -1), ("row", "col")).reshape(-1, H)
 
     grad_attn_all = gather_tiles(grad_attn, "col").reshape(-1, H)
 
@@ -234,15 +242,10 @@
     grad_pre = (gate_live[:, None] * grad_hidden * silu_grad(preact)).astype(jnp.bfloat16)
     g_msg = jnp.einsum("gh,ge->he", message, grad_pre, preferred_element_type=jnp.float32)
 
-    devices = lax.axis_size("row") * lax.axis_size("col")
-    grads = [g_msg, g_query, g_key, g_value, g_out, g_score[None]]
-    used = 5 * H + 1
-    per_device = -(-used // devices)
-    per_device = -(-per_device // 8) * 8
-    grads.append(jnp.zeros((per_device * devices - used, H), jnp.float32))
-    summed = all_reduce_a2a(jnp.concatenate(grads, axis=0), ("row", "col"))
-    outs = [summed[i * H:(i + 1) * H] for i in range(5)]
-    g_score_sum = summed[5 * H]
+    late = jnp.concatenate([g_msg, g_query, g_key, g_value], axis=0)
+    late = all_reduce_a2a(late, ("row", "col")).reshape(-1, H)
+    outs = [late[i * H:(i + 1) * H] for i in range(4)] + [early[:H]]
+    g_score_sum = early[H]
     return (value_out[None, None], *outs, g_score_sum)
 
 

time: 236 us -> 234 us (level)
  blocking collectives: 34.2 us -> 0 us
  starting transfers between devices: 38.4 us -> 56.8 us
  waiting for transfers between devices: 65.3 us -> 83.1 us
  matrix products: 35.3 us -> 23.4 us
  other arithmetic: 10.6 us -> 15.3 us
  local copies, waits for them, and re-layouts: 12.8 us -> 16 us
    all_to_all x1 -> x0, blocking collectives: 34.2 us -> none  [all_reduce_a2a(): lax.all_to_all(rows_in.reshape(size, -1, rows_in.shape[1]), axes, 0, 0, t...]
    all_to_all x1 -> x4, starting transfers between devices: 5.66 us -> 25.3 us  [the longest x2 15.4 us: all_reduce_a2a(): chunks = lax.all_to_all(rows_in, axes, 0, 0, tiled=True)]
    all_to_all x1 -> x4, waiting for transfers between devices: 28.1 us -> 43.7 us  [the longest x2 27 us: all_reduce_a2a(): return lax.all_to_all(copies, axes, 0, 0, tiled=True)]
    dot_general x6 -> x2, matrix products: 9.98 us -> 2.21 us  [project(): jnp.dot(rows_in, weight_mat, preferred_element_type=jnp.float32)]
    slice x2 -> x5, local copies, waits for them, and re-layouts: 1.63 us -> 5.91 us  [the longest x1 2.75 us: body(): query_all = qkv_all[:, :H]]
    concatenate x1 -> x2, local copies, waits for them, and re-layouts: 4.82 us -> 0.62 us  [the longest x1 0.61 us: body(): jnp.concatenate([g_out, g_score[None], jnp.zeros((3 * devices - H - 1, H)...]
  transfers between devices with their start and end apart: 7 -> 10, of which waited for: 4 -> 6; matrix products, arithmetic and copies ran while one was open for 9% -> 15% of each run, Pallas kernels for 5% -> 11%
where the time goes in v2:
time: 234 us; the launch traced here: 233 us
  waiting for transfers between devices  83.1 us (36%)
  starting transfers between devices  56.8 us (24%)
  Pallas kernels  35.6 us (15%)
  matrix products  23.4 us (10%)
  local copies, waits for them, and re-layouts  16 us (7%)
  other arithmetic  15.3 us (7%)
  between operations  2.51 us (1%)
    all_to_all x2, waiting for transfers between devices, gather_tiles(): return lax.all_to_all(copies, axis, 0, 0, tiled=True)  32.3 us
    all_to_all x2, waiting for transfers between devices, all_reduce_a2a(): return lax.all_to_all(copies, axes, 0, 0, tiled=True)  27 us
    all_to_all x2, starting transfers between devices, gather_tiles(): return lax.all_to_all(copies, axis, 0, 0, tiled=True)  19.5 us
    all_to_all x2, waiting for transfers between devices, all_reduce_a2a(): chunks = lax.all_to_all(rows_in, axes, 0, 0, tiled=True)  16.7 us
    all_to_all x2, starting transfers between devices, all_reduce_a2a(): chunks = lax.all_to_all(rows_in, axes, 0, 0, tiled=True)  15.4 us
    pallas_call x1, Pallas kernels, attend_gkv(): pl.pallas_call(_gkv_kernel, out_shape=(sh, sh), scratch_shapes=[pltpu.VME...  14.2 us
    ppermute x4, starting transfers between devices, from_neighbour(): return lax.ppermute(array, axis, pairs)  12 us
    pallas_call x1, Pallas kernels, attend_gq(): pl.pallas_call(_gq_kernel, out_shape=jax.ShapeDtypeStruct(q.shape, jnp.bf...  11.8 us
  transfers between devices with their start and end apart: 10, of which 6 were waited for; matrix products, arithmetic and copies ran while one was open for 15% of the time, Pallas kernels for 11%

profile of v2, /device:TPU:0, one launch (start us, length us, event | category | flops | bytes accessed | tf_op | source)
XLA Modules:
  0.0 232.6 jit_solution(17627925565976001657)
XLA Ops:
  1.4 2.0 fusion.13
  3.4 2.3 %collective-permute-start = (bf16[1024,256]{1,0:T(8,128)(2,1)}, bf16[1024,256]{1,0:T(8,128)(2,1)}, u32[]{:S(2)}, u32[]{:S(2)}) collective-permute-start(bf16[1024,256]{1,0:T(8,128)(2,1)} %fusion.13), channel_id=1, source_target_pairs={{0,8},{8,16},{16,24},{24,32},{32,40},{40,48},{48,56},{56,64},{64,7... | collective-permute-start | bytes 1572872 | tf_op jit(solution)/shard_map/ppermute | solution.py:98
  7.0 7.1 %collective-permute-start.2 = (bf16[1024,256]{1,0:T(8,128)(2,1)}, bf16[1024,256]{1,0:T(8,128)(2,1)}, u32[]{:S(2)}, u32[]{:S(2)}) collective-permute-start(bf16[1024,256]{1,0:T(8,128)(2,1)} %fusion.13), channel_id=1, source_target_pairs={{0,1},{1,2},{2,3},{3,4},{4,5},{5,6},{6,7},{8,9},{9,10},{10,11},{11... | collective-permute-start | bytes 1572872 | tf_op jit(solution)/shard_map/ppermute | solution.py:98
  15.4 3.1 %fusion.5 = bf16[8,5,128,128]{3,2,0,1:T(8,128)(2,1)} fusion(s32[1,1,8,5,128,128]{5,4,3,2,1,0:T(8,128)} %param.13), kind=kLoop, calls=%fused_computation.11 | loop fusion | flops 655360 | bytes 3932160 | tf_op jit(solution)/shard_map/convert.6
  18.5 1.8 reduce_sum.93
  21.2 1.4 fusion.21
  22.7 7.1 %collective-permute-done.3 = bf16[1024,256]{1,0:T(8,128)(2,1)} collective-permute-done((bf16[1024,256]{1,0:T(8,128)(2,1)}, bf16[1024,256]{1,0:T(8,128)(2,1)}, u32[]{:S(2)}, u32[]{:S(2)}) %collective-permute-start.3) | collective-permute-done | bytes 524320 | tf_op jit(solution)/shard_map/ppermute | solution.py:98
  33.9 1.6 fusion.6
  37.0 1.5 broadcast_in_dim.12
  38.5 15.9 %all-to-all-start = ((bf16[8,512,256]{2,1,0:T(8,128)(2,1)}), bf16[8,512,256]{2,1,0:T(8,128)(2,1)S(1)}, u32[]{:S(2)}, u32[]{:S(2)}) async-start(bf16[8,512,256]{2,1,0:T(8,128)(2,1)} %broadcast_in_dim.12), calls=%async_computation | async-start | bytes 4194304 | tf_op jit(solution)/shard_map/all_to_all | solution.py:104
  58.2 25.0 %all-to-all-done = bf16[8,512,256]{2,1,0:T(8,128)(2,1)S(1)} async-done(((bf16[8,512,256]{2,1,0:T(8,128)(2,1)}), bf16[8,512,256]{2,1,0:T(8,128)(2,1)S(1)}, u32[]{:S(2)}, u32[]{:S(2)}) %all-to-all-start) | async-done | bytes 2097184 | tf_op jit(solution)/shard_map/all_to_all | solution.py:104
  83.2 1.8 convolution_convert_fusion
  85.0 2.8 %fusion.57 = (bf16[4096,256]{1,0:T(8,128)(2,1)}, bf16[4096,256]{1,0:T(8,128)(2,1)}, bf16[4096,256]{1,0:T(8,128)(2,1)}) fusion(bf16[4096,768]{1,0:T(8,128)(2,1)S(1)} %convolution_convert_fusion), kind=kLoop, calls=%fused_computation.96 | loop fusion | bytes 12582912 | tf_op jit(solution)/shard_map/slice | solution.py:201
  87.8 9.6 %shard_map.171 = bf16[512,256]{1,0:T(8,128)(2,1)} custom-call(bf16[512,256]{1,0:T(8,128)(2,1)} %get-tuple-element.23.q_ref, bf16[4096,256]{1,0:T(8,128)(2,1)} %get-tuple-element.16.k_ref, bf16[4096,256]{1,0:T(8,128)(2,1)} %get-tuple-element.15.v_ref), custom_call_target="tpu_custom_call" | custom-call | tf_op jit(solution)/shard_map/pallas_call | solution.py:82
  99.9 1.5 broadcast_in_dim.13
  101.3 3.6 %all-to-all-start.1 = ((bf16[8,512,256]{2,1,0:T(8,128)(2,1)}), bf16[8,512,256]{2,1,0:T(8,128)(2,1)S(1)}, u32[]{:S(2)}, u32[]{:S(2)}) async-start(bf16[8,512,256]{2,1,0:T(8,128)(2,1)} %broadcast_in_dim.13), calls=%async_computation.1 | async-start | bytes 4194304 | tf_op jit(solution)/shard_map/all_to_all | solution.py:104
  105.5 11.8 %shard_map.172 = bf16[512,256]{1,0:T(8,128)(2,1)} custom-call(bf16[512,256]{1,0:T(8,128)(2,1)} %get-tuple-element.23.q_ref, bf16[512,256]{1,0:T(8,128)(2,1)} %copy-done.10, bf16[4096,256]{1,0:T(8,128)(2,1)} %get-tuple-element.16.k_ref, bf16[4096,256]{1,0:T(8,128)(2,1)} %get-tuple-element.15.v_ref), custom_call_target="tpu_custom_call" | custom-call | tf_op jit(solution)/shard_map/pallas_call | solution.py:86
  118.7 1.6 maximum_maximum_fusion
  120.3 2.1 all_to_all.29
  122.5 1.9 fusion.61
  125.4 7.3 %all-to-all-done.1 = bf16[8,512,256]{2,1,0:T(8,128)(2,1)S(1)} async-done(((bf16[8,512,256]{2,1,0:T(8,128)(2,1)}), bf16[8,512,256]{2,1,0:T(8,128)(2,1)S(1)}, u32[]{:S(2)}, u32[]{:S(2)}) %all-to-all-start.1) | async-done | bytes 2097184 | tf_op jit(solution)/shard_map/all_to_all | solution.py:104
  132.7 5.9 %all-to-all-start.4 = ((f32[128,1,768]{2,1,0:T(1,128)}), f32[128,1,768]{2,1,0:T(1,128)}, u32[]{:S(2)}, u32[]{:S(2)}) async-start(f32[128,1,768]{2,1,0:T(1,128)} %all_to_all.29), calls=%async_computation.4 | async-start | bytes 786432 | tf_op jit(solution)/shard_map/all_to_all | solution.py:113
  138.6 14.2 %shard_map.173 = (bf16[512,256]{1,0:T(8,128)(2,1)}, bf16[512,256]{1,0:T(8,128)(2,1)}) custom-call(bf16[4096,256]{1,0:T(8,128)(2,1)} %get-tuple-element.14.q_ref, bf16[4096,256]{1,0:T(8,128)(2,1)} %bitcast.122, bf16[512,256]{1,0:T(8,128)(2,1)} %get-tuple-element.22.k_ref, bf16[512,256]{1,0:T(8,128)(2,1)} %get-tuple-element.21.v_ref), custom_call_target="tpu_custom_call" | custom-call | tf_op jit(solution)/shard_map/pallas_call | solution.py:91
  154.3 2.1 fusion.23
  156.4 3.3 %fusion.8 = f32[256,256]{1,0:T(8,128)} fusion(bf16[1024,256]{1,0:T(8,128)(2,1)} %bitcast.125, f32[1024,256]{1,0:T(8,128)} %copy-done.12, f32[1024]{0:T(1024)S(1)} %copy-done.18, s32[1,1,512,1024]{3,2,1,0:T(8,128)S(1)} %copy-done.7, f32[512,256]{0,1:T(8,128)} %get-tuple-element.29, f32[256,512]{1,0:T(8,128)S(1)} %get-tuple-element.25, ...), kind=kOutput, calls=%fused_computation.15 | convolution fusion | flops 406585344 | bytes 4990976 | tf_op jit(solution)/shard_map/gh,ge->he/dot_general | solution.py:243
  160.1 2.1 maximum_bitcast_fusion
  162.2 9.5 %all-to-all-start.2 = ((f32[128,8,256]{2,1,0:T(8,128)}), f32[128,8,256]{2,1,0:T(8,128)S(1)}, u32[]{:S(2)}, u32[]{:S(2)}) async-start(f32[128,8,256]{2,1,0:T(8,128)} %maximum_bitcast_fusion), calls=%async_computation.2 | async-start | bytes 2097152 | tf_op jit(solution)/shard_map/all_to_all | solution.py:113
  173.0 16.7 %all-to-all-done.2 = f32[128,8,256]{2,1,0:T(8,128)S(1)} async-done(((f32[128,8,256]{2,1,0:T(8,128)}), f32[128,8,256]{2,1,0:T(8,128)S(1)}, u32[]{:S(2)}, u32[]{:S(2)}) %all-to-all-start.2) | async-done | bytes 1048608 | tf_op jit(solution)/shard_map/all_to_all | solution.py:113
  190.7 5.2 %all-to-all-start.5 = ((f32[128,1,768]{2,1,0:T(1,128)}), f32[128,1,768]{2,1,0:T(1,128)S(1)}, u32[]{:S(2)}, u32[]{:S(2)}) async-start(f32[128,1,768]{2,1,0:T(1,128)} %broadcast_in_dim.17), calls=%async_computation.5 | async-start | bytes 786432 | tf_op jit(solution)/shard_map/all_to_all | solution.py:116
  196.1 11.9 %all-to-all-done.5 = f32[128,1,768]{2,1,0:T(1,128)S(1)} async-done(((f32[128,1,768]{2,1,0:T(1,128)}), f32[128,1,768]{2,1,0:T(1,128)S(1)}, u32[]{:S(2)}, u32[]{:S(2)}) %all-to-all-start.5) | async-done | bytes 393248 | tf_op jit(solution)/shard_map/all_to_all | solution.py:116
  209.0 4.6 %all-to-all-start.3 = ((f32[128,8,256]{2,1,0:T(8,128)}), f32[128,8,256]{2,1,0:T(8,128)S(1)}, u32[]{:S(2)}, u32[]{:S(2)}) async-start(f32[128,8,256]{2,1,0:T(8,128)} %broadcast_in_dim.14), calls=%async_computation.3 | async-start | bytes 2097152 | tf_op jit(solution)/shard_map/all_to_all | solution.py:116
  216.5 15.1 %all-to-all-done.3 = f32[128,8,256]{2,1,0:T(8,128)S(1)} async-done(((f32[128,8,256]{2,1,0:T(8,128)}), f32[128,8,256]{2,1,0:T(8,128)S(1)}, u32[]{:S(2)}, u32[]{:S(2)}) %all-to-all-start.3) | async-done | bytes 1048608 | tf_op jit(solution)/shard_map/all_to_all | solution.py:116
  (103 shorter events, 26.8 us)
Async XLA Ops:
  0.6 96.7 %copy-start = (bf16[256,256]{1,0:T(8,128)(2,1)S(1)}, bf16[256,256]{1,0:T(8,128)(2,1)}, u32[]{:S(2)}) copy-start(bf16[256,256]{1,0:T(8,128)(2,1)} %param.21) | copy-start | bytes 393220
  1.3 34.4 %copy-start.17 = (f32[1024]{0:T(1024)}, f32[1024]{0:T(1024)S(1)}, u32[]{:S(2)}) copy-start(f32[1024]{0:T(1024)S(1)} %fusion.49) | copy-start | bytes 12292
  3.4 17.6 %copy-start.1 = (s32[1,1,8,5,128,128]{5,4,3,2,1,0:T(8,128)S(1)}, s32[1,1,8,5,128,128]{5,4,3,2,1,0:T(8,128)}, u32[]{:S(2)}) copy-start(s32[1,1,8,5,128,128]{5,4,3,2,1,0:T(8,128)} %param.13) | copy-start | bytes 7864324
  3.4 29.1 %collective-permute-start = (bf16[1024,256]{1,0:T(8,128)(2,1)}, bf16[1024,256]{1,0:T(8,128)(2,1)}, u32[]{:S(2)}, u32[]{:S(2)}) collective-permute-start(bf16[1024,256]{1,0:T(8,128)(2,1)} %fusion.13), channel_id=1, source_target_pairs={{0,8},{8,16},{16,24},{24,32},{32,40},{40,48},{48,56},{56,64},{64,7... | collective-permute-start | bytes 1572872 | tf_op jit(solution)/shard_map/ppermute | solution.py:98
  5.7 24.0 %collective-permute-start.3 = (bf16[1024,256]{1,0:T(8,128)(2,1)}, bf16[1024,256]{1,0:T(8,128)(2,1)}, u32[]{:S(2)}, u32[]{:S(2)}) collective-permute-start(bf16[1024,256]{1,0:T(8,128)(2,1)} %fusion.13), channel_id=1, source_target_pairs={{1,0},{2,1},{3,2},{4,3},{5,4},{6,5},{7,6},{9,8},{10,9},{11,10},{12... | collective-permute-start | bytes 1572872 | tf_op jit(solution)/shard_map/ppermute | solution.py:98
  7.0 24.1 %collective-permute-start.2 = (bf16[1024,256]{1,0:T(8,128)(2,1)}, bf16[1024,256]{1,0:T(8,128)(2,1)}, u32[]{:S(2)}, u32[]{:S(2)}) collective-permute-start(bf16[1024,256]{1,0:T(8,128)(2,1)} %fusion.13), channel_id=1, source_target_pairs={{0,1},{1,2},{2,3},{3,4},{4,5},{5,6},{6,7},{8,9},{9,10},{10,11},{11... | collective-permute-start | bytes 1572872 | tf_op jit(solution)/shard_map/ppermute | solution.py:98
  14.1 19.8 %collective-permute-start.1 = (bf16[1024,256]{1,0:T(8,128)(2,1)}, bf16[1024,256]{1,0:T(8,128)(2,1)}, u32[]{:S(2)}, u32[]{:S(2)}) collective-permute-start(bf16[1024,256]{1,0:T(8,128)(2,1)} %fusion.13), channel_id=1, source_target_pairs={{8,0},{16,8},{24,16},{32,24},{40,32},{48,40},{56,48},{64,56},{72,6... | collective-permute-start | bytes 1572872 | tf_op jit(solution)/shard_map/ppermute | solution.py:98
  18.5 2.8 %copy-start.5 = (bf16[1,1,1024,256]{3,2,1,0:T(8,128)(2,1)S(1)}, bf16[1,1,1024,256]{3,2,1,0:T(8,128)(2,1)}, u32[]{:S(2)}) copy-start(bf16[1,1,1024,256]{3,2,1,0:T(8,128)(2,1)} %param.12) | copy-start | bytes 1572868
  20.3 15.4 %copy-start.24 = (f32[512]{0:T(512)}, f32[512]{0:T(512)S(1)}, u32[]{:S(2)}) copy-start(f32[512]{0:T(512)S(1)} %convert_add_fusion.2) | copy-start | bytes 6148
  21.2 9.9 %copy-start.3 = (bf16[8,5,128,128]{3,2,0,1:T(8,128)(2,1)S(1)}, bf16[8,5,128,128]{3,2,0,1:T(8,128)(2,1)}, u32[]{:S(2)}) copy-start(bf16[8,5,128,128]{3,2,0,1:T(8,128)(2,1)} %fusion.5) | copy-start | bytes 3932164
  33.9 1.9 copy-start.6
  38.5 15.9 %copy-start.26 = (bf16[256]{0:T(256)(128)(2,1)S(1)}, bf16[256]{0:T(256)(128)(2,1)}, u32[]{:S(2)}) copy-start(bf16[256]{0:T(256)(128)(2,1)} %param.22) | copy-start | bytes 1540
  38.5 18.3 %copy-start.13 = (bf16[256,256]{1,0:T(8,128)(2,1)S(1)}, bf16[256,256]{1,0:T(8,128)(2,1)}, u32[]{:S(2)}) copy-start(bf16[256,256]{1,0:T(8,128)(2,1)} %param.20) | copy-start | bytes 393220
  38.5 44.7 %all-to-all-start = ((bf16[8,512,256]{2,1,0:T(8,128)(2,1)}), bf16[8,512,256]{2,1,0:T(8,128)(2,1)S(1)}, u32[]{:S(2)}, u32[]{:S(2)}) async-start(bf16[8,512,256]{2,1,0:T(8,128)(2,1)} %broadcast_in_dim.12), calls=%async_computation | async-start | bytes 4194304 | tf_op jit(solution)/shard_map/all_to_all | solution.py:104
  87.8 10.8 %copy-start.23 = (f32[1,1,512]{2,1,0:T(1,128)S(1)}, f32[1,1,512]{2,1,0:T(1,128)}, u32[]{:S(2)}) copy-start(f32[1,1,512]{2,1,0:T(1,128)} %param.23) | copy-start | bytes 6148
  87.8 10.8 %copy-start.19 = (f32[256]{0:T(256)S(1)}, f32[256]{0:T(256)}, u32[]{:S(2)}) copy-start(f32[256]{0:T(256)} %convert_element_type.136) | copy-start | bytes 3076
  101.3 31.4 %all-to-all-start.1 = ((bf16[8,512,256]{2,1,0:T(8,128)(2,1)}), bf16[8,512,256]{2,1,0:T(8,128)(2,1)S(1)}, u32[]{:S(2)}, u32[]{:S(2)}) async-start(bf16[8,512,256]{2,1,0:T(8,128)(2,1)} %broadcast_in_dim.13), calls=%async_computation.1 | async-start | bytes 4194304 | tf_op jit(solution)/shard_map/all_to_all | solution.py:104
  118.7 5.7 %copy-start.4 = (bf16[512,256]{1,0:T(8,128)(2,1)S(1)}, bf16[512,256]{1,0:T(8,128)(2,1)}, u32[]{:S(2)}) copy-start(bf16[512,256]{1,0:T(8,128)(2,1)} %shard_map.172) | copy-start | bytes 786436
  118.7 5.6 %copy-start.15 = (bf16[256,256]{1,0:T(8,128)(2,1)S(1)}, bf16[256,256]{1,0:T(8,128)(2,1)}, u32[]{:S(2)}) copy-start(bf16[256,256]{1,0:T(8,128)(2,1)} %param.18) | copy-start | bytes 393220
  118.7 5.6 %copy-start.20 = (f32[256]{0:T(256)S(1)}, f32[256]{0:T(256)}, u32[]{:S(2)}) copy-start(f32[256]{0:T(256)} %convert_element_type.136) | copy-start | bytes 3076
  132.7 5.9 %copy-start.2 = (bf16[8,512,256]{2,1,0:T(8,128)(2,1)}, bf16[8,512,256]{2,1,0:T(8,128)(2,1)S(1)}, u32[]{:S(2)}) copy-start(bf16[8,512,256]{2,1,0:T(8,128)(2,1)S(1)} %all-to-all-done.1) | copy-start | bytes 6291460
  132.7 29.5 %all-to-all-start.4 = ((f32[128,1,768]{2,1,0:T(1,128)}), f32[128,1,768]{2,1,0:T(1,128)}, u32[]{:S(2)}, u32[]{:S(2)}) async-start(f32[128,1,768]{2,1,0:T(1,128)} %all_to_all.29), calls=%async_computation.4 | async-start | bytes 786432 | tf_op jit(solution)/shard_map/all_to_all | solution.py:113
  138.6 14.3 %copy-start.8 = (f32[512,256]{0,1:T(8,128)S(1)}, f32[512,256]{0,1:T(8,128)}, u32[]{:S(2)}) copy-start(f32[512,256]{0,1:T(8,128)} %convolution_add_fusion.4) | copy-start | bytes 1572868
  152.8 3.5 %copy-start.7 = (s32[1,1,512,1024]{3,2,1,0:T(8,128)S(1)}, s32[1,1,512,1024]{3,2,1,0:T(8,128)}, u32[]{:S(2)}) copy-start(s32[1,1,512,1024]{3,2,1,0:T(8,128)} %param.15) | copy-start | bytes 6291460
  152.8 3.5 %copy-start.18 = (f32[1024]{0:T(1024)S(1)}, f32[1024]{0:T(1024)}, u32[]{:S(2)}) copy-start(f32[1024]{0:T(1024)} %copy-done.17) | copy-start | bytes 12292
  152.8 3.5 %copy-start.25 = (f32[512]{0:T(512)S(1)}, f32[512]{0:T(512)}, u32[]{:S(2)}) copy-start(f32[512]{0:T(512)} %copy-done.24) | copy-start | bytes 6148
  156.3 3.3 %copy-start.11 = (bf16[512,256]{1,0:T(8,128)(2,1)S(1)}, bf16[512,256]{1,0:T(8,128)(2,1)}, u32[]{:S(2)}) copy-start(bf16[512,256]{1,0:T(8,128)(2,1)} %get-tuple-element.9) | copy-start | bytes 786436
  156.4 3.5 %copy-start.9 = (bf16[512,256]{1,0:T(8,128)(2,1)S(1)}, bf16[512,256]{1,0:T(8,128)(2,1)}, u32[]{:S(2)}) copy-start(bf16[512,256]{1,0:T(8,128)(2,1)} %get-tuple-element.10) | copy-start | bytes 786436
  162.2 27.5 %all-to-all-start.2 = ((f32[128,8,256]{2,1,0:T(8,128)}), f32[128,8,256]{2,1,0:T(8,128)S(1)}, u32[]{:S(2)}, u32[]{:S(2)}) async-start(f32[128,8,256]{2,1,0:T(8,128)} %maximum_bitcast_fusion), calls=%async_computation.2 | async-start | bytes 2097152 | tf_op jit(solution)/shard_map/all_to_all | solution.py:113
  190.7 17.3 %all-to-all-start.5 = ((f32[128,1,768]{2,1,0:T(1,128)}), f32[128,1,768]{2,1,0:T(1,128)S(1)}, u32[]{:S(2)}, u32[]{:S(2)}) async-start(f32[128,1,768]{2,1,0:T(1,128)} %broadcast_in_dim.17), calls=%async_computation.5 | async-start | bytes 786432 | tf_op jit(solution)/shard_map/all_to_all | solution.py:116
  195.9 17.7 %copy-start.21 = (f32[512]{0:T(512)S(1)}, f32[512]{0:T(512)}, u32[]{:S(2)}) copy-start(f32[512]{0:T(512)} %get-tuple-element.12) | copy-start | bytes 6148
  209.0 22.6 %all-to-all-start.3 = ((f32[128,8,256]{2,1,0:T(8,128)}), f32[128,8,256]{2,1,0:T(8,128)S(1)}, u32[]{:S(2)}, u32[]{:S(2)}) async-start(f32[128,8,256]{2,1,0:T(8,128)} %broadcast_in_dim.14), calls=%async_computation.3 | async-start | bytes 2097152 | tf_op jit(solution)/shard_map/all_to_all | solution.py:116
  (5 other events, 7.2 us)

commit v3 on v2

--- a/solution.py
+++ b/solution.py
@@ -111,9 +111,9 @@
     if rows_in.shape[0] != size:
         rows_in = rows_in.reshape(size, -1, rows_in.shape[-1])
     chunks = lax.all_to_all(rows_in, axes, 0, 0, tiled=True)
-    total = jnp.sum(chunks, axis=0, keepdims=True)
+    total = jnp.sum(chunks, axis=0, keepdims=True).astype(jnp.bfloat16)
     copies = jnp.broadcast_to(total, chunks.shape)
-    return lax.all_to_all(copies, axes, 0, 0, tiled=True)
+    return lax.all_to_all(copies, axes, 0, 0, tiled=True).astype(jnp.float32)
 
 
 def silu_grad(preact):
@@ -221,9 +221,10 @@
     grad_attn = jnp.dot(grad_proj, w_out.T, preferred_element_type=jnp.float32).astype(jnp.bfloat16)
     devices = lax.axis_size("row") * lax.axis_size("col")
     early = jnp.concatenate([g_out, g_score[None], jnp.zeros((3 * devices - H - 1, H), jnp.float32)])
+
+    grad_attn_all = gather_tiles(grad_attn, "col").reshape(-1, H)
+    early, grad_attn_all = lax.optimization_barrier((early, grad_attn_all))
     early = all_reduce_a2a(early.reshape(devices, -1), ("row", "col")).reshape(-1, H)
-
-    grad_attn_all = gather_tiles(grad_attn, "col").reshape(-1, H)
 
     grad_query = attend_gq(query_own, grad_attn, key_all, value_all)
     grad_key, grad_val = attend_gkv(query_all, grad_attn_all, key_own, value_own)
@@ -243,6 +244,7 @@
     g_msg = jnp.einsum("gh,ge->he", message, grad_pre, preferred_element_type=jnp.float32)
 
     late = jnp.concatenate([g_msg, g_query, g_key, g_value], axis=0)
+    early, late = lax.optimization_barrier((early, late))
     late = all_reduce_a2a(late, ("row", "col")).reshape(-1, H)
     outs = [late[i * H:(i + 1) * H] for i in range(4)] + [early[:H]]
     g_score_sum = early[H]

time: 234 us -> 234 us (level)
  blocking collectives: 0 us -> 22 us
  waiting for transfers between devices: 83.1 us -> 72 us
  starting transfers between devices: 56.8 us -> 46.1 us
    all_to_all x0 -> x1, blocking collectives: none -> 22 us  [all_reduce_a2a(): chunks = lax.all_to_all(rows_in, axes, 0, 0, tiled=True)]
    all_to_all x2 -> x1, starting transfers between devices: 15.4 us -> 4.6 us  [all_reduce_a2a(): chunks = lax.all_to_all(rows_in, axes, 0, 0, tiled=True)]
    all_to_all x2 -> x1, waiting for transfers between devices: 16.7 us -> 8.74 us  [all_reduce_a2a(): chunks = lax.all_to_all(rows_in, axes, 0, 0, tiled=True)]
    all_to_all x2, waiting for transfers between devices: 27 us -> 21.2 us  [all_reduce_a2a(): return lax.all_to_all(copies, axes, 0, 0, tiled=True).astype(jnp.float32)]
    unnamed x56 -> x66, local copies, waits for them, and re-layouts: 2.17 us -> 5.02 us
    all_to_all x2, waiting for transfers between devices: 32.3 us -> 35 us  [gather_tiles(): return lax.all_to_all(copies, axis, 0, 0, tiled=True)]
  transfers between devices with their start and end apart: 10 -> 9, of which waited for: 6 -> 6; matrix products, arithmetic and copies ran while one was open for 15% -> 11% of each run, Pallas kernels for 11% -> 5%
where the time goes in v3:
time: 234 us; the launch traced here: 233 us
  waiting for transfers between devices  72 us (31%)
  starting transfers between devices  46.1 us (20%)
  Pallas kernels  35.6 us (15%)
  matrix products  23.2 us (10%)
  blocking collectives  22 us (9%)
  local copies, waits for them, and re-layouts  17.5 us (7%)
  other arithmetic  14.3 us (6%)
  between operations  2.56 us (1%)
    all_to_all x2, waiting for transfers between devices, gather_tiles(): return lax.all_to_all(copies, axis, 0, 0, tiled=True)  35 us
    all_to_all x1, blocking collectives, all_reduce_a2a(): chunks = lax.all_to_all(rows_in, axes, 0, 0, tiled=True)  22 us
    all_to_all x2, waiting for transfers between devices, all_reduce_a2a(): return lax.all_to_all(copies, axes, 0, 0, tiled=True).astype(jnp.float32)  21.2 us
    all_to_all x2, starting transfers between devices, gather_tiles(): return lax.all_to_all(copies, axis, 0, 0, tiled=True)  19.7 us
    pallas_call x1, Pallas kernels, attend_gkv(): pl.pallas_call(_gkv_kernel, out_shape=(sh, sh), scratch_shapes=[pltpu.VME...  14.2 us
    ppermute x4, starting transfers between devices, from_neighbour(): return lax.ppermute(array, axis, pairs)  12 us
    pallas_call x1, Pallas kernels, attend_gq(): pl.pallas_call(_gq_kernel, out_shape=jax.ShapeDtypeStruct(q.shape, jnp.bf...  11.8 us
    all_to_all x2, starting transfers between devices, all_reduce_a2a(): return lax.all_to_all(copies, axes, 0, 0, tiled=True).astype(jnp.float32)  9.85 us
  transfers between devices with their start and end apart: 9, of which 6 were waited for; matrix products, arithmetic and copies ran while one was open for 11% of the time, Pallas kernels for 5%

profile of v3, /device:TPU:0, one launch (start us, length us, event | category | flops | bytes accessed | tf_op | source)
XLA Modules:
  0.0 233.3 jit_solution(11937452187925184512)
XLA Ops:
  1.4 2.0 fusion.13
  3.4 2.3 %collective-permute-start = (bf16[1024,256]{1,0:T(8,128)(2,1)}, bf16[1024,256]{1,0:T(8,128)(2,1)}, u32[]{:S(2)}, u32[]{:S(2)}) collective-permute-start(bf16[1024,256]{1,0:T(8,128)(2,1)} %fusion.13), channel_id=1, source_target_pairs={{0,8},{8,16},{16,24},{24,32},{32,40},{40,48},{48,56},{56,64},{64,7... | collective-permute-start | bytes 1572872 | tf_op jit(solution)/shard_map/ppermute | solution.py:98
  7.0 7.1 %collective-permute-start.2 = (bf16[1024,256]{1,0:T(8,128)(2,1)}, bf16[1024,256]{1,0:T(8,128)(2,1)}, u32[]{:S(2)}, u32[]{:S(2)}) collective-permute-start(bf16[1024,256]{1,0:T(8,128)(2,1)} %fusion.13), channel_id=1, source_target_pairs={{0,1},{1,2},{2,3},{3,4},{4,5},{5,6},{6,7},{8,9},{9,10},{10,11},{11... | collective-permute-start | bytes 1572872 | tf_op jit(solution)/shard_map/ppermute | solution.py:98
  15.4 3.1 %fusion.5 = bf16[8,5,128,128]{3,2,0,1:T(8,128)(2,1)} fusion(s32[1,1,8,5,128,128]{5,4,3,2,1,0:T(8,128)} %param.13), kind=kLoop, calls=%fused_computation.11 | loop fusion | flops 655360 | bytes 3932160 | tf_op jit(solution)/shard_map/convert.7
  18.5 1.8 reduce_sum.93
  21.2 1.4 fusion.21
  22.7 7.0 %collective-permute-done.3 = bf16[1024,256]{1,0:T(8,128)(2,1)} collective-permute-done((bf16[1024,256]{1,0:T(8,128)(2,1)}, bf16[1024,256]{1,0:T(8,128)(2,1)}, u32[]{:S(2)}, u32[]{:S(2)}) %collective-permute-start.3) | collective-permute-done | bytes 524320 | tf_op jit(solution)/shard_map/ppermute | solution.py:98
  29.7 1.4 fusion.38
  33.9 1.6 fusion.6
  37.0 1.5 broadcast_in_dim.12
  38.5 15.9 %all-to-all-start = ((bf16[8,512,256]{2,1,0:T(8,128)(2,1)}), bf16[8,512,256]{2,1,0:T(8,128)(2,1)S(1)}, u32[]{:S(2)}, u32[]{:S(2)}) async-start(bf16[8,512,256]{2,1,0:T(8,128)(2,1)} %broadcast_in_dim.12), calls=%async_computation | async-start | bytes 4194304 | tf_op jit(solution)/shard_map/all_to_all | solution.py:104
  58.2 25.0 %all-to-all-done = bf16[8,512,256]{2,1,0:T(8,128)(2,1)S(1)} async-done(((bf16[8,512,256]{2,1,0:T(8,128)(2,1)}), bf16[8,512,256]{2,1,0:T(8,128)(2,1)S(1)}, u32[]{:S(2)}, u32[]{:S(2)}) %all-to-all-start) | async-done | bytes 2097184 | tf_op jit(solution)/shard_map/all_to_all | solution.py:104
  83.2 1.8 convolution_convert_fusion
  85.0 2.7 %fusion.57 = (bf16[4096,256]{1,0:T(8,128)(2,1)}, bf16[4096,256]{1,0:T(8,128)(2,1)}, bf16[4096,256]{1,0:T(8,128)(2,1)}) fusion(bf16[4096,768]{1,0:T(8,128)(2,1)S(1)} %convolution_convert_fusion), kind=kLoop, calls=%fused_computation.97 | loop fusion | bytes 12582912 | tf_op jit(solution)/shard_map/slice | solution.py:201
  87.8 9.6 %shard_map.171 = bf16[512,256]{1,0:T(8,128)(2,1)} custom-call(bf16[512,256]{1,0:T(8,128)(2,1)} %get-tuple-element.31.q_ref, bf16[4096,256]{1,0:T(8,128)(2,1)} %get-tuple-element.24.k_ref, bf16[4096,256]{1,0:T(8,128)(2,1)} %get-tuple-element.23.v_ref), custom_call_target="tpu_custom_call" | custom-call | tf_op jit(solution)/shard_map/pallas_call | solution.py:82
  100.5 1.5 broadcast_in_dim.15
  102.0 3.8 %all-to-all-start.1 = ((bf16[8,512,256]{2,1,0:T(8,128)(2,1)}), bf16[8,512,256]{2,1,0:T(8,128)(2,1)S(1)}, u32[]{:S(2)}, u32[]{:S(2)}) async-start(bf16[8,512,256]{2,1,0:T(8,128)(2,1)} %broadcast_in_dim.15), calls=%async_computation.1 | async-start | bytes 4194304 | tf_op jit(solution)/shard_map/all_to_all | solution.py:104
  106.5 11.8 %shard_map.172 = bf16[512,256]{1,0:T(8,128)(2,1)} custom-call(bf16[512,256]{1,0:T(8,128)(2,1)} %get-tuple-element.31.q_ref, bf16[512,256]{1,0:T(8,128)(2,1)} %copy-done.11, bf16[4096,256]{1,0:T(8,128)(2,1)} %get-tuple-element.24.k_ref, bf16[4096,256]{1,0:T(8,128)(2,1)} %get-tuple-element.23.v_ref), custom_call_target="tpu_custom_call" | custom-call | tf_op jit(solution)/shard_map/pallas_call | solution.py:86
  119.7 1.6 maximum_maximum_fusion
  121.2 1.9 fusion.61
  123.4 10.0 %all-to-all-done.1 = bf16[8,512,256]{2,1,0:T(8,128)(2,1)S(1)} async-done(((bf16[8,512,256]{2,1,0:T(8,128)(2,1)}), bf16[8,512,256]{2,1,0:T(8,128)(2,1)S(1)}, u32[]{:S(2)}, u32[]{:S(2)}) %all-to-all-start.1) | async-done | bytes 2097184 | tf_op jit(solution)/shard_map/all_to_all | solution.py:104
  134.7 14.2 %shard_map.173 = (bf16[512,256]{1,0:T(8,128)(2,1)}, bf16[512,256]{1,0:T(8,128)(2,1)}) custom-call(bf16[4096,256]{1,0:T(8,128)(2,1)} %get-tuple-element.22.q_ref, bf16[4096,256]{1,0:T(8,128)(2,1)} %bitcast.121, bf16[512,256]{1,0:T(8,128)(2,1)} %get-tuple-element.30.k_ref, bf16[512,256]{1,0:T(8,128)(2,1)} %get-tuple-element.29.v_ref), custom_call_target="tpu_custom_call" | custom-call | tf_op jit(solution)/shard_map/pallas_call | solution.py:91
  148.9 2.0 fusion.62
  154.4 4.6 %all-to-all-start.2 = ((f32[128,1,768]{2,1,0:T(1,128)}), f32[128,1,768]{2,1,0:T(1,128)S(1)}, u32[]{:S(2)}, u32[]{:S(2)}) async-start(f32[128,1,768]{2,1,0:T(1,128)} %all_to_all.29), calls=%async_computation.2 | async-start | bytes 786432 | tf_op jit(solution)/shard_map/all_to_all | solution.py:113
  159.0 3.2 %fusion.8 = f32[256,256]{1,0:T(8,128)} fusion(bf16[1024,256]{1,0:T(8,128)(2,1)} %bitcast.125, f32[1024,256]{1,0:T(8,128)} %copy-done.12, f32[1024]{0:T(1024)S(1)} %copy-done.22, s32[1,1,512,1024]{3,2,1,0:T(8,128)S(1)} %copy-done.7, f32[512,256]{0,1:T(8,128)} %get-tuple-element.37, f32[256,512]{1,0:T(8,128)S(1)} %get-tuple-element.33, ...), kind=kOutput, calls=%fused_computation.15 | convolution fusion | flops 406585344 | bytes 4990976 | tf_op jit(solution)/shard_map/gh,ge->he/dot_general | solution.py:244
  162.3 8.7 %all-to-all-done.2 = f32[128,1,768]{2,1,0:T(1,128)S(1)} async-done(((f32[128,1,768]{2,1,0:T(1,128)}), f32[128,1,768]{2,1,0:T(1,128)S(1)}, u32[]{:S(2)}, u32[]{:S(2)}) %all-to-all-start.2) | async-done | bytes 393248 | tf_op jit(solution)/shard_map/all_to_all | solution.py:113
  172.0 1.8 reduce.6
  174.6 4.6 %all-to-all-start.3 = ((bf16[128,2,384]{2,1,0:T(2,128)(2,1)}), bf16[128,2,384]{2,1,0:T(2,128)(2,1)S(1)}, u32[]{:S(2)}, u32[]{:S(2)}) async-start(bf16[128,2,384]{2,1,0:T(2,128)(2,1)} %reshape.165), calls=%async_computation.3 | async-start | bytes 393216 | tf_op jit(solution)/shard_map/all_to_all | solution.py:116
  179.6 9.7 %all-to-all-done.3 = bf16[128,2,384]{2,1,0:T(2,128)(2,1)S(1)} async-done(((bf16[128,2,384]{2,1,0:T(2,128)(2,1)}), bf16[128,2,384]{2,1,0:T(2,128)(2,1)S(1)}, u32[]{:S(2)}, u32[]{:S(2)}) %all-to-all-start.3) | async-done | bytes 196640 | tf_op jit(solution)/shard_map/all_to_all | solution.py:116
  190.6 22.0 %all_to_all.36 = f32[128,8,256]{2,1,0:T(8,128)S(1)} all-to-all(f32[128,8,256]{2,1,0:T(8,128)S(1)} %bitcast.122), channel_id=1, replica_groups=mesh['row'=16,'col'=8] {'row','col'}, dimensions={0} | all-to-all | bytes 2097152 | tf_op jit(solution)/shard_map/all_to_all | solution.py:113
  213.6 5.2 %all-to-all-start.5 = ((bf16[128,8,256]{2,1,0:T(8,128)(2,1)}), bf16[128,8,256]{2,1,0:T(8,128)(2,1)S(1)}, u32[]{:S(2)}, u32[]{:S(2)}) async-start(bf16[128,8,256]{2,1,0:T(8,128)(2,1)} %broadcast_in_dim.17), calls=%async_computation.5 | async-start | bytes 1048576 | tf_op jit(solution)/shard_map/all_to_all | solution.py:116
  220.8 11.4 %all-to-all-done.5 = bf16[128,8,256]{2,1,0:T(8,128)(2,1)S(1)} async-done(((bf16[128,8,256]{2,1,0:T(8,128)(2,1)}), bf16[128,8,256]{2,1,0:T(8,128)(2,1)S(1)}, u32[]{:S(2)}, u32[]{:S(2)}) %all-to-all-start.5) | async-done | bytes 524320 | tf_op jit(solution)/shard_map/all_to_all | solution.py:116
  (115 shorter events, 28.3 us)
Async XLA Ops:
  0.6 96.7 %copy-start = (bf16[256,256]{1,0:T(8,128)(2,1)S(1)}, bf16[256,256]{1,0:T(8,128)(2,1)}, u32[]{:S(2)}) copy-start(bf16[256,256]{1,0:T(8,128)(2,1)} %param.21) | copy-start | bytes 393220
  1.3 34.4 %copy-start.21 = (f32[1024]{0:T(1024)}, f32[1024]{0:T(1024)S(1)}, u32[]{:S(2)}) copy-start(f32[1024]{0:T(1024)S(1)} %fusion.49) | copy-start | bytes 12292
  3.4 17.6 %copy-start.1 = (s32[1,1,8,5,128,128]{5,4,3,2,1,0:T(8,128)S(1)}, s32[1,1,8,5,128,128]{5,4,3,2,1,0:T(8,128)}, u32[]{:S(2)}) copy-start(s32[1,1,8,5,128,128]{5,4,3,2,1,0:T(8,128)} %param.13) | copy-start | bytes 7864324
  3.4 29.1 %collective-permute-start = (bf16[1024,256]{1,0:T(8,128)(2,1)}, bf16[1024,256]{1,0:T(8,128)(2,1)}, u32[]{:S(2)}, u32[]{:S(2)}) collective-permute-start(bf16[1024,256]{1,0:T(8,128)(2,1)} %fusion.13), channel_id=1, source_target_pairs={{0,8},{8,16},{16,24},{24,32},{32,40},{40,48},{48,56},{56,64},{64,7... | collective-permute-start | bytes 1572872 | tf_op jit(solution)/shard_map/ppermute | solution.py:98
  5.7 24.0 %collective-permute-start.3 = (bf16[1024,256]{1,0:T(8,128)(2,1)}, bf16[1024,256]{1,0:T(8,128)(2,1)}, u32[]{:S(2)}, u32[]{:S(2)}) collective-permute-start(bf16[1024,256]{1,0:T(8,128)(2,1)} %fusion.13), channel_id=1, source_target_pairs={{1,0},{2,1},{3,2},{4,3},{5,4},{6,5},{7,6},{9,8},{10,9},{11,10},{12... | collective-permute-start | bytes 1572872 | tf_op jit(solution)/shard_map/ppermute | solution.py:98
  7.0 24.1 %collective-permute-start.2 = (bf16[1024,256]{1,0:T(8,128)(2,1)}, bf16[1024,256]{1,0:T(8,128)(2,1)}, u32[]{:S(2)}, u32[]{:S(2)}) collective-permute-start(bf16[1024,256]{1,0:T(8,128)(2,1)} %fusion.13), channel_id=1, source_target_pairs={{0,1},{1,2},{2,3},{3,4},{4,5},{5,6},{6,7},{8,9},{9,10},{10,11},{11... | collective-permute-start | bytes 1572872 | tf_op jit(solution)/shard_map/ppermute | solution.py:98
  14.1 19.7 %collective-permute-start.1 = (bf16[1024,256]{1,0:T(8,128)(2,1)}, bf16[1024,256]{1,0:T(8,128)(2,1)}, u32[]{:S(2)}, u32[]{:S(2)}) collective-permute-start(bf16[1024,256]{1,0:T(8,128)(2,1)} %fusion.13), channel_id=1, source_target_pairs={{8,0},{16,8},{24,16},{32,24},{40,32},{48,40},{56,48},{64,56},{72,6... | collective-permute-start | bytes 1572872 | tf_op jit(solution)/shard_map/ppermute | solution.py:98
  20.3 15.4 %copy-start.28 = (f32[512]{0:T(512)}, f32[512]{0:T(512)S(1)}, u32[]{:S(2)}) copy-start(f32[512]{0:T(512)S(1)} %convert_add_fusion.2) | copy-start | bytes 6148
  21.2 9.9 %copy-start.3 = (bf16[8,5,128,128]{3,2,0,1:T(8,128)(2,1)S(1)}, bf16[8,5,128,128]{3,2,0,1:T(8,128)(2,1)}, u32[]{:S(2)}) copy-start(bf16[8,5,128,128]{3,2,0,1:T(8,128)(2,1)} %fusion.5) | copy-start | bytes 3932164
  38.5 15.9 %copy-start.30 = (bf16[256]{0:T(256)(128)(2,1)S(1)}, bf16[256]{0:T(256)(128)(2,1)}, u32[]{:S(2)}) copy-start(bf16[256]{0:T(256)(128)(2,1)} %param.22) | copy-start | bytes 1540
  38.5 18.4 %copy-start.15 = (bf16[256,256]{1,0:T(8,128)(2,1)S(1)}, bf16[256,256]{1,0:T(8,128)(2,1)}, u32[]{:S(2)}) copy-start(bf16[256,256]{1,0:T(8,128)(2,1)} %param.20) | copy-start | bytes 393220
  38.5 44.7 %all-to-all-start = ((bf16[8,512,256]{2,1,0:T(8,128)(2,1)}), bf16[8,512,256]{2,1,0:T(8,128)(2,1)S(1)}, u32[]{:S(2)}, u32[]{:S(2)}) async-start(bf16[8,512,256]{2,1,0:T(8,128)(2,1)} %broadcast_in_dim.12), calls=%async_computation | async-start | bytes 4194304 | tf_op jit(solution)/shard_map/all_to_all | solution.py:104
  87.8 10.8 %copy-start.27 = (f32[1,1,512]{2,1,0:T(1,128)S(1)}, f32[1,1,512]{2,1,0:T(1,128)}, u32[]{:S(2)}) copy-start(f32[1,1,512]{2,1,0:T(1,128)} %param.23) | copy-start | bytes 6148
  87.8 10.8 %copy-start.23 = (f32[256]{0:T(256)S(1)}, f32[256]{0:T(256)}, u32[]{:S(2)}) copy-start(f32[256]{0:T(256)} %convert_element_type.162) | copy-start | bytes 3076
  102.0 31.4 %all-to-all-start.1 = ((bf16[8,512,256]{2,1,0:T(8,128)(2,1)}), bf16[8,512,256]{2,1,0:T(8,128)(2,1)S(1)}, u32[]{:S(2)}, u32[]{:S(2)}) async-start(bf16[8,512,256]{2,1,0:T(8,128)(2,1)} %broadcast_in_dim.15), calls=%async_computation.1 | async-start | bytes 4194304 | tf_op jit(solution)/shard_map/all_to_all | solution.py:104
  118.3 4.8 %copy-start.4 = (bf16[512,256]{1,0:T(8,128)(2,1)S(1)}, bf16[512,256]{1,0:T(8,128)(2,1)}, u32[]{:S(2)}) copy-start(bf16[512,256]{1,0:T(8,128)(2,1)} %shard_map.172) | copy-start | bytes 786436
  118.3 4.8 %copy-start.18 = (bf16[256,256]{1,0:T(8,128)(2,1)S(1)}, bf16[256,256]{1,0:T(8,128)(2,1)}, u32[]{:S(2)}) copy-start(bf16[256,256]{1,0:T(8,128)(2,1)} %param.18) | copy-start | bytes 393220
  118.3 4.8 %copy-start.24 = (f32[256]{0:T(256)S(1)}, f32[256]{0:T(256)}, u32[]{:S(2)}) copy-start(f32[256]{0:T(256)} %convert_element_type.162) | copy-start | bytes 3076
  148.9 3.2 %copy-start.9 = (bf16[512,256]{1,0:T(8,128)(2,1)S(1)}, bf16[512,256]{1,0:T(8,128)(2,1)}, u32[]{:S(2)}) copy-start(bf16[512,256]{1,0:T(8,128)(2,1)} %get-tuple-element.16) | copy-start | bytes 786436
  148.9 3.3 %copy-start.16 = (bf16[256,256]{1,0:T(8,128)(2,1)S(1)}, bf16[256,256]{1,0:T(8,128)(2,1)}, u32[]{:S(2)}) copy-start(bf16[256,256]{1,0:T(8,128)(2,1)} %param.20) | copy-start | bytes 393220
  148.9 4.3 %copy-start.8 = (f32[384,256]{1,0:T(8,128)S(1)}, f32[384,256]{1,0:T(8,128)}, u32[]{:S(2)}) copy-start(f32[384,256]{1,0:T(8,128)} %maximum_maximum_fusion) | copy-start | bytes 1179652
  152.1 6.9 %copy-start.7 = (s32[1,1,512,1024]{3,2,1,0:T(8,128)S(1)}, s32[1,1,512,1024]{3,2,1,0:T(8,128)}, u32[]{:S(2)}) copy-start(s32[1,1,512,1024]{3,2,1,0:T(8,128)} %param.15) | copy-start | bytes 6291460
  152.1 6.9 %copy-start.22 = (f32[1024]{0:T(1024)S(1)}, f32[1024]{0:T(1024)}, u32[]{:S(2)}) copy-start(f32[1024]{0:T(1024)} %copy-done.21) | copy-start | bytes 12292
  152.1 6.9 %copy-start.29 = (f32[512]{0:T(512)S(1)}, f32[512]{0:T(512)}, u32[]{:S(2)}) copy-start(f32[512]{0:T(512)} %copy-done.28) | copy-start | bytes 6148
  154.4 16.6 %all-to-all-start.2 = ((f32[128,1,768]{2,1,0:T(1,128)}), f32[128,1,768]{2,1,0:T(1,128)S(1)}, u32[]{:S(2)}, u32[]{:S(2)}) async-start(f32[128,1,768]{2,1,0:T(1,128)} %all_to_all.29), calls=%async_computation.2 | async-start | bytes 786432 | tf_op jit(solution)/shard_map/all_to_all | solution.py:113
  162.3 16.9 %copy-start.10 = (bf16[512,256]{1,0:T(8,128)(2,1)S(1)}, bf16[512,256]{1,0:T(8,128)(2,1)}, u32[]{:S(2)}) copy-start(bf16[512,256]{1,0:T(8,128)(2,1)} %get-tuple-element.16) | copy-start | bytes 786436
  162.3 17.2 %copy-start.13 = (f32[256,256]{1,0:T(8,128)S(1)}, f32[256,256]{1,0:T(8,128)}, u32[]{:S(2)}) copy-start(f32[256,256]{1,0:T(8,128)} %fusion.61) | copy-start | bytes 786436
  162.3 17.2 %copy-start.14 = (f32[256,256]{1,0:T(8,128)S(1)}, f32[256,256]{1,0:T(8,128)}, u32[]{:S(2)}) copy-start(f32[256,256]{1,0:T(8,128)} %fusion.62) | copy-start | bytes 786436
  162.3 17.2 %copy-start.19 = (f32[256,256]{1,0:T(8,128)S(1)}, f32[256,256]{1,0:T(8,128)}, u32[]{:S(2)}) copy-start(f32[256,256]{1,0:T(8,128)} %fusion.8) | copy-start | bytes 786436
  174.6 14.7 %all-to-all-start.3 = ((bf16[128,2,384]{2,1,0:T(2,128)(2,1)}), bf16[128,2,384]{2,1,0:T(2,128)(2,1)S(1)}, u32[]{:S(2)}, u32[]{:S(2)}) async-start(bf16[128,2,384]{2,1,0:T(2,128)(2,1)} %reshape.165), calls=%async_computation.3 | async-start | bytes 393216 | tf_op jit(solution)/shard_map/all_to_all | solution.py:116
  190.6 28.3 %copy-start.25 = (f32[512]{0:T(512)S(1)}, f32[512]{0:T(512)}, u32[]{:S(2)}) copy-start(f32[512]{0:T(512)} %get-tuple-element.20) | copy-start | bytes 6148
  213.6 18.6 %all-to-all-start.5 = ((bf16[128,8,256]{2,1,0:T(8,128)(2,1)}), bf16[128,8,256]{2,1,0:T(8,128)(2,1)S(1)}, u32[]{:S(2)}, u32[]{:S(2)}) async-start(bf16[128,8,256]{2,1,0:T(8,128)(2,1)} %broadcast_in_dim.17), calls=%async_computation.5 | async-start | bytes 1048576 | tf_op jit(solution)/shard_map/all_to_all | solution.py:116
  (8 other events, 13.1 us)

commit v4 on v3

--- a/solution.py
+++ b/solution.py
@@ -17,6 +17,7 @@
 
 EPS = 1e-06
 SHIFT = math.log(NT)
+KB = 1024
 
 def _nt(a, b):
     return lax.dot_general(a, b, (((1,), (1,)), ((), ())), preferred_element_type=jnp.float32)
@@ -28,10 +29,10 @@
     return jnp.tanh(_nt(q, k) * (0.5 / math.sqrt(HD)) - 0.5 * SHIFT)
 
 def _fwd_kernel(q_ref, k_ref, v_ref, o_ref, acc_ref):
-    blocks = k_ref.shape[0] // NT
+    blocks = k_ref.shape[0] // KB
     acc_ref[...] = jnp.zeros_like(acc_ref)
     def step(j, carry):
-        rows = pl.ds(pl.multiple_of(j * NT, NT), NT)
+        rows = pl.ds(pl.multiple_of(j * KB, KB), KB)
         for h in range(HEADS):
             cols = slice(h * HD, (h + 1) * HD)
             t = _half_tanh(q_ref[:, cols], k_ref[rows, cols])
@@ -42,10 +43,10 @@
     o_ref[...] = acc_ref[...].astype(o_ref.dtype)
 
 def _gq_kernel(q_ref, g_ref, k_ref, v_ref, o_ref, acc_ref):
-    blocks = k_ref.shape[0] // NT
+    blocks = k_ref.shape[0] // KB
     acc_ref[...] = jnp.zeros_like(acc_ref)
     def step(j, carry):
-        rows = pl.ds(pl.multiple_of(j * NT, NT), NT)
+        rows = pl.ds(pl.multiple_of(j * KB, KB), KB)
         for h in range(HEADS):
             cols = slice(h * HD, (h + 1) * HD)
             k = k_ref[rows, cols]
@@ -58,11 +59,11 @@
     o_ref[...] = acc_ref[...].astype(o_ref.dtype)
 
 def _gkv_kernel(q_ref, g_ref, k_ref, v_ref, dk_ref, dv_ref, acck_ref, accv_ref):
-    blocks = q_ref.shape[0] // NT
+    blocks = q_ref.shape[0] // KB
     acck_ref[...] = jnp.zeros_like(acck_ref)
     accv_ref[...] = jnp.zeros_like(accv_ref)
     def step(i, carry):
-        rows = pl.ds(pl.multiple_of(i * NT, NT), NT)
+        rows = pl.ds(pl.multiple_of(i * KB, KB), KB)
         for h in range(HEADS):
             cols = slice(h * HD, (h + 1) * HD)
             q = q_ref[rows, cols]
@@ -219,12 +220,8 @@
     grad_proj = rms_backward(grad_mixed, pnormed, pscale).astype(jnp.bfloat16)
     g_out = jnp.einsum("nh,ne->he", attended, grad_proj, preferred_element_type=jnp.float32)
     grad_attn = jnp.dot(grad_proj, w_out.T, preferred_element_type=jnp.float32).astype(jnp.bfloat16)
-    devices = lax.axis_size("row") * lax.axis_size("col")
-    early = jnp.concatenate([g_out, g_score[None], jnp.zeros((3 * devices - H - 1, H), jnp.float32)])
 
     grad_attn_all = gather_tiles(grad_attn, "col").reshape(-1, H)
-    early, grad_attn_all = lax.optimization_barrier((early, grad_attn_all))
-    early = all_reduce_a2a(early.reshape(devices, -1), ("row", "col")).reshape(-1, H)
 
     grad_query = attend_gq(query_own, grad_attn, key_all, value_all)
     grad_key, grad_val = attend_gkv(query_all, grad_attn_all, key_own, value_own)
@@ -243,11 +240,15 @@
     grad_pre = (gate_live[:, None] * grad_hidden * silu_grad(preact)).astype(jnp.bfloat16)
     g_msg = jnp.einsum("gh,ge->he", message, grad_pre, preferred_element_type=jnp.float32)
 
-    late = jnp.concatenate([g_msg, g_query, g_key, g_value], axis=0)
-    early, late = lax.optimization_barrier((early, late))
-    late = all_reduce_a2a(late, ("row", "col")).reshape(-1, H)
-    outs = [late[i * H:(i + 1) * H] for i in range(4)] + [early[:H]]
-    g_score_sum = early[H]
+    devices = lax.axis_size("row") * lax.axis_size("col")
+    used = 5 * H + 1
+    per_device = -(-used * H // (devices * 128))
+    grads = [g_msg, g_query, g_key, g_value, g_out, g_score[None]]
+    grads.append(jnp.zeros((per_device * devices * 128 // H - used, H), jnp.float32))
+    buffer = jnp.concatenate(grads, axis=0).reshape(devices, per_device, 128)
+    summed = all_reduce_a2a(buffer, ("row", "col")).reshape(-1, H)
+    outs = [summed[i * H:(i + 1) * H] for i in range(5)]
+    g_score_sum = summed[5 * H]
     return (value_out[None, None], *outs, g_score_sum)
 
 

time: 234 us -> 214 us (0.915)
  waiting for transfers between devices: 72 us -> 57.3 us
  starting transfers between devices: 46.1 us -> 37.1 us
  blocking collectives: 22 us -> 27.4 us
  other arithmetic: 14.3 us -> 9.44 us
  matrix products: 23.2 us -> 27.7 us
    all_to_all x1 -> x0, waiting for transfers between devices: 8.74 us -> none  [all_reduce_a2a(): chunks = lax.all_to_all(rows_in, axes, 0, 0, tiled=True)]
    all_to_all x2 -> x1, waiting for transfers between devices: 21.2 us -> 15 us  [all_reduce_a2a(): return lax.all_to_all(copies, axes, 0, 0, tiled=True).astype(jnp.float32)]
    all_to_all x1, blocking collectives: 22 us -> 27.4 us  [all_reduce_a2a(): chunks = lax.all_to_all(rows_in, axes, 0, 0, tiled=True)]
    all_to_all x1 -> x0, starting transfers between devices: 4.6 us -> none  [all_reduce_a2a(): chunks = lax.all_to_all(rows_in, axes, 0, 0, tiled=True)]
    all_to_all x2 -> x1, starting transfers between devices: 9.85 us -> 5.42 us  [all_reduce_a2a(): return lax.all_to_all(copies, axes, 0, 0, tiled=True).astype(jnp.float32)]
    concatenate x1, local copies, waits for them, and re-layouts: 0.67 us -> 3.15 us  [body(): buffer = jnp.concatenate(grads, axis=0).reshape(devices, per_device, 128)]
    unnamed x66 -> x54, local copies, waits for them, and re-layouts: 5.02 us -> 4.15 us
  transfers between devices with their start and end apart: 9 -> 7, of which waited for: 6 -> 4; matrix products, arithmetic and copies ran while one was open for 11% -> 10% of each run, Pallas kernels for 5% -> 5%
where the time goes in v4:
time: 214 us; the launch traced here: 213 us
  waiting for transfers between devices  57.3 us (27%)
  starting transfers between devices  37.1 us (17%)
  Pallas kernels  34.6 us (16%)
  matrix products  27.7 us (13%)
  blocking collectives  27.4 us (13%)
  local copies, waits for them, and re-layouts  17.1 us (8%)
  other arithmetic  9.44 us (4%)
  between operations  2.43 us (1%)
    all_to_all x2, waiting for transfers between devices, gather_tiles(): return lax.all_to_all(copies, axis, 0, 0, tiled=True)  35.2 us
    all_to_all x1, blocking collectives, all_reduce_a2a(): chunks = lax.all_to_all(rows_in, axes, 0, 0, tiled=True)  27.4 us
    all_to_all x2, starting transfers between devices, gather_tiles(): return lax.all_to_all(copies, axis, 0, 0, tiled=True)  19.7 us
    all_to_all x1, waiting for transfers between devices, all_reduce_a2a(): return lax.all_to_all(copies, axes, 0, 0, tiled=True).astype(jnp.float32)  15 us
    pallas_call x1, Pallas kernels, attend_gkv(): pl.pallas_call(_gkv_kernel, out_shape=(sh, sh), scratch_shapes=[pltpu.VME...  14.1 us
    ppermute x4, starting transfers between devices, from_neighbour(): return lax.ppermute(array, axis, pairs)  12 us
    pallas_call x1, Pallas kernels, attend_gq(): pl.pallas_call(_gq_kernel, out_shape=jax.ShapeDtypeStruct(q.shape, jnp.bf...  11.5 us
    pallas_call x1, Pallas kernels, attend_fwd(): pl.pallas_call(_fwd_kernel, out_shape=jax.ShapeDtypeStruct(q.shape, jnp.b...  8.97 us
  transfers between devices with their start and end apart: 7, of which 4 were waited for; matrix products, arithmetic and copies ran while one was open for 10% of the time, Pallas kernels for 5%

profile of v4, /device:TPU:0, one launch (start us, length us, event | category | flops | bytes accessed | tf_op | source)
XLA Modules:
  0.0 213.0 jit_solution(6606720884111627008)
XLA Ops:
  1.4 2.0 fusion.13
  3.4 2.3 %collective-permute-start = (bf16[1024,256]{1,0:T(8,128)(2,1)}, bf16[1024,256]{1,0:T(8,128)(2,1)}, u32[]{:S(2)}, u32[]{:S(2)}) collective-permute-start(bf16[1024,256]{1,0:T(8,128)(2,1)} %fusion.13), channel_id=1, source_target_pairs={{0,8},{8,16},{16,24},{24,32},{32,40},{40,48},{48,56},{56,64},{64,7... | collective-permute-start | bytes 1572872 | tf_op jit(solution)/shard_map/ppermute | solution.py:99
  7.0 7.1 %collective-permute-start.2 = (bf16[1024,256]{1,0:T(8,128)(2,1)}, bf16[1024,256]{1,0:T(8,128)(2,1)}, u32[]{:S(2)}, u32[]{:S(2)}) collective-permute-start(bf16[1024,256]{1,0:T(8,128)(2,1)} %fusion.13), channel_id=1, source_target_pairs={{0,1},{1,2},{2,3},{3,4},{4,5},{5,6},{6,7},{8,9},{9,10},{10,11},{11... | collective-permute-start | bytes 1572872 | tf_op jit(solution)/shard_map/ppermute | solution.py:99
  15.4 3.1 %fusion.5 = bf16[8,5,128,128]{3,2,0,1:T(8,128)(2,1)} fusion(s32[1,1,8,5,128,128]{5,4,3,2,1,0:T(8,128)} %param.13), kind=kLoop, calls=%fused_computation.11 | loop fusion | flops 655360 | bytes 3932160 | tf_op jit(solution)/shard_map/convert.7
  18.5 1.8 reduce_sum.84
  21.2 1.4 fusion.21
  22.7 7.0 %collective-permute-done.3 = bf16[1024,256]{1,0:T(8,128)(2,1)} collective-permute-done((bf16[1024,256]{1,0:T(8,128)(2,1)}, bf16[1024,256]{1,0:T(8,128)(2,1)}, u32[]{:S(2)}, u32[]{:S(2)}) %collective-permute-start.3) | collective-permute-done | bytes 524320 | tf_op jit(solution)/shard_map/ppermute | solution.py:99
  29.7 1.4 fusion.38
  32.5 1.3 convolution_add_fusion.1
  33.9 1.6 fusion.6
  37.0 1.5 broadcast_in_dim.10
  38.5 15.9 %all-to-all-start = ((bf16[8,512,256]{2,1,0:T(8,128)(2,1)}), bf16[8,512,256]{2,1,0:T(8,128)(2,1)S(1)}, u32[]{:S(2)}, u32[]{:S(2)}) async-start(bf16[8,512,256]{2,1,0:T(8,128)(2,1)} %broadcast_in_dim.10), calls=%async_computation | async-start | bytes 4194304 | tf_op jit(solution)/shard_map/all_to_all | solution.py:105
  58.2 25.0 %all-to-all-done = bf16[8,512,256]{2,1,0:T(8,128)(2,1)S(1)} async-done(((bf16[8,512,256]{2,1,0:T(8,128)(2,1)}), bf16[8,512,256]{2,1,0:T(8,128)(2,1)S(1)}, u32[]{:S(2)}, u32[]{:S(2)}) %all-to-all-start) | async-done | bytes 2097184 | tf_op jit(solution)/shard_map/all_to_all | solution.py:105
  83.2 1.8 convolution_convert_fusion
  85.0 2.7 %fusion.57 = (bf16[4096,256]{1,0:T(8,128)(2,1)}, bf16[4096,256]{1,0:T(8,128)(2,1)}, bf16[4096,256]{1,0:T(8,128)(2,1)}) fusion(bf16[4096,768]{1,0:T(8,128)(2,1)S(1)} %convolution_convert_fusion), kind=kLoop, calls=%fused_computation.90 | loop fusion | bytes 12582912 | tf_op jit(solution)/shard_map/slice | solution.py:202
  87.8 9.0 %shard_map.171 = bf16[512,256]{1,0:T(8,128)(2,1)} custom-call(bf16[512,256]{1,0:T(8,128)(2,1)} %get-tuple-element.24.q_ref, bf16[4096,256]{1,0:T(8,128)(2,1)} %get-tuple-element.16.k_ref, bf16[4096,256]{1,0:T(8,128)(2,1)} %get-tuple-element.15.v_ref), custom_call_target="tpu_custom_call" | custom-call | tf_op jit(solution)/shard_map/pallas_call | solution.py:83
  99.9 1.5 broadcast_in_dim.11
  101.4 3.8 %all-to-all-start.1 = ((bf16[8,512,256]{2,1,0:T(8,128)(2,1)}), bf16[8,512,256]{2,1,0:T(8,128)(2,1)S(1)}, u32[]{:S(2)}, u32[]{:S(2)}) async-start(bf16[8,512,256]{2,1,0:T(8,128)(2,1)} %broadcast_in_dim.11), calls=%async_computation.1 | async-start | bytes 4194304 | tf_op jit(solution)/shard_map/all_to_all | solution.py:105
  105.2 11.5 %shard_map.172 = bf16[512,256]{1,0:T(8,128)(2,1)} custom-call(bf16[512,256]{1,0:T(8,128)(2,1)} %get-tuple-element.24.q_ref, bf16[512,256]{1,0:T(8,128)(2,1)} %copy-done.10, bf16[4096,256]{1,0:T(8,128)(2,1)} %get-tuple-element.16.k_ref, bf16[4096,256]{1,0:T(8,128)(2,1)} %get-tuple-element.15.v_ref), custom_call_target="tpu_custom_call" | custom-call | tf_op jit(solution)/shard_map/pallas_call | solution.py:87
  116.7 1.9 fusion.62
  118.6 2.1 convolution_add_fusion.4
  120.6 2.0 fusion.53
  122.7 10.1 %all-to-all-done.1 = bf16[8,512,256]{2,1,0:T(8,128)(2,1)S(1)} async-done(((bf16[8,512,256]{2,1,0:T(8,128)(2,1)}), bf16[8,512,256]{2,1,0:T(8,128)(2,1)S(1)}, u32[]{:S(2)}, u32[]{:S(2)}) %all-to-all-start.1) | async-done | bytes 2097184 | tf_op jit(solution)/shard_map/all_to_all | solution.py:105
  134.1 14.1 %shard_map.173 = (bf16[512,256]{1,0:T(8,128)(2,1)}, bf16[512,256]{1,0:T(8,128)(2,1)}) custom-call(bf16[4096,256]{1,0:T(8,128)(2,1)} %get-tuple-element.14.q_ref, bf16[4096,256]{1,0:T(8,128)(2,1)} %bitcast.112, bf16[512,256]{1,0:T(8,128)(2,1)} %get-tuple-element.23.k_ref, bf16[512,256]{1,0:T(8,128)(2,1)} %get-tuple-element.22.v_ref), custom_call_target="tpu_custom_call" | custom-call | tf_op jit(solution)/shard_map/pallas_call | solution.py:92
  148.2 2.0 fusion.64
  150.2 2.0 fusion.63
  152.2 1.4 convolution_add_fusion.3
  154.8 3.3 %fusion.8 = f32[256,256]{1,0:T(8,128)} fusion(bf16[1024,256]{1,0:T(8,128)(2,1)} %bitcast.115, f32[1024,256]{1,0:T(8,128)} %copy-done.11, f32[1024]{0:T(1024)S(1)} %copy-done.17, s32[1,1,512,1024]{3,2,1,0:T(8,128)S(1)} %copy-done.6, f32[512,256]{0,1:T(8,128)} %get-tuple-element.30, f32[256,512]{1,0:T(8,128)S(1)} %get-tuple-element.26, ...), kind=kOutput, calls=%fused_computation.15 | convolution fusion | flops 406585344 | bytes 4990976 | tf_op jit(solution)/shard_map/gh,ge->he/dot_general | solution.py:241
  158.1 3.2 %concatenate.7 = f32[1344,256]{1,0:T(8,128)S(1)} concatenate(f32[256,256]{1,0:T(8,128)} %fusion.8, f32[256,256]{1,0:T(8,128)S(1)} %copy-done.7, f32[256,256]{1,0:T(8,128)} %fusion.63, f32[256,256]{1,0:T(8,128)} %fusion.64, f32[256,256]{1,0:T(8,128)S(1)} %copy-done.8, f32[1,256]{1,0:T(1,128)S(1)} %bitcast.117, f32[63,256]{1,0:T(8,128)S(1)} %broadcast_in_dim.13), dimensions={0} | concatenate | bytes 2752512 | tf_op jit(solution)/shard_map/concatenate | solution.py:248
  161.5 27.4 %all_to_all.20 = f32[128,21,128]{2,1,0:T(8,128)S(1)} all-to-all(f32[128,21,128]{2,1,0:T(8,128)S(1)} %reshape.142), channel_id=1, replica_groups=mesh['row'=16,'col'=8] {'row','col'}, dimensions={0} | all-to-all | bytes 2752512 | tf_op jit(solution)/shard_map/all_to_all | solution.py:114
  190.0 5.4 %all-to-all-start.3 = ((bf16[128,21,128]{2,1,0:T(8,128)(2,1)}), bf16[128,21,128]{2,1,0:T(8,128)(2,1)S(1)}, u32[]{:S(2)}, u32[]{:S(2)}) async-start(bf16[128,21,128]{2,1,0:T(8,128)(2,1)} %broadcast_in_dim.14), calls=%async_computation.3 | async-start | bytes 1572864 | tf_op jit(solution)/shard_map/all_to_all | solution.py:117
  196.0 15.0 %all-to-all-done.3 = bf16[128,21,128]{2,1,0:T(8,128)(2,1)S(1)} async-done(((bf16[128,21,128]{2,1,0:T(8,128)(2,1)}), bf16[128,21,128]{2,1,0:T(8,128)(2,1)S(1)}, u32[]{:S(2)}, u32[]{:S(2)}) %all-to-all-start.3) | async-done | bytes 688160 | tf_op jit(solution)/shard_map/all_to_all | solution.py:117
  (90 shorter events, 18.8 us)
Async XLA Ops:
  0.6 96.1 %copy-start = (bf16[256,256]{1,0:T(8,128)(2,1)S(1)}, bf16[256,256]{1,0:T(8,128)(2,1)}, u32[]{:S(2)}) copy-start(bf16[256,256]{1,0:T(8,128)(2,1)} %param.21) | copy-start | bytes 393220
  1.3 34.4 %copy-start.16 = (f32[1024]{0:T(1024)}, f32[1024]{0:T(1024)S(1)}, u32[]{:S(2)}) copy-start(f32[1024]{0:T(1024)S(1)} %fusion.49) | copy-start | bytes 12292
  3.4 17.6 %copy-start.1 = (s32[1,1,8,5,128,128]{5,4,3,2,1,0:T(8,128)S(1)}, s32[1,1,8,5,128,128]{5,4,3,2,1,0:T(8,128)}, u32[]{:S(2)}) copy-start(s32[1,1,8,5,128,128]{5,4,3,2,1,0:T(8,128)} %param.13) | copy-start | bytes 7864324
  3.4 29.1 %collective-permute-start = (bf16[1024,256]{1,0:T(8,128)(2,1)}, bf16[1024,256]{1,0:T(8,128)(2,1)}, u32[]{:S(2)}, u32[]{:S(2)}) collective-permute-start(bf16[1024,256]{1,0:T(8,128)(2,1)} %fusion.13), channel_id=1, source_target_pairs={{0,8},{8,16},{16,24},{24,32},{32,40},{40,48},{48,56},{56,64},{64,7... | collective-permute-start | bytes 1572872 | tf_op jit(solution)/shard_map/ppermute | solution.py:99
  5.7 24.0 %collective-permute-start.3 = (bf16[1024,256]{1,0:T(8,128)(2,1)}, bf16[1024,256]{1,0:T(8,128)(2,1)}, u32[]{:S(2)}, u32[]{:S(2)}) collective-permute-start(bf16[1024,256]{1,0:T(8,128)(2,1)} %fusion.13), channel_id=1, source_target_pairs={{1,0},{2,1},{3,2},{4,3},{5,4},{6,5},{7,6},{9,8},{10,9},{11,10},{12... | collective-permute-start | bytes 1572872 | tf_op jit(solution)/shard_map/ppermute | solution.py:99
  7.0 24.1 %collective-permute-start.2 = (bf16[1024,256]{1,0:T(8,128)(2,1)}, bf16[1024,256]{1,0:T(8,128)(2,1)}, u32[]{:S(2)}, u32[]{:S(2)}) collective-permute-start(bf16[1024,256]{1,0:T(8,128)(2,1)} %fusion.13), channel_id=1, source_target_pairs={{0,1},{1,2},{2,3},{3,4},{4,5},{5,6},{6,7},{8,9},{9,10},{10,11},{11... | collective-permute-start | bytes 1572872 | tf_op jit(solution)/shard_map/ppermute | solution.py:99
  14.1 19.7 %collective-permute-start.1 = (bf16[1024,256]{1,0:T(8,128)(2,1)}, bf16[1024,256]{1,0:T(8,128)(2,1)}, u32[]{:S(2)}, u32[]{:S(2)}) collective-permute-start(bf16[1024,256]{1,0:T(8,128)(2,1)} %fusion.13), channel_id=1, source_target_pairs={{8,0},{16,8},{24,16},{32,24},{40,32},{48,40},{56,48},{64,56},{72,6... | collective-permute-start | bytes 1572872 | tf_op jit(solution)/shard_map/ppermute | solution.py:99
  18.5 2.8 %copy-start.4 = (bf16[1,1,1024,256]{3,2,1,0:T(8,128)(2,1)S(1)}, bf16[1,1,1024,256]{3,2,1,0:T(8,128)(2,1)}, u32[]{:S(2)}) copy-start(bf16[1,1,1024,256]{3,2,1,0:T(8,128)(2,1)} %param.12) | copy-start | bytes 1572868
  20.3 15.4 %copy-start.23 = (f32[512]{0:T(512)}, f32[512]{0:T(512)S(1)}, u32[]{:S(2)}) copy-start(f32[512]{0:T(512)S(1)} %convert_add_fusion.2) | copy-start | bytes 6148
  21.2 9.9 %copy-start.3 = (bf16[8,5,128,128]{3,2,0,1:T(8,128)(2,1)S(1)}, bf16[8,5,128,128]{3,2,0,1:T(8,128)(2,1)}, u32[]{:S(2)}) copy-start(bf16[8,5,128,128]{3,2,0,1:T(8,128)(2,1)} %fusion.5) | copy-start | bytes 3932164
  33.8 1.6 copy-start.15
  33.8 1.9 copy-start.5
  35.4 1.2 copy-start.14
  35.8 1.0 copy-start.11
  38.5 15.9 %copy-start.25 = (bf16[256]{0:T(256)(128)(2,1)S(1)}, bf16[256]{0:T(256)(128)(2,1)}, u32[]{:S(2)}) copy-start(bf16[256]{0:T(256)(128)(2,1)} %param.22) | copy-start | bytes 1540
  38.5 18.4 %copy-start.12 = (bf16[256,256]{1,0:T(8,128)(2,1)S(1)}, bf16[256,256]{1,0:T(8,128)(2,1)}, u32[]{:S(2)}) copy-start(bf16[256,256]{1,0:T(8,128)(2,1)} %param.20) | copy-start | bytes 393220
  38.5 44.7 %all-to-all-start = ((bf16[8,512,256]{2,1,0:T(8,128)(2,1)}), bf16[8,512,256]{2,1,0:T(8,128)(2,1)S(1)}, u32[]{:S(2)}, u32[]{:S(2)}) async-start(bf16[8,512,256]{2,1,0:T(8,128)(2,1)} %broadcast_in_dim.10), calls=%async_computation | async-start | bytes 4194304 | tf_op jit(solution)/shard_map/all_to_all | solution.py:105
  87.8 10.2 %copy-start.22 = (f32[1,1,512]{2,1,0:T(1,128)S(1)}, f32[1,1,512]{2,1,0:T(1,128)}, u32[]{:S(2)}) copy-start(f32[1,1,512]{2,1,0:T(1,128)} %param.23) | copy-start | bytes 6148
  87.8 10.2 %copy-start.18 = (f32[256]{0:T(256)S(1)}, f32[256]{0:T(256)}, u32[]{:S(2)}) copy-start(f32[256]{0:T(256)} %convert_element_type.145) | copy-start | bytes 3076
  98.8 2.5 %copy-start.20 = (f32[512]{0:T(512)}, f32[512]{0:T(512)S(1)}, u32[]{:S(2)}) copy-start(f32[512]{0:T(512)S(1)} %broadcast_multiply_fusion.1) | copy-start | bytes 6148
  101.4 31.4 %all-to-all-start.1 = ((bf16[8,512,256]{2,1,0:T(8,128)(2,1)}), bf16[8,512,256]{2,1,0:T(8,128)(2,1)S(1)}, u32[]{:S(2)}, u32[]{:S(2)}) async-start(bf16[8,512,256]{2,1,0:T(8,128)(2,1)} %broadcast_in_dim.11), calls=%async_computation.1 | async-start | bytes 4194304 | tf_op jit(solution)/shard_map/all_to_all | solution.py:105
  132.8 1.3 copy-start.2
  148.2 5.5 %copy-start.9 = (bf16[512,256]{1,0:T(8,128)(2,1)S(1)}, bf16[512,256]{1,0:T(8,128)(2,1)}, u32[]{:S(2)}) copy-start(bf16[512,256]{1,0:T(8,128)(2,1)} %get-tuple-element.10) | copy-start | bytes 786436
  148.2 5.5 %copy-start.13 = (bf16[256,256]{1,0:T(8,128)(2,1)S(1)}, bf16[256,256]{1,0:T(8,128)(2,1)}, u32[]{:S(2)}) copy-start(bf16[256,256]{1,0:T(8,128)(2,1)} %param.20) | copy-start | bytes 393220
  150.2 4.6 %copy-start.6 = (s32[1,1,512,1024]{3,2,1,0:T(8,128)S(1)}, s32[1,1,512,1024]{3,2,1,0:T(8,128)}, u32[]{:S(2)}) copy-start(s32[1,1,512,1024]{3,2,1,0:T(8,128)} %param.15) | copy-start | bytes 6291460
  150.2 4.6 %copy-start.17 = (f32[1024]{0:T(1024)S(1)}, f32[1024]{0:T(1024)}, u32[]{:S(2)}) copy-start(f32[1024]{0:T(1024)} %copy-done.16) | copy-start | bytes 12292
  150.2 4.6 %copy-start.24 = (f32[512]{0:T(512)S(1)}, f32[512]{0:T(512)}, u32[]{:S(2)}) copy-start(f32[512]{0:T(512)} %copy-done.23) | copy-start | bytes 6148
  154.8 3.3 %copy-start.7 = (f32[256,256]{1,0:T(8,128)S(1)}, f32[256,256]{1,0:T(8,128)}, u32[]{:S(2)}) copy-start(f32[256,256]{1,0:T(8,128)} %fusion.62) | copy-start | bytes 786436
  154.8 3.3 %copy-start.8 = (f32[256,256]{1,0:T(8,128)S(1)}, f32[256,256]{1,0:T(8,128)}, u32[]{:S(2)}) copy-start(f32[256,256]{1,0:T(8,128)} %fusion.53) | copy-start | bytes 786436
  154.8 3.3 %copy-start.21 = (f32[256]{0:T(256)S(1)}, f32[256]{0:T(256)}, u32[]{:S(2)}) copy-start(f32[256]{0:T(256)} %get-tuple-element.11) | copy-start | bytes 3076
  188.8 6.6 %copy-start.19 = (f32[512]{0:T(512)S(1)}, f32[512]{0:T(512)}, u32[]{:S(2)}) copy-start(f32[512]{0:T(512)} %get-tuple-element.12) | copy-start | bytes 6148
  190.0 21.1 %all-to-all-start.3 = ((bf16[128,21,128]{2,1,0:T(8,128)(2,1)}), bf16[128,21,128]{2,1,0:T(8,128)(2,1)S(1)}, u32[]{:S(2)}, u32[]{:S(2)}) async-start(bf16[128,21,128]{2,1,0:T(8,128)(2,1)} %broadcast_in_dim.14), calls=%async_computation.3 | async-start | bytes 1572864 | tf_op jit(solution)/shard_map/all_to_all | solution.py:117
  (1 other events, 0.7 us)

commit v5 on v4

--- a/solution.py
+++ b/solution.py
@@ -28,37 +28,37 @@
 def _half_tanh(q, k):
     return jnp.tanh(_nt(q, k) * (0.5 / math.sqrt(HD)) - 0.5 * SHIFT)
 
-def _fwd_kernel(q_ref, k_ref, v_ref, o_ref, acc_ref):
-    blocks = k_ref.shape[0] // KB
+def _fwd_kernel(q_ref, kv_ref, o_ref, acc_ref):
+    blocks = kv_ref.shape[0] // KB
     acc_ref[...] = jnp.zeros_like(acc_ref)
     def step(j, carry):
         rows = pl.ds(pl.multiple_of(j * KB, KB), KB)
         for h in range(HEADS):
             cols = slice(h * HD, (h + 1) * HD)
-            t = _half_tanh(q_ref[:, cols], k_ref[rows, cols])
+            t = _half_tanh(q_ref[:, cols], kv_ref[rows, pl.ds(H + h * HD, HD)])
             w = (0.5 * t + 0.5).astype(jnp.bfloat16)
-            acc_ref[:, cols] += _nn(w, v_ref[rows, cols])
+            acc_ref[:, cols] += _nn(w, kv_ref[rows, pl.ds(2 * H + h * HD, HD)])
         return carry
     lax.fori_loop(0, blocks, step, 0)
     o_ref[...] = acc_ref[...].astype(o_ref.dtype)
 
-def _gq_kernel(q_ref, g_ref, k_ref, v_ref, o_ref, acc_ref):
-    blocks = k_ref.shape[0] // KB
+def _gq_kernel(q_ref, g_ref, kv_ref, o_ref, acc_ref):
+    blocks = kv_ref.shape[0] // KB
     acc_ref[...] = jnp.zeros_like(acc_ref)
     def step(j, carry):
         rows = pl.ds(pl.multiple_of(j * KB, KB), KB)
         for h in range(HEADS):
             cols = slice(h * HD, (h + 1) * HD)
-            k = k_ref[rows, cols]
+            k = kv_ref[rows, pl.ds(H + h * HD, HD)]
             t = _half_tanh(q_ref[:, cols], k)
-            dp = _nt(g_ref[:, cols], v_ref[rows, cols])
+            dp = _nt(g_ref[:, cols], kv_ref[rows, pl.ds(2 * H + h * HD, HD)])
             ds = (dp * (1.0 - t * t) * (0.25 / math.sqrt(HD))).astype(jnp.bfloat16)
             acc_ref[:, cols] += _nn(ds, k)
         return carry
     lax.fori_loop(0, blocks, step, 0)
     o_ref[...] = acc_ref[...].astype(o_ref.dtype)
 
-def _gkv_kernel(q_ref, g_ref, k_ref, v_ref, dk_ref, dv_ref, acck_ref, accv_ref):
+def _gkv_kernel(q_ref, g_ref, kv_ref, dk_ref, dv_ref, acck_ref, accv_ref):
     blocks = q_ref.shape[0] // KB
     acck_ref[...] = jnp.zeros_like(acck_ref)
     accv_ref[...] = jnp.zeros_like(accv_ref)
@@ -68,9 +68,9 @@
             cols = slice(h * HD, (h + 1) * HD)
             q = q_ref[rows, cols]
             g = g_ref[rows, cols]
-            t = _half_tanh(k_ref[:, cols], q)
+            t = _half_tanh(kv_ref[:, pl.ds(H + h * HD, HD)], q)
             w = (0.5 * t + 0.5).astype(jnp.bfloat16)
-            dp = _nt(v_ref[:, cols], g)
+            dp = _nt(kv_ref[:, pl.ds(2 * H + h * HD, HD)], g)
             ds = (dp * (1.0 - t * t) * (0.25 / math.sqrt(HD))).astype(jnp.bfloat16)
             acck_ref[:, cols] += _nn(ds, q)
             accv_ref[:, cols] += _nn(w, g)
@@ -79,18 +79,21 @@
     dk_ref[...] = acck_ref[...].astype(dk_ref.dtype)
     dv_ref[...] = accv_ref[...].astype(dv_ref.dtype)
 
-def attend_fwd(q, k_all, v_all):
-    return pl.pallas_call(_fwd_kernel, out_shape=jax.ShapeDtypeStruct(q.shape, jnp.bfloat16),
-        scratch_shapes=[pltpu.VMEM(q.shape, jnp.float32)])(q, k_all, v_all)
-
-def attend_gq(q, g, k_all, v_all):
-    return pl.pallas_call(_gq_kernel, out_shape=jax.ShapeDtypeStruct(q.shape, jnp.bfloat16),
-        scratch_shapes=[pltpu.VMEM(q.shape, jnp.float32)])(q, g, k_all, v_all)
-
-def attend_gkv(q_all, g_all, k, v):
-    sh = jax.ShapeDtypeStruct(k.shape, jnp.bfloat16)
+def attend_fwd(qkv_own, qkv_all):
+    shape = (qkv_own.shape[0], H)
+    return pl.pallas_call(_fwd_kernel, out_shape=jax.ShapeDtypeStruct(shape, jnp.bfloat16),
+        scratch_shapes=[pltpu.VMEM(shape, jnp.float32)])(qkv_own, qkv_all)
+
+def attend_gq(qkv_own, g, qkv_all):
+    shape = (qkv_own.shape[0], H)
+    return pl.pallas_call(_gq_kernel, out_shape=jax.ShapeDtypeStruct(shape, jnp.bfloat16),
+        scratch_shapes=[pltpu.VMEM(shape, jnp.float32)])(qkv_own, g, qkv_all)
+
+def attend_gkv(qkv_all, g_all, qkv_own):
+    shape = (qkv_own.shape[0], H)
+    sh = jax.ShapeDtypeStruct(shape, jnp.bfloat16)
     return pl.pallas_call(_gkv_kernel, out_shape=(sh, sh),
-        scratch_shapes=[pltpu.VMEM(k.shape, jnp.float32), pltpu.VMEM(k.shape, jnp.float32)],)(q_all, g_all, k, v)
+        scratch_shapes=[pltpu.VMEM(shape, jnp.float32), pltpu.VMEM(shape, jnp.float32)])(qkv_all, g_all, qkv_own)
 
 
 def from_neighbour(array, axis, step):
@@ -199,15 +202,9 @@
     tokens_all = gather_tiles(tokens, "col").reshape(-1, H)
     w_qkv = jnp.concatenate([w_query, w_key, w_value], axis=1)
     qkv_all = project(tokens_all, w_qkv)
-    query_all = qkv_all[:, :H]
-    key_all = qkv_all[:, H:2 * H]
-    value_all = qkv_all[:, 2 * H:]
     qkv_own = project(tokens, w_qkv)
-    query_own = qkv_own[:, :H]
-    key_own = qkv_own[:, H:2 * H]
-    value_own = qkv_own[:, 2 * H:]
-
-    attended = attend_fwd(query_own, key_all, value_all)
+
+    attended = attend_fwd(qkv_own, qkv_all)
     proj = jnp.dot(attended, w_out, preferred_element_type=jnp.float32)
     pnormed, pscale = rms_forward(proj)
     mixed = tokens.astype(jnp.float32) + pnormed
@@ -223,15 +220,12 @@
 
     grad_attn_all = gather_tiles(grad_attn, "col").reshape(-1, H)
 
-    grad_query = attend_gq(query_own, grad_attn, key_all, value_all)
-    grad_key, grad_val = attend_gkv(query_all, grad_attn_all, key_own, value_own)
-
-    g_query = jnp.einsum("nh,ne->he", tokens, grad_query, preferred_element_type=jnp.float32)
-    g_key = jnp.einsum("nh,ne->he", tokens, grad_key, preferred_element_type=jnp.float32)
-    g_value = jnp.einsum("nh,ne->he", tokens, grad_val, preferred_element_type=jnp.float32)
-    grad_tokens = grad_mixed + jnp.dot(grad_query, w_query.T, preferred_element_type=jnp.float32)
-    grad_tokens = grad_tokens + jnp.dot(grad_key, w_key.T, preferred_element_type=jnp.float32)
-    grad_tokens = grad_tokens + jnp.dot(grad_val, w_value.T, preferred_element_type=jnp.float32)
+    grad_query = attend_gq(qkv_own, grad_attn, qkv_all)
+    grad_key, grad_val = attend_gkv(qkv_all, grad_attn_all, qkv_own)
+
+    grad_qkv = jnp.concatenate([grad_query, grad_key, grad_val], axis=1)
+    g_qkv = jnp.einsum("nh,ne->he", tokens, grad_qkv, preferred_element_type=jnp.float32)
+    grad_tokens = grad_mixed + jnp.dot(grad_qkv, w_qkv.T, preferred_element_type=jnp.float32)
     grad_pooled = rms_backward(token_live * grad_tokens, normed, rscale)
     grad_scaled = (grad_pooled / (member_count + 1.0)).astype(jnp.bfloat16)
     grad_hidden = jnp.einsum(
@@ -241,14 +235,17 @@
     g_msg = jnp.einsum("gh,ge->he", message, grad_pre, preferred_element_type=jnp.float32)
 
     devices = lax.axis_size("row") * lax.axis_size("col")
-    used = 5 * H + 1
-    per_device = -(-used * H // (devices * 128))
-    grads = [g_msg, g_query, g_key, g_value, g_out, g_score[None]]
-    grads.append(jnp.zeros((per_device * devices * 128 // H - used, H), jnp.float32))
-    buffer = jnp.concatenate(grads, axis=0).reshape(devices, per_device, 128)
-    summed = all_reduce_a2a(buffer, ("row", "col")).reshape(-1, H)
-    outs = [summed[i * H:(i + 1) * H] for i in range(5)]
-    g_score_sum = summed[5 * H]
+    pieces = [g_msg.reshape(-1), g_qkv.reshape(-1), g_out.reshape(-1), g_score]
+    used = sum(p.shape[0] for p in pieces)
+    per_device = -(-used // (devices * 128))
+    pieces.append(jnp.zeros((per_device * devices * 128 - used,), jnp.float32))
+    buffer = jnp.concatenate(pieces).reshape(devices, per_device, 128)
+    summed = all_reduce_a2a(buffer, ("row", "col")).reshape(-1)
+    sq = H * H
+    g_qkv_sum = summed[sq:4 * sq].reshape(H, 3 * H)
+    outs = [summed[:sq].reshape(H, H)] + [g_qkv_sum[:, i * H:(i + 1) * H] for i in range(3)]
+    outs.append(summed[4 * sq:5 * sq].reshape(H, H))
+    g_score_sum = summed[5 * sq:5 * sq + H]
     return (value_out[None, None], *outs, g_score_sum)
 
 

time: 214 us -> 222 us (1.037)
  waiting for transfers between devices: 57.3 us -> 70.1 us
  starting transfers between devices: 37.1 us -> 29.2 us
  matrix products: 27.7 us -> 23.1 us
  local copies, waits for them, and re-layouts: 17.1 us -> 21.2 us
  Pallas kernels: 34.6 us -> 37.5 us
    ppermute x4, waiting for transfers between devices: 7.04 us -> 17.1 us  [from_neighbour(): return lax.ppermute(array, axis, pairs)]
    all_to_all x2, starting transfers between devices: 19.7 us -> 11.4 us  [gather_tiles(): return lax.all_to_all(copies, axis, 0, 0, tiled=True)]
    dot_general x6 -> x2, matrix products: 10.5 us -> 4.17 us  [the longest x1 2.91 us: body(): jnp.dot(grad_qkv, w_qkv.T, preferred_element_type=jnp.float32)]
    unnamed x54 -> x78, local copies, waits for them, and re-layouts: 4.15 us -> 9.15 us
    dot_general x2, matrix products: 2.21 us -> 5.74 us  [project(): jnp.dot(rows_in, weight_mat, preferred_element_type=jnp.float32)]
    all_to_all x2, waiting for transfers between devices: 35.2 us -> 38 us  [gather_tiles(): return lax.all_to_all(copies, axis, 0, 0, tiled=True)]
    slice x4 -> x5, local copies, waits for them, and re-layouts: 5.27 us -> 2.63 us  [the longest x1 0.89 us: body(): g_qkv_sum[:, i * H:(i + 1) * H]]
    reshape x2 -> x4, local copies, waits for them, and re-layouts: 0.47 us -> 2.91 us  [the longest x1 1.38 us: body(): buffer = jnp.concatenate(pieces).reshape(devices, per_device, 128)]
  transfers between devices with their start and end apart: 7 -> 7, of which waited for: 4 -> 4; matrix products, arithmetic and copies ran while one was open for 10% -> 6% of each run, Pallas kernels for 5% -> 6%
where the time goes in v5:
time: 222 us; the launch traced here: 221 us
  waiting for transfers between devices  70.1 us (32%)
  Pallas kernels  37.5 us (17%)
  starting transfers between devices  29.2 us (13%)
  blocking collectives  28.7 us (13%)
  matrix products  23.1 us (10%)
  local copies, waits for them, and re-layouts  21.2 us (10%)
  other arithmetic  8.34 us (4%)
  between operations  2.46 us (1%)
    all_to_all x2, waiting for transfers between devices, gather_tiles(): return lax.all_to_all(copies, axis, 0, 0, tiled=True)  38 us
    all_to_all x1, blocking collectives, all_reduce_a2a(): chunks = lax.all_to_all(rows_in, axes, 0, 0, tiled=True)  28.7 us
    ppermute x4, waiting for transfers between devices, from_neighbour(): return lax.ppermute(array, axis, pairs)  17.1 us
    pallas_call x1, Pallas kernels, attend_gkv(): pl.pallas_call(_gkv_kernel, out_shape=(sh, sh), scratch_shapes=[pltpu.VME...  15.5 us
    all_to_all x1, waiting for transfers between devices, all_reduce_a2a(): return lax.all_to_all(copies, axes, 0, 0, tiled=True).astype(jnp.float32)  15 us
    ppermute x4, starting transfers between devices, from_neighbour(): return lax.ppermute(array, axis, pairs)  12.4 us
    pallas_call x1, Pallas kernels, attend_gq(): pl.pallas_call(_gq_kernel, out_shape=jax.ShapeDtypeStruct(shape, jnp.bflo...  12.3 us
    all_to_all x2, starting transfers between devices, gather_tiles(): return lax.all_to_all(copies, axis, 0, 0, tiled=True)  11.4 us
  transfers between devices with their start and end apart: 7, of which 4 were waited for; matrix products, arithmetic and copies ran while one was open for 6% of the time, Pallas kernels for 6%

profile of v5, /device:TPU:0, one launch (start us, length us, event | category | flops | bytes accessed | tf_op | source)
XLA Modules:
  0.0 220.6 jit_solution(15173149020883204639)
XLA Ops:
  1.4 2.2 fusion.14
  3.6 6.0 %collective-permute-start.2 = (bf16[1024,256]{1,0:T(8,128)(2,1)}, bf16[1024,256]{1,0:T(8,128)(2,1)}, u32[]{:S(2)}, u32[]{:S(2)}) collective-permute-start(bf16[1024,256]{1,0:T(8,128)(2,1)} %fusion.14), channel_id=1, source_target_pairs={{0,1},{1,2},{2,3},{3,4},{4,5},{5,6},{6,7},{8,9},{9,10},{10,11},{11... | collective-permute-start | bytes 1572872 | tf_op jit(solution)/shard_map/ppermute | solution.py:102
  9.5 1.3 collective-permute-start.1
  10.8 3.8 %collective-permute-start = (bf16[1024,256]{1,0:T(8,128)(2,1)}, bf16[1024,256]{1,0:T(8,128)(2,1)}, u32[]{:S(2)}, u32[]{:S(2)}) collective-permute-start(bf16[1024,256]{1,0:T(8,128)(2,1)} %fusion.14), channel_id=1, source_target_pairs={{0,8},{8,16},{16,24},{24,32},{32,40},{40,48},{48,56},{56,64},{64,7... | collective-permute-start | bytes 1572872 | tf_op jit(solution)/shard_map/ppermute | solution.py:102
  16.6 1.8 reduce_sum.84
  18.4 1.3 fusion.5
  20.8 1.3 fusion.22
  22.1 17.1 %collective-permute-done.3 = bf16[1024,256]{1,0:T(8,128)(2,1)} collective-permute-done((bf16[1024,256]{1,0:T(8,128)(2,1)}, bf16[1024,256]{1,0:T(8,128)(2,1)}, u32[]{:S(2)}, u32[]{:S(2)}) %collective-permute-start.3) | collective-permute-done | bytes 524320 | tf_op jit(solution)/shard_map/ppermute | solution.py:102
  39.2 1.3 fusion.40
  40.6 1.3 fusion.41
  41.9 1.3 convolution_add_fusion.1
  43.3 1.6 fusion.6
  46.5 1.5 broadcast_in_dim.8
  47.9 7.6 %all-to-all-start = ((bf16[8,512,256]{2,1,0:T(8,128)(2,1)}), bf16[8,512,256]{2,1,0:T(8,128)(2,1)S(1)}, u32[]{:S(2)}, u32[]{:S(2)}) async-start(bf16[8,512,256]{2,1,0:T(8,128)(2,1)} %broadcast_in_dim.8), calls=%async_computation | async-start | bytes 4194304 | tf_op jit(solution)/shard_map/all_to_all | solution.py:108
  58.0 1.3 convolution_convert_fusion.1.q_ref.kv_ref
  59.3 23.9 %all-to-all-done = bf16[8,512,256]{2,1,0:T(8,128)(2,1)S(1)} async-done(((bf16[8,512,256]{2,1,0:T(8,128)(2,1)}), bf16[8,512,256]{2,1,0:T(8,128)(2,1)S(1)}, u32[]{:S(2)}, u32[]{:S(2)}) %all-to-all-start) | async-done | bytes 2097184 | tf_op jit(solution)/shard_map/all_to_all | solution.py:108
  83.2 4.5 %convolution_convert_fusion.kv_ref.q_ref = bf16[4096,768]{1,0:T(8,128)(2,1)} fusion(bf16[4096,256]{1,0:T(8,128)(2,1)S(1)} %bitcast.107, bf16[256,768]{1,0:T(8,128)(2,1)S(1)} %constant_dynamic-update-slice_fusion), kind=kOutput, calls=%fused_computation | convolution fusion | flops 1613758464 | bytes 8781824 | tf_op jit(solution)/shard_map/dot_general | solution.py:152
  87.6 9.7 %shard_map.171 = bf16[512,256]{1,0:T(8,128)(2,1)} custom-call(bf16[512,768]{1,0:T(8,128)(2,1)} %convolution_convert_fusion.1.q_ref.kv_ref, bf16[4096,768]{1,0:T(8,128)(2,1)} %convolution_convert_fusion.kv_ref.q_ref), custom_call_target="tpu_custom_call" | custom-call | tf_op jit(solution)/shard_map/pallas_call | solution.py:84
  99.8 1.5 broadcast_in_dim.9
  101.4 3.8 %all-to-all-start.1 = ((bf16[8,512,256]{2,1,0:T(8,128)(2,1)}), bf16[8,512,256]{2,1,0:T(8,128)(2,1)S(1)}, u32[]{:S(2)}, u32[]{:S(2)}) async-start(bf16[8,512,256]{2,1,0:T(8,128)(2,1)} %broadcast_in_dim.9), calls=%async_computation.1 | async-start | bytes 4194304 | tf_op jit(solution)/shard_map/all_to_all | solution.py:108
  105.2 12.3 %shard_map.172 = bf16[512,256]{1,0:T(8,128)(2,1)} custom-call(bf16[512,768]{1,0:T(8,128)(2,1)} %convolution_convert_fusion.1.q_ref.kv_ref, bf16[512,256]{1,0:T(8,128)(2,1)} %copy-done.14, bf16[4096,768]{1,0:T(8,128)(2,1)} %convolution_convert_fusion.kv_ref.q_ref), custom_call_target="tpu_custom_call" | custom-call | tf_op jit(solution)/shard_map/pallas_call | solution.py:89
  118.7 14.1 %all-to-all-done.1 = bf16[8,512,256]{2,1,0:T(8,128)(2,1)S(1)} async-done(((bf16[8,512,256]{2,1,0:T(8,128)(2,1)}), bf16[8,512,256]{2,1,0:T(8,128)(2,1)S(1)}, u32[]{:S(2)}, u32[]{:S(2)}) %all-to-all-start.1) | async-done | bytes 2097184 | tf_op jit(solution)/shard_map/all_to_all | solution.py:108
  132.7 1.4 copy-done.2
  134.1 15.5 %shard_map.173 = (bf16[512,256]{1,0:T(8,128)(2,1)}, bf16[512,256]{1,0:T(8,128)(2,1)}) custom-call(bf16[4096,768]{1,0:T(8,128)(2,1)} %convolution_convert_fusion.kv_ref.q_ref, bf16[4096,256]{1,0:T(8,128)(2,1)} %bitcast.108, bf16[512,768]{1,0:T(8,128)(2,1)} %convolution_convert_fusion.1.q_ref.kv_ref), custom_call_target="tpu_custom_call" | custom-call | tf_op jit(solution)/shard_map/pallas_call | solution.py:95
  149.7 2.9 %fusion.24 = (f32[512]{0:T(512)}, f32[512,256]{0,1:T(8,128)}) fusion(f32[256,512]{1,0:T(8,128)S(1)} %copy-done.11, f32[512]{0:T(512)S(1)} %add_rsqrt_fusion.1, bf16[256,768]{1,0:T(8,128)(2,1)S(1)} %copy-done.6, bf16[512,256]{1,0:T(8,128)(2,1)} %get-tuple-element.10, bf16[512,256]{1,0:T(8,128)(2,1)} %get-tuple-element.9, bf16[512,256]{1,0:T(8,128)(2,1)} %shard_map.172, ...), kind=kOutput, calls=%fused_computation.43 | convolution fusion | flops 204471808 | bytes 2237440 | tf_op jit(solution)/shard_map/dot_general | solution.py:228
  155.7 3.2 %fusion.10 = f32[32,2,8,128]{3,2,1,0:T(8,128)} fusion(bf16[1024,256]{1,0:T(8,128)(2,1)} %bitcast.113, f32[1024,256]{1,0:T(8,128)} %copy-done.13, f32[1024]{0:T(1024)S(1)} %copy-done.20, s32[1,1,512,1024]{3,2,1,0:T(8,128)S(1)} %copy-done.9, f32[512,256]{0,1:T(8,128)} %get-tuple-element.24, f32[256,512]{1,0:T(8,128)S(1)} %copy-done.11, ...), kind=kOutput, calls=%fused_computation.20 | convolution fusion | flops 406585344 | bytes 4990976 | tf_op jit(solution)/shard_map/gh,ge->he/dot_general | solution.py:235
  162.5 1.3 constant_dynamic-update-slice_fusion.4
  163.8 1.5 broadcast_dynamic-update-slice_fusion
  165.3 1.4 reshape.160
  166.6 28.7 %all_to_all.20 = f32[128,21,128]{2,1,0:T(8,128)S(1)} all-to-all(f32[128,21,128]{2,1,0:T(8,128)S(1)} %reshape.160), channel_id=1, replica_groups=mesh['row'=16,'col'=8] {'row','col'}, dimensions={0} | all-to-all | bytes 2752512 | tf_op jit(solution)/shard_map/all_to_all | solution.py:117
  196.6 5.4 %all-to-all-start.3 = ((bf16[128,21,128]{2,1,0:T(8,128)(2,1)}), bf16[128,21,128]{2,1,0:T(8,128)(2,1)S(1)}, u32[]{:S(2)}, u32[]{:S(2)}) async-start(bf16[128,21,128]{2,1,0:T(8,128)(2,1)} %broadcast_in_dim.11), calls=%async_computation.3 | async-start | bytes 1572864 | tf_op jit(solution)/shard_map/all_to_all | solution.py:120
  202.6 15.0 %all-to-all-done.3 = bf16[128,21,128]{2,1,0:T(8,128)(2,1)S(1)} async-done(((bf16[128,21,128]{2,1,0:T(8,128)(2,1)}), bf16[128,21,128]{2,1,0:T(8,128)(2,1)S(1)}, u32[]{:S(2)}, u32[]{:S(2)}) %all-to-all-start.3) | async-done | bytes 688160 | tf_op jit(solution)/shard_map/all_to_all | solution.py:120
  (112 shorter events, 21.3 us)
Async XLA Ops:
  0.6 96.7 %copy-start = (bf16[256,256]{1,0:T(8,128)(2,1)S(1)}, bf16[256,256]{1,0:T(8,128)(2,1)}, u32[]{:S(2)}) copy-start(bf16[256,256]{1,0:T(8,128)(2,1)} %param.21) | copy-start | bytes 393220
  1.3 43.8 %copy-start.19 = (f32[1024]{0:T(1024)}, f32[1024]{0:T(1024)S(1)}, u32[]{:S(2)}) copy-start(f32[1024]{0:T(1024)S(1)} %fusion.51) | copy-start | bytes 12292
  1.4 17.1 %copy-start.1 = (s32[1,1,8,5,128,128]{5,4,3,2,1,0:T(8,128)S(1)}, s32[1,1,8,5,128,128]{5,4,3,2,1,0:T(8,128)}, u32[]{:S(2)}) copy-start(s32[1,1,8,5,128,128]{5,4,3,2,1,0:T(8,128)} %param.13) | copy-start | bytes 7864324
  3.6 37.0 %collective-permute-start.2 = (bf16[1024,256]{1,0:T(8,128)(2,1)}, bf16[1024,256]{1,0:T(8,128)(2,1)}, u32[]{:S(2)}, u32[]{:S(2)}) collective-permute-start(bf16[1024,256]{1,0:T(8,128)(2,1)} %fusion.14), channel_id=1, source_target_pairs={{0,1},{1,2},{2,3},{3,4},{4,5},{5,6},{6,7},{8,9},{9,10},{10,11},{11... | collective-permute-start | bytes 1572872 | tf_op jit(solution)/shard_map/ppermute | solution.py:102
  9.5 33.7 %collective-permute-start.1 = (bf16[1024,256]{1,0:T(8,128)(2,1)}, bf16[1024,256]{1,0:T(8,128)(2,1)}, u32[]{:S(2)}, u32[]{:S(2)}) collective-permute-start(bf16[1024,256]{1,0:T(8,128)(2,1)} %fusion.14), channel_id=1, source_target_pairs={{8,0},{16,8},{24,16},{32,24},{40,32},{48,40},{56,48},{64,56},{72,6... | collective-permute-start | bytes 1572872 | tf_op jit(solution)/shard_map/ppermute | solution.py:102
  10.8 31.1 %collective-permute-start = (bf16[1024,256]{1,0:T(8,128)(2,1)}, bf16[1024,256]{1,0:T(8,128)(2,1)}, u32[]{:S(2)}, u32[]{:S(2)}) collective-permute-start(bf16[1024,256]{1,0:T(8,128)(2,1)} %fusion.14), channel_id=1, source_target_pairs={{0,8},{8,16},{16,24},{24,32},{32,40},{40,48},{48,56},{56,64},{64,7... | collective-permute-start | bytes 1572872 | tf_op jit(solution)/shard_map/ppermute | solution.py:102
  14.7 24.5 %collective-permute-start.3 = (bf16[1024,256]{1,0:T(8,128)(2,1)}, bf16[1024,256]{1,0:T(8,128)(2,1)}, u32[]{:S(2)}, u32[]{:S(2)}) collective-permute-start(bf16[1024,256]{1,0:T(8,128)(2,1)} %fusion.14), channel_id=1, source_target_pairs={{1,0},{2,1},{3,2},{4,3},{5,4},{6,5},{7,6},{9,8},{10,9},{11,10},{12... | collective-permute-start | bytes 1572872 | tf_op jit(solution)/shard_map/ppermute | solution.py:102
  18.4 26.8 %copy-start.29 = (f32[512]{0:T(512)}, f32[512]{0:T(512)S(1)}, u32[]{:S(2)}) copy-start(f32[512]{0:T(512)S(1)} %convert_add_fusion.2) | copy-start | bytes 6148
  20.0 19.2 %copy-start.3 = (bf16[8,5,128,128]{3,2,0,1:T(8,128)(2,1)S(1)}, bf16[8,5,128,128]{3,2,0,1:T(8,128)(2,1)}, u32[]{:S(2)}) copy-start(bf16[8,5,128,128]{3,2,0,1:T(8,128)(2,1)} %fusion.5) | copy-start | bytes 3932164
  46.3 52.4 %copy-start.10 = (f32[256,512]{1,0:T(8,128)}, f32[256,512]{1,0:T(8,128)S(1)}, u32[]{:S(2)}) copy-start(f32[256,512]{1,0:T(8,128)S(1)} %get-tuple-element.20) | copy-start | bytes 1572868
  47.9 7.6 %copy-start.34 = (bf16[256]{0:T(256)(128)(2,1)S(1)}, bf16[256]{0:T(256)(128)(2,1)}, u32[]{:S(2)}) copy-start(bf16[256]{0:T(256)(128)(2,1)} %param.22) | copy-start | bytes 1540
  47.9 8.2 %copy-start.17 = (bf16[256,256]{1,0:T(8,128)(2,1)S(1)}, bf16[256,256]{1,0:T(8,128)(2,1)}, u32[]{:S(2)}) copy-start(bf16[256,256]{1,0:T(8,128)(2,1)} %param.18) | copy-start | bytes 393220
  47.9 35.2 %all-to-all-start = ((bf16[8,512,256]{2,1,0:T(8,128)(2,1)}), bf16[8,512,256]{2,1,0:T(8,128)(2,1)S(1)}, u32[]{:S(2)}, u32[]{:S(2)}) async-start(bf16[8,512,256]{2,1,0:T(8,128)(2,1)} %broadcast_in_dim.8), calls=%async_computation | async-start | bytes 4194304 | tf_op jit(solution)/shard_map/all_to_all | solution.py:108
  58.0 29.6 %copy-start.5 = (bf16[256,768]{1,0:T(8,128)(2,1)}, bf16[256,768]{1,0:T(8,128)(2,1)S(1)}, u32[]{:S(2)}) copy-start(bf16[256,768]{1,0:T(8,128)(2,1)S(1)} %constant_dynamic-update-slice_fusion) | copy-start | bytes 1179652
  87.6 11.0 %copy-start.28 = (f32[1,1,512]{2,1,0:T(1,128)S(1)}, f32[1,1,512]{2,1,0:T(1,128)}, u32[]{:S(2)}) copy-start(f32[1,1,512]{2,1,0:T(1,128)} %param.23) | copy-start | bytes 6148
  87.6 11.0 %copy-start.24 = (f32[256]{0:T(256)S(1)}, f32[256]{0:T(256)}, u32[]{:S(2)}) copy-start(f32[256]{0:T(256)} %convert_element_type.147) | copy-start | bytes 3076
  101.4 31.4 %all-to-all-start.1 = ((bf16[8,512,256]{2,1,0:T(8,128)(2,1)}), bf16[8,512,256]{2,1,0:T(8,128)(2,1)S(1)}, u32[]{:S(2)}, u32[]{:S(2)}) async-start(bf16[8,512,256]{2,1,0:T(8,128)(2,1)} %broadcast_in_dim.9), calls=%async_computation.1 | async-start | bytes 4194304 | tf_op jit(solution)/shard_map/all_to_all | solution.py:108
  105.2 12.3 %copy-start.4 = (bf16[512,256]{1,0:T(8,128)(2,1)S(1)}, bf16[512,256]{1,0:T(8,128)(2,1)}, u32[]{:S(2)}) copy-start(bf16[512,256]{1,0:T(8,128)(2,1)} %shard_map.171) | copy-start | bytes 786436
  105.2 12.3 %copy-start.23 = (f32[512]{0:T(512)S(1)}, f32[512]{0:T(512)}, u32[]{:S(2)}) copy-start(f32[512]{0:T(512)} %copy-done.22) | copy-start | bytes 6148
  105.2 12.3 %copy-start.25 = (f32[256]{0:T(256)S(1)}, f32[256]{0:T(256)}, u32[]{:S(2)}) copy-start(f32[256]{0:T(256)} %convert_element_type.147) | copy-start | bytes 3076
  134.1 15.5 %copy-start.6 = (bf16[256,768]{1,0:T(8,128)(2,1)S(1)}, bf16[256,768]{1,0:T(8,128)(2,1)}, u32[]{:S(2)}) copy-start(bf16[256,768]{1,0:T(8,128)(2,1)} %copy-done.5) | copy-start | bytes 1179652
  134.1 15.5 %copy-start.11 = (f32[256,512]{1,0:T(8,128)S(1)}, f32[256,512]{1,0:T(8,128)}, u32[]{:S(2)}) copy-start(f32[256,512]{1,0:T(8,128)} %copy-done.10) | copy-start | bytes 1572868
  134.1 15.5 %copy-start.26 = (f32[256]{0:T(256)S(1)}, f32[256]{0:T(256)}, u32[]{:S(2)}) copy-start(f32[256]{0:T(256)} %convert_element_type.147) | copy-start | bytes 3076
  149.7 3.0 %copy-start.16 = (bf16[512,256]{1,0:T(8,128)(2,1)S(1)}, bf16[512,256]{1,0:T(8,128)(2,1)}, u32[]{:S(2)}) copy-start(bf16[512,256]{1,0:T(8,128)(2,1)} %shard_map.172) | copy-start | bytes 786436
  149.7 2.9 %copy-start.32 = (bf16[512,256]{1,0:T(8,128)(2,1)S(1)}, bf16[512,256]{1,0:T(8,128)(2,1)}, u32[]{:S(2)}) copy-start(bf16[512,256]{1,0:T(8,128)(2,1)} %get-tuple-element.9) | copy-start | bytes 786436
  149.7 2.9 %copy-start.33 = (bf16[512,256]{1,0:T(8,128)(2,1)S(1)}, bf16[512,256]{1,0:T(8,128)(2,1)}, u32[]{:S(2)}) copy-start(bf16[512,256]{1,0:T(8,128)(2,1)} %get-tuple-element.10) | copy-start | bytes 786436
  152.6 3.1 %copy-start.9 = (s32[1,1,512,1024]{3,2,1,0:T(8,128)S(1)}, s32[1,1,512,1024]{3,2,1,0:T(8,128)}, u32[]{:S(2)}) copy-start(s32[1,1,512,1024]{3,2,1,0:T(8,128)} %param.15) | copy-start | bytes 6291460
  152.6 3.1 %copy-start.20 = (f32[1024]{0:T(1024)S(1)}, f32[1024]{0:T(1024)}, u32[]{:S(2)}) copy-start(f32[1024]{0:T(1024)} %copy-done.19) | copy-start | bytes 12292
  152.7 3.1 %copy-start.30 = (f32[512]{0:T(512)S(1)}, f32[512]{0:T(512)}, u32[]{:S(2)}) copy-start(f32[512]{0:T(512)} %copy-done.29) | copy-start | bytes 6148
  158.9 3.5 %copy-start.27 = (f32[256]{0:T(256)S(1)}, f32[256]{0:T(256)}, u32[]{:S(2)}) copy-start(f32[256]{0:T(256)} %get-tuple-element.11) | copy-start | bytes 3076
  195.6 6.4 %copy-start.21 = (f32[512]{0:T(512)S(1)}, f32[512]{0:T(512)}, u32[]{:S(2)}) copy-start(f32[512]{0:T(512)} %get-tuple-element.12) | copy-start | bytes 6148
  196.6 21.1 %all-to-all-start.3 = ((bf16[128,21,128]{2,1,0:T(8,128)(2,1)}), bf16[128,21,128]{2,1,0:T(8,128)(2,1)S(1)}, u32[]{:S(2)}, u32[]{:S(2)}) async-start(bf16[128,21,128]{2,1,0:T(8,128)(2,1)} %broadcast_in_dim.11), calls=%async_computation.3 | async-start | bytes 1572864 | tf_op jit(solution)/shard_map/all_to_all | solution.py:120
  (10 other events, 17.0 us)

commit v6 on v4

--- a/solution.py
+++ b/solution.py
@@ -103,6 +103,16 @@
     size = lax.axis_size(axis)
     copies = jnp.broadcast_to(rows_in[None], (size,) + rows_in.shape)
     return lax.all_to_all(copies, axis, 0, 0, tiled=True)
+
+
+def reduce_chunks(rows_in, axes):
+    chunks = lax.all_to_all(rows_in, axes, 0, 0, tiled=True)
+    return jnp.sum(chunks, axis=0, keepdims=True)
+
+
+def share_chunks(total, axes, size):
+    copies = jnp.broadcast_to(total.astype(jnp.bfloat16), (size,) + total.shape[1:])
+    return lax.all_to_all(copies, axes, 0, 0, tiled=True).astype(jnp.float32)
 
 
 def all_reduce_a2a(rows_in, axes):
@@ -224,9 +234,14 @@
     grad_attn_all = gather_tiles(grad_attn, "col").reshape(-1, H)
 
     grad_query = attend_gq(query_own, grad_attn, key_all, value_all)
+    g_query = jnp.einsum("nh,ne->he", tokens, grad_query, preferred_element_type=jnp.float32)
+    devices = lax.axis_size("row") * lax.axis_size("col")
+    axes = ("row", "col")
+    early = jnp.concatenate([g_out, g_query], axis=0)
+    early_rows = early.shape[0] * H // (devices * 128)
+    early = reduce_chunks(early.reshape(devices, early_rows, 128), axes)
     grad_key, grad_val = attend_gkv(query_all, grad_attn_all, key_own, value_own)
 
-    g_query = jnp.einsum("nh,ne->he", tokens, grad_query, preferred_element_type=jnp.float32)
     g_key = jnp.einsum("nh,ne->he", tokens, grad_key, preferred_element_type=jnp.float32)
     g_value = jnp.einsum("nh,ne->he", tokens, grad_val, preferred_element_type=jnp.float32)
     grad_tokens = grad_mixed + jnp.dot(grad_query, w_query.T, preferred_element_type=jnp.float32)
@@ -240,15 +255,16 @@
     grad_pre = (gate_live[:, None] * grad_hidden * silu_grad(preact)).astype(jnp.bfloat16)
     g_msg = jnp.einsum("gh,ge->he", message, grad_pre, preferred_element_type=jnp.float32)
 
-    devices = lax.axis_size("row") * lax.axis_size("col")
-    used = 5 * H + 1
-    per_device = -(-used * H // (devices * 128))
-    grads = [g_msg, g_query, g_key, g_value, g_out, g_score[None]]
-    grads.append(jnp.zeros((per_device * devices * 128 // H - used, H), jnp.float32))
-    buffer = jnp.concatenate(grads, axis=0).reshape(devices, per_device, 128)
-    summed = all_reduce_a2a(buffer, ("row", "col")).reshape(-1, H)
-    outs = [summed[i * H:(i + 1) * H] for i in range(5)]
-    g_score_sum = summed[5 * H]
+    used = 3 * H + 1
+    late_rows = -(-used * H // (devices * 128))
+    late = [g_msg, g_key, g_value, g_score[None]]
+    late.append(jnp.zeros((late_rows * devices * 128 // H - used, H), jnp.float32))
+    late = reduce_chunks(jnp.concatenate(late, axis=0).reshape(devices, late_rows, 128), axes)
+    both = share_chunks(jnp.concatenate([early, late], axis=1), axes, devices)
+    early_sum = both[:, :early_rows].reshape(-1, H)
+    late_sum = both[:, early_rows:].reshape(-1, H)
+    outs = [late_sum[:H], early_sum[H:], late_sum[H:2 * H], late_sum[2 * H:3 * H], early_sum[:H]]
+    g_score_sum = late_sum[3 * H]
     return (value_out[None, None], *outs, g_score_sum)
 
 

time: 214 us -> 218 us (1.019)
  blocking collectives: 27.4 us -> 0 us
  waiting for transfers between devices: 57.3 us -> 73.2 us
  starting transfers between devices: 37.1 us -> 52.4 us
  matrix products: 27.7 us -> 24.5 us
    all_to_all x1 -> x0, blocking collectives: 27.4 us -> none  [all_reduce_a2a(): chunks = lax.all_to_all(rows_in, axes, 0, 0, tiled=True)]
    all_to_all x1 -> x3, waiting for transfers between devices: 15 us -> 31.9 us  [the longest x2 16.8 us: reduce_chunks(): chunks = lax.all_to_all(rows_in, axes, 0, 0, tiled=True)]
    all_to_all x1 -> x3, starting transfers between devices: 5.42 us -> 20.8 us  [the longest x2 15.6 us: reduce_chunks(): chunks = lax.all_to_all(rows_in, axes, 0, 0, tiled=True)]
    reshape x2 -> x3, local copies, waits for them, and re-layouts: 0.47 us -> 3.26 us  [the longest x1 1.88 us: body(): early = reduce_chunks(early.reshape(devices, early_rows, 128), axes)]
  transfers between devices with their start and end apart: 7 -> 9, of which waited for: 4 -> 5; matrix products, arithmetic and copies ran while one was open for 10% -> 16% of each run, Pallas kernels for 5% -> 12%
where the time goes in v6:
time: 218 us; the launch traced here: 217 us
  waiting for transfers between devices  73.2 us (34%)
  starting transfers between devices  52.4 us (24%)
  Pallas kernels  34.6 us (16%)
  matrix products  24.5 us (11%)
  local copies, waits for them, and re-layouts  18.2 us (8%)
  other arithmetic  11.4 us (5%)
  between operations  2.51 us (1%)
    all_to_all x2, waiting for transfers between devices, gather_tiles(): return lax.all_to_all(copies, axis, 0, 0, tiled=True)  34.3 us
    all_to_all x2, starting transfers between devices, gather_tiles(): return lax.all_to_all(copies, axis, 0, 0, tiled=True)  19.6 us
    all_to_all x2, waiting for transfers between devices, reduce_chunks(): chunks = lax.all_to_all(rows_in, axes, 0, 0, tiled=True)  16.8 us
    all_to_all x2, starting transfers between devices, reduce_chunks(): chunks = lax.all_to_all(rows_in, axes, 0, 0, tiled=True)  15.6 us
    all_to_all x1, waiting for transfers between devices, share_chunks(): return lax.all_to_all(copies, axes, 0, 0, tiled=True).astype(jnp.float32)  15 us
    pallas_call x1, Pallas kernels, attend_gkv(): pl.pallas_call(_gkv_kernel, out_shape=(sh, sh), scratch_shapes=[pltpu.VME...  14.1 us
    ppermute x4, starting transfers between devices, from_neighbour(): return lax.ppermute(array, axis, pairs)  12 us
    pallas_call x1, Pallas kernels, attend_gq(): pl.pallas_call(_gq_kernel, out_shape=jax.ShapeDtypeStruct(q.shape, jnp.bf...  11.5 us
  transfers between devices with their start and end apart: 9, of which 5 were waited for; matrix products, arithmetic and copies ran while one was open for 16% of the time, Pallas kernels for 12%

profile of v6, /device:TPU:0, one launch (start us, length us, event | category | flops | bytes accessed | tf_op | source)
XLA Modules:
  0.0 216.8 jit_solution(9143529243895226026)
XLA Ops:
  1.4 2.0 fusion.13
  3.4 2.3 %collective-permute-start = (bf16[1024,256]{1,0:T(8,128)(2,1)}, bf16[1024,256]{1,0:T(8,128)(2,1)}, u32[]{:S(2)}, u32[]{:S(2)}) collective-permute-start(bf16[1024,256]{1,0:T(8,128)(2,1)} %fusion.13), channel_id=1, source_target_pairs={{0,8},{8,16},{16,24},{24,32},{32,40},{40,48},{48,56},{56,64},{64,7... | collective-permute-start | bytes 1572872 | tf_op jit(solution)/shard_map/ppermute | solution.py:99
  7.0 7.1 %collective-permute-start.2 = (bf16[1024,256]{1,0:T(8,128)(2,1)}, bf16[1024,256]{1,0:T(8,128)(2,1)}, u32[]{:S(2)}, u32[]{:S(2)}) collective-permute-start(bf16[1024,256]{1,0:T(8,128)(2,1)} %fusion.13), channel_id=1, source_target_pairs={{0,1},{1,2},{2,3},{3,4},{4,5},{5,6},{6,7},{8,9},{9,10},{10,11},{11... | collective-permute-start | bytes 1572872 | tf_op jit(solution)/shard_map/ppermute | solution.py:99
  15.4 3.1 %fusion.5 = bf16[8,5,128,128]{3,2,0,1:T(8,128)(2,1)} fusion(s32[1,1,8,5,128,128]{5,4,3,2,1,0:T(8,128)} %param.13), kind=kLoop, calls=%fused_computation.11 | loop fusion | flops 655360 | bytes 3932160 | tf_op jit(solution)/shard_map/convert.8
  18.5 1.8 reduce_sum.93
  21.2 1.4 fusion.21
  22.7 7.1 %collective-permute-done.3 = bf16[1024,256]{1,0:T(8,128)(2,1)} collective-permute-done((bf16[1024,256]{1,0:T(8,128)(2,1)}, bf16[1024,256]{1,0:T(8,128)(2,1)}, u32[]{:S(2)}, u32[]{:S(2)}) %collective-permute-start.3) | collective-permute-done | bytes 524320 | tf_op jit(solution)/shard_map/ppermute | solution.py:99
  29.7 1.4 fusion.38
  31.1 1.3 fusion.39
  32.5 1.3 convolution_add_fusion.1
  33.8 1.6 fusion.6
  37.0 1.5 broadcast_in_dim.10
  38.5 16.0 %all-to-all-start = ((bf16[8,512,256]{2,1,0:T(8,128)(2,1)}), bf16[8,512,256]{2,1,0:T(8,128)(2,1)S(1)}, u32[]{:S(2)}, u32[]{:S(2)}) async-start(bf16[8,512,256]{2,1,0:T(8,128)(2,1)} %broadcast_in_dim.10), calls=%async_computation | async-start | bytes 4194304 | tf_op jit(solution)/shard_map/all_to_all | solution.py:105
  58.2 25.0 %all-to-all-done = bf16[8,512,256]{2,1,0:T(8,128)(2,1)S(1)} async-done(((bf16[8,512,256]{2,1,0:T(8,128)(2,1)}), bf16[8,512,256]{2,1,0:T(8,128)(2,1)S(1)}, u32[]{:S(2)}, u32[]{:S(2)}) %all-to-all-start) | async-done | bytes 2097184 | tf_op jit(solution)/shard_map/all_to_all | solution.py:105
  83.2 1.8 convolution_convert_fusion
  85.0 2.7 %fusion.57 = (bf16[4096,256]{1,0:T(8,128)(2,1)}, bf16[4096,256]{1,0:T(8,128)(2,1)}, bf16[4096,256]{1,0:T(8,128)(2,1)}) fusion(bf16[4096,768]{1,0:T(8,128)(2,1)S(1)} %convolution_convert_fusion), kind=kLoop, calls=%fused_computation.92 | loop fusion | bytes 12582912 | tf_op jit(solution)/shard_map/slice | solution.py:212
  87.8 9.0 %shard_map.171 = bf16[512,256]{1,0:T(8,128)(2,1)} custom-call(bf16[512,256]{1,0:T(8,128)(2,1)} %get-tuple-element.24.q_ref, bf16[4096,256]{1,0:T(8,128)(2,1)} %get-tuple-element.16.k_ref, bf16[4096,256]{1,0:T(8,128)(2,1)} %get-tuple-element.15.v_ref), custom_call_target="tpu_custom_call" | custom-call | tf_op jit(solution)/shard_map/pallas_call | solution.py:83
  99.9 1.4 broadcast_in_dim.11
  101.4 3.6 %all-to-all-start.2 = ((bf16[8,512,256]{2,1,0:T(8,128)(2,1)}), bf16[8,512,256]{2,1,0:T(8,128)(2,1)S(1)}, u32[]{:S(2)}, u32[]{:S(2)}) async-start(bf16[8,512,256]{2,1,0:T(8,128)(2,1)} %broadcast_in_dim.11), calls=%async_computation.2 | async-start | bytes 4194304 | tf_op jit(solution)/shard_map/all_to_all | solution.py:105
  105.0 11.5 %shard_map.172 = bf16[512,256]{1,0:T(8,128)(2,1)} custom-call(bf16[512,256]{1,0:T(8,128)(2,1)} %get-tuple-element.24.q_ref, bf16[512,256]{1,0:T(8,128)(2,1)} %copy-done.9, bf16[4096,256]{1,0:T(8,128)(2,1)} %get-tuple-element.16.k_ref, bf16[4096,256]{1,0:T(8,128)(2,1)} %get-tuple-element.15.v_ref), custom_call_target="tpu_custom_call" | custom-call | tf_op jit(solution)/shard_map/pallas_call | solution.py:87
  119.9 1.9 reshape.162
  121.7 1.8 convolution_add_fusion.4
  123.5 9.3 %all-to-all-done.2 = bf16[8,512,256]{2,1,0:T(8,128)(2,1)S(1)} async-done(((bf16[8,512,256]{2,1,0:T(8,128)(2,1)}), bf16[8,512,256]{2,1,0:T(8,128)(2,1)S(1)}, u32[]{:S(2)}, u32[]{:S(2)}) %all-to-all-start.2) | async-done | bytes 2097184 | tf_op jit(solution)/shard_map/all_to_all | solution.py:105
  132.8 5.9 %all-to-all-start.1 = ((f32[128,8,128]{2,1,0:T(8,128)}), f32[128,8,128]{2,1,0:T(8,128)}, u32[]{:S(2)}, u32[]{:S(2)}) async-start(f32[128,8,128]{2,1,0:T(8,128)} %reshape.162), calls=%async_computation.1 | async-start | bytes 1048576 | tf_op jit(solution)/shard_map/all_to_all | solution.py:109
  138.7 14.1 %shard_map.173 = (bf16[512,256]{1,0:T(8,128)(2,1)}, bf16[512,256]{1,0:T(8,128)(2,1)}) custom-call(bf16[4096,256]{1,0:T(8,128)(2,1)} %get-tuple-element.14.q_ref, bf16[4096,256]{1,0:T(8,128)(2,1)} %bitcast.112, bf16[512,256]{1,0:T(8,128)(2,1)} %get-tuple-element.23.k_ref, bf16[512,256]{1,0:T(8,128)(2,1)} %get-tuple-element.22.v_ref), custom_call_target="tpu_custom_call" | custom-call | tf_op jit(solution)/shard_map/pallas_call | solution.py:92
  154.1 1.3 fusion.64
  155.4 1.5 convolution_add_fusion.3
  158.1 3.2 %fusion.8 = f32[256,256]{1,0:T(8,128)} fusion(bf16[1024,256]{1,0:T(8,128)(2,1)} %bitcast.115, f32[1024,256]{1,0:T(8,128)} %copy-done.10, f32[1024]{0:T(1024)S(1)} %copy-done.17, s32[1,1,512,1024]{3,2,1,0:T(8,128)S(1)} %copy-done.7, f32[512,256]{0,1:T(8,128)} %get-tuple-element.30, f32[256,512]{1,0:T(8,128)S(1)} %get-tuple-element.26, ...), kind=kOutput, calls=%fused_computation.15 | convolution fusion | flops 406585344 | bytes 4990976 | tf_op jit(solution)/shard_map/gh,ge->he/dot_general | solution.py:256
  163.6 9.7 %all-to-all-start.3 = ((f32[128,13,128]{2,1,0:T(8,128)}), f32[128,13,128]{2,1,0:T(8,128)S(1)}, u32[]{:S(2)}, u32[]{:S(2)}) async-start(f32[128,13,128]{2,1,0:T(8,128)} %reshape.164), calls=%async_computation.3 | async-start | bytes 2097152 | tf_op jit(solution)/shard_map/all_to_all | solution.py:109
  174.5 16.8 %all-to-all-done.3 = f32[128,13,128]{2,1,0:T(8,128)S(1)} async-done(((f32[128,13,128]{2,1,0:T(8,128)}), f32[128,13,128]{2,1,0:T(8,128)S(1)}, u32[]{:S(2)}, u32[]{:S(2)}) %all-to-all-start.3) | async-done | bytes 852000 | tf_op jit(solution)/shard_map/all_to_all | solution.py:109
  192.5 5.2 %all-to-all-start.4 = ((bf16[128,21,128]{2,1,0:T(8,128)(2,1)}), bf16[128,21,128]{2,1,0:T(8,128)(2,1)S(1)}, u32[]{:S(2)}, u32[]{:S(2)}) async-start(bf16[128,21,128]{2,1,0:T(8,128)(2,1)} %broadcast_in_dim.14), calls=%async_computation.4 | async-start | bytes 1572864 | tf_op jit(solution)/shard_map/all_to_all | solution.py:115
  198.3 15.0 %all-to-all-done.4 = bf16[128,21,128]{2,1,0:T(8,128)(2,1)S(1)} async-done(((bf16[128,21,128]{2,1,0:T(8,128)(2,1)}), bf16[128,21,128]{2,1,0:T(8,128)(2,1)S(1)}, u32[]{:S(2)}, u32[]{:S(2)}) %all-to-all-start.4) | async-done | bytes 688160 | tf_op jit(solution)/shard_map/all_to_all | solution.py:115
  (101 shorter events, 25.6 us)
Async XLA Ops:
  0.6 96.1 %copy-start = (bf16[256,256]{1,0:T(8,128)(2,1)S(1)}, bf16[256,256]{1,0:T(8,128)(2,1)}, u32[]{:S(2)}) copy-start(bf16[256,256]{1,0:T(8,128)(2,1)} %param.21) | copy-start | bytes 393220
  1.3 34.4 %copy-start.16 = (f32[1024]{0:T(1024)}, f32[1024]{0:T(1024)S(1)}, u32[]{:S(2)}) copy-start(f32[1024]{0:T(1024)S(1)} %fusion.49) | copy-start | bytes 12292
  3.4 17.6 %copy-start.1 = (s32[1,1,8,5,128,128]{5,4,3,2,1,0:T(8,128)S(1)}, s32[1,1,8,5,128,128]{5,4,3,2,1,0:T(8,128)}, u32[]{:S(2)}) copy-start(s32[1,1,8,5,128,128]{5,4,3,2,1,0:T(8,128)} %param.13) | copy-start | bytes 7864324
  3.4 29.1 %collective-permute-start = (bf16[1024,256]{1,0:T(8,128)(2,1)}, bf16[1024,256]{1,0:T(8,128)(2,1)}, u32[]{:S(2)}, u32[]{:S(2)}) collective-permute-start(bf16[1024,256]{1,0:T(8,128)(2,1)} %fusion.13), channel_id=1, source_target_pairs={{0,8},{8,16},{16,24},{24,32},{32,40},{40,48},{48,56},{56,64},{64,7... | collective-permute-start | bytes 1572872 | tf_op jit(solution)/shard_map/ppermute | solution.py:99
  5.7 24.0 %collective-permute-start.3 = (bf16[1024,256]{1,0:T(8,128)(2,1)}, bf16[1024,256]{1,0:T(8,128)(2,1)}, u32[]{:S(2)}, u32[]{:S(2)}) collective-permute-start(bf16[1024,256]{1,0:T(8,128)(2,1)} %fusion.13), channel_id=1, source_target_pairs={{1,0},{2,1},{3,2},{4,3},{5,4},{6,5},{7,6},{9,8},{10,9},{11,10},{12... | collective-permute-start | bytes 1572872 | tf_op jit(solution)/shard_map/ppermute | solution.py:99
  7.0 24.1 %collective-permute-start.2 = (bf16[1024,256]{1,0:T(8,128)(2,1)}, bf16[1024,256]{1,0:T(8,128)(2,1)}, u32[]{:S(2)}, u32[]{:S(2)}) collective-permute-start(bf16[1024,256]{1,0:T(8,128)(2,1)} %fusion.13), channel_id=1, source_target_pairs={{0,1},{1,2},{2,3},{3,4},{4,5},{5,6},{6,7},{8,9},{9,10},{10,11},{11... | collective-permute-start | bytes 1572872 | tf_op jit(solution)/shard_map/ppermute | solution.py:99
  14.1 19.7 %collective-permute-start.1 = (bf16[1024,256]{1,0:T(8,128)(2,1)}, bf16[1024,256]{1,0:T(8,128)(2,1)}, u32[]{:S(2)}, u32[]{:S(2)}) collective-permute-start(bf16[1024,256]{1,0:T(8,128)(2,1)} %fusion.13), channel_id=1, source_target_pairs={{8,0},{16,8},{24,16},{32,24},{40,32},{48,40},{56,48},{64,56},{72,6... | collective-permute-start | bytes 1572872 | tf_op jit(solution)/shard_map/ppermute | solution.py:99
  18.5 2.8 %copy-start.5 = (bf16[1,1,1024,256]{3,2,1,0:T(8,128)(2,1)S(1)}, bf16[1,1,1024,256]{3,2,1,0:T(8,128)(2,1)}, u32[]{:S(2)}) copy-start(bf16[1,1,1024,256]{3,2,1,0:T(8,128)(2,1)} %param.12) | copy-start | bytes 1572868
  20.3 15.4 %copy-start.23 = (f32[512]{0:T(512)}, f32[512]{0:T(512)S(1)}, u32[]{:S(2)}) copy-start(f32[512]{0:T(512)S(1)} %convert_add_fusion.2) | copy-start | bytes 6148
  21.2 9.9 %copy-start.3 = (bf16[8,5,128,128]{3,2,0,1:T(8,128)(2,1)S(1)}, bf16[8,5,128,128]{3,2,0,1:T(8,128)(2,1)}, u32[]{:S(2)}) copy-start(bf16[8,5,128,128]{3,2,0,1:T(8,128)(2,1)} %fusion.5) | copy-start | bytes 3932164
  33.8 1.6 copy-start.15
  33.8 1.9 copy-start.6
  38.5 16.0 %copy-start.25 = (bf16[256]{0:T(256)(128)(2,1)S(1)}, bf16[256]{0:T(256)(128)(2,1)}, u32[]{:S(2)}) copy-start(bf16[256]{0:T(256)(128)(2,1)} %param.22) | copy-start | bytes 1540
  38.5 18.4 %copy-start.11 = (bf16[256,256]{1,0:T(8,128)(2,1)S(1)}, bf16[256,256]{1,0:T(8,128)(2,1)}, u32[]{:S(2)}) copy-start(bf16[256,256]{1,0:T(8,128)(2,1)} %param.20) | copy-start | bytes 393220
  38.5 44.7 %all-to-all-start = ((bf16[8,512,256]{2,1,0:T(8,128)(2,1)}), bf16[8,512,256]{2,1,0:T(8,128)(2,1)S(1)}, u32[]{:S(2)}, u32[]{:S(2)}) async-start(bf16[8,512,256]{2,1,0:T(8,128)(2,1)} %broadcast_in_dim.10), calls=%async_computation | async-start | bytes 4194304 | tf_op jit(solution)/shard_map/all_to_all | solution.py:105
  87.8 10.2 %copy-start.22 = (f32[1,1,512]{2,1,0:T(1,128)S(1)}, f32[1,1,512]{2,1,0:T(1,128)}, u32[]{:S(2)}) copy-start(f32[1,1,512]{2,1,0:T(1,128)} %param.23) | copy-start | bytes 6148
  87.8 10.2 %copy-start.18 = (f32[256]{0:T(256)S(1)}, f32[256]{0:T(256)}, u32[]{:S(2)}) copy-start(f32[256]{0:T(256)} %convert_element_type.145) | copy-start | bytes 3076
  98.9 2.5 %copy-start.20 = (f32[512]{0:T(512)}, f32[512]{0:T(512)S(1)}, u32[]{:S(2)}) copy-start(f32[512]{0:T(512)S(1)} %broadcast_multiply_fusion.1) | copy-start | bytes 6148
  101.4 31.4 %all-to-all-start.2 = ((bf16[8,512,256]{2,1,0:T(8,128)(2,1)}), bf16[8,512,256]{2,1,0:T(8,128)(2,1)S(1)}, u32[]{:S(2)}, u32[]{:S(2)}) async-start(bf16[8,512,256]{2,1,0:T(8,128)(2,1)} %broadcast_in_dim.11), calls=%async_computation.2 | async-start | bytes 4194304 | tf_op jit(solution)/shard_map/all_to_all | solution.py:105
  119.0 2.7 %copy-start.4 = (bf16[512,256]{1,0:T(8,128)(2,1)S(1)}, bf16[512,256]{1,0:T(8,128)(2,1)}, u32[]{:S(2)}) copy-start(bf16[512,256]{1,0:T(8,128)(2,1)} %shard_map.172) | copy-start | bytes 786436
  119.0 2.7 %copy-start.14 = (bf16[256,256]{1,0:T(8,128)(2,1)S(1)}, bf16[256,256]{1,0:T(8,128)(2,1)}, u32[]{:S(2)}) copy-start(bf16[256,256]{1,0:T(8,128)(2,1)} %param.18) | copy-start | bytes 393220
  132.8 5.9 %copy-start.2 = (bf16[8,512,256]{2,1,0:T(8,128)(2,1)}, bf16[8,512,256]{2,1,0:T(8,128)(2,1)S(1)}, u32[]{:S(2)}) copy-start(bf16[8,512,256]{2,1,0:T(8,128)(2,1)S(1)} %all-to-all-done.2) | copy-start | bytes 6291460
  132.8 30.9 %all-to-all-start.1 = ((f32[128,8,128]{2,1,0:T(8,128)}), f32[128,8,128]{2,1,0:T(8,128)}, u32[]{:S(2)}, u32[]{:S(2)}) async-start(f32[128,8,128]{2,1,0:T(8,128)} %reshape.162), calls=%async_computation.1 | async-start | bytes 1048576 | tf_op jit(solution)/shard_map/all_to_all | solution.py:109
  152.8 4.1 %copy-start.8 = (bf16[512,256]{1,0:T(8,128)(2,1)S(1)}, bf16[512,256]{1,0:T(8,128)(2,1)}, u32[]{:S(2)}) copy-start(bf16[512,256]{1,0:T(8,128)(2,1)} %get-tuple-element.10) | copy-start | bytes 786436
  152.8 4.1 %copy-start.12 = (bf16[256,256]{1,0:T(8,128)(2,1)S(1)}, bf16[256,256]{1,0:T(8,128)(2,1)}, u32[]{:S(2)}) copy-start(bf16[256,256]{1,0:T(8,128)(2,1)} %param.20) | copy-start | bytes 393220
  154.1 4.0 %copy-start.7 = (s32[1,1,512,1024]{3,2,1,0:T(8,128)S(1)}, s32[1,1,512,1024]{3,2,1,0:T(8,128)}, u32[]{:S(2)}) copy-start(s32[1,1,512,1024]{3,2,1,0:T(8,128)} %param.15) | copy-start | bytes 6291460
  154.1 3.9 %copy-start.17 = (f32[1024]{0:T(1024)S(1)}, f32[1024]{0:T(1024)}, u32[]{:S(2)}) copy-start(f32[1024]{0:T(1024)} %copy-done.16) | copy-start | bytes 12292
  154.1 3.9 %copy-start.24 = (f32[512]{0:T(512)S(1)}, f32[512]{0:T(512)}, u32[]{:S(2)}) copy-start(f32[512]{0:T(512)} %copy-done.23) | copy-start | bytes 6148
  158.0 3.2 %copy-start.21 = (f32[256]{0:T(256)S(1)}, f32[256]{0:T(256)}, u32[]{:S(2)}) copy-start(f32[256]{0:T(256)} %get-tuple-element.11) | copy-start | bytes 3076
  163.6 27.7 %all-to-all-start.3 = ((f32[128,13,128]{2,1,0:T(8,128)}), f32[128,13,128]{2,1,0:T(8,128)S(1)}, u32[]{:S(2)}, u32[]{:S(2)}) async-start(f32[128,13,128]{2,1,0:T(8,128)} %reshape.164), calls=%async_computation.3 | async-start | bytes 2097152 | tf_op jit(solution)/shard_map/all_to_all | solution.py:109
  173.3 24.4 %copy-start.19 = (f32[512]{0:T(512)S(1)}, f32[512]{0:T(512)}, u32[]{:S(2)}) copy-start(f32[512]{0:T(512)} %get-tuple-element.12) | copy-start | bytes 6148
  192.5 20.9 %all-to-all-start.4 = ((bf16[128,21,128]{2,1,0:T(8,128)(2,1)}), bf16[128,21,128]{2,1,0:T(8,128)(2,1)S(1)}, u32[]{:S(2)}, u32[]{:S(2)}) async-start(bf16[128,21,128]{2,1,0:T(8,128)(2,1)} %broadcast_in_dim.14), calls=%async_computation.4 | async-start | bytes 1572864 | tf_op jit(solution)/shard_map/all_to_all | solution.py:115
  (3 other events, 3.0 us)

commit v7 on v4

--- a/solution.py
+++ b/solution.py
@@ -42,7 +42,7 @@
     lax.fori_loop(0, blocks, step, 0)
     o_ref[...] = acc_ref[...].astype(o_ref.dtype)
 
-def _gq_kernel(q_ref, g_ref, k_ref, v_ref, o_ref, acc_ref):
+def _gq_kernel(q_ref, g_ref, k_ref, v_ref, tt_ref, wt_ref, gw_ref, gt_ref, acc_ref):
     blocks = k_ref.shape[0] // KB
     acc_ref[...] = jnp.zeros_like(acc_ref)
     def step(j, carry):
@@ -56,9 +56,11 @@
             acc_ref[:, cols] += _nn(ds, k)
         return carry
     lax.fori_loop(0, blocks, step, 0)
-    o_ref[...] = acc_ref[...].astype(o_ref.dtype)
-
-def _gkv_kernel(q_ref, g_ref, k_ref, v_ref, dk_ref, dv_ref, acck_ref, accv_ref):
+    grad_rows = acc_ref[...].astype(jnp.bfloat16)
+    gw_ref[...] = _nn(tt_ref[...], grad_rows)
+    gt_ref[...] = _nn(grad_rows, wt_ref[...])
+
+def _gkv_kernel(q_ref, g_ref, k_ref, v_ref, tt_ref, wkt_ref, wvt_ref, gk_ref, gv_ref, gt_ref, acck_ref, accv_ref):
     blocks = q_ref.shape[0] // KB
     acck_ref[...] = jnp.zeros_like(acck_ref)
     accv_ref[...] = jnp.zeros_like(accv_ref)
@@ -76,21 +78,29 @@
             accv_ref[:, cols] += _nn(w, g)
         return carry
     lax.fori_loop(0, blocks, step, 0)
-    dk_ref[...] = acck_ref[...].astype(dk_ref.dtype)
-    dv_ref[...] = accv_ref[...].astype(dv_ref.dtype)
+    grad_key = acck_ref[...].astype(jnp.bfloat16)
+    grad_val = accv_ref[...].astype(jnp.bfloat16)
+    gk_ref[...] = _nn(tt_ref[...], grad_key)
+    gv_ref[...] = _nn(tt_ref[...], grad_val)
+    gt_ref[...] = _nn(grad_key, wkt_ref[...]) + _nn(grad_val, wvt_ref[...])
 
 def attend_fwd(q, k_all, v_all):
     return pl.pallas_call(_fwd_kernel, out_shape=jax.ShapeDtypeStruct(q.shape, jnp.bfloat16),
         scratch_shapes=[pltpu.VMEM(q.shape, jnp.float32)])(q, k_all, v_all)
 
-def attend_gq(q, g, k_all, v_all):
-    return pl.pallas_call(_gq_kernel, out_shape=jax.ShapeDtypeStruct(q.shape, jnp.bfloat16),
-        scratch_shapes=[pltpu.VMEM(q.shape, jnp.float32)])(q, g, k_all, v_all)
-
-def attend_gkv(q_all, g_all, k, v):
-    sh = jax.ShapeDtypeStruct(k.shape, jnp.bfloat16)
-    return pl.pallas_call(_gkv_kernel, out_shape=(sh, sh),
-        scratch_shapes=[pltpu.VMEM(k.shape, jnp.float32), pltpu.VMEM(k.shape, jnp.float32)],)(q_all, g_all, k, v)
+def attend_gq(q, g, k_all, v_all, tokens_t, w_t):
+    f32 = jnp.float32
+    outs = (jax.ShapeDtypeStruct((H, H), f32), jax.ShapeDtypeStruct(q.shape, f32))
+    return pl.pallas_call(_gq_kernel, out_shape=outs,
+        scratch_shapes=[pltpu.VMEM(q.shape, f32)])(q, g, k_all, v_all, tokens_t, w_t)
+
+def attend_gkv(q_all, g_all, k, v, tokens_t, wk_t, wv_t):
+    f32 = jnp.float32
+    outs = (jax.ShapeDtypeStruct((H, H), f32), jax.ShapeDtypeStruct((H, H), f32),
+            jax.ShapeDtypeStruct(k.shape, f32))
+    return pl.pallas_call(_gkv_kernel, out_shape=outs,
+        scratch_shapes=[pltpu.VMEM(k.shape, f32), pltpu.VMEM(k.shape, f32)],
+        )(q_all, g_all, k, v, tokens_t, wk_t, wv_t)
 
 
 def from_neighbour(array, axis, step):
@@ -223,15 +233,13 @@
 
     grad_attn_all = gather_tiles(grad_attn, "col").reshape(-1, H)
 
-    grad_query = attend_gq(query_own, grad_attn, key_all, value_all)
-    grad_key, grad_val = attend_gkv(query_all, grad_attn_all, key_own, value_own)
-
-    g_query = jnp.einsum("nh,ne->he", tokens, grad_query, preferred_element_type=jnp.float32)
-    g_key = jnp.einsum("nh,ne->he", tokens, grad_key, preferred_element_type=jnp.float32)
-    g_value = jnp.einsum("nh,ne->he", tokens, grad_val, preferred_element_type=jnp.float32)
-    grad_tokens = grad_mixed + jnp.dot(grad_query, w_query.T, preferred_element_type=jnp.float32)
-    grad_tokens = grad_tokens + jnp.dot(grad_key, w_key.T, preferred_element_type=jnp.float32)
-    grad_tokens = grad_tokens + jnp.dot(grad_val, w_value.T, preferred_element_type=jnp.float32)
+    tokens_t = tokens.T
+    g_query, tokens_grad_q = attend_gq(query_own, grad_attn, key_all, value_all, tokens_t, w_query.T)
+    g_key, g_value, tokens_grad_kv = attend_gkv(
+        query_all, grad_attn_all, key_own, value_own, tokens_t, w_key.T, w_value.T
+    )
+
+    grad_tokens = grad_mixed + tokens_grad_q + tokens_grad_kv
     grad_pooled = rms_backward(token_live * grad_tokens, normed, rscale)
     grad_scaled = (grad_pooled / (member_count + 1.0)).astype(jnp.bfloat16)
     grad_hidden = jnp.einsum(

time: 214 us -> 214 us (level)
  matrix products: 27.7 us -> 17.1 us
  local copies, waits for them, and re-layouts: 17.1 us -> 26.1 us
  other arithmetic: 9.44 us -> 12.2 us
  waiting for transfers between devices: 57.3 us -> 55 us
    dot_general x6 -> x0, matrix products: 10.5 us -> none  [the longest x1 2.09 us: body(): jnp.dot(grad_query, w_query.T, preferred_element_type=jnp.float32)]
    pallas_call x0 -> x2, local copies, waits for them, and re-layouts: none -> 4.24 us  [the longest x1 2.2 us: attend_gkv(): pl.pallas_call(_gkv_kernel, out_shape=outs, scratch_shapes=[pltpu.VMEM(k....]
    all_to_all x2, waiting for transfers between devices: 35.2 us -> 32.9 us  [gather_tiles(): return lax.all_to_all(copies, axis, 0, 0, tiled=True)]
    unnamed x54 -> x55, local copies, waits for them, and re-layouts: 4.15 us -> 6.42 us
  transfers between devices with their start and end apart: 7 -> 7, of which waited for: 4 -> 4; matrix products, arithmetic and copies ran while one was open for 10% -> 11% of each run, Pallas kernels for 5% -> 6%
where the time goes in v7:
time: 214 us; the launch traced here: 213 us
  waiting for transfers between devices  55 us (26%)
  starting transfers between devices  37.2 us (17%)
  Pallas kernels  35.8 us (17%)
  blocking collectives  27.4 us (13%)
  local copies, waits for them, and re-layouts  26.1 us (12%)
  matrix products  17.1 us (8%)
  other arithmetic  12.2 us (6%)
  between operations  2.36 us (1%)
    all_to_all x2, waiting for transfers between devices, gather_tiles(): return lax.all_to_all(copies, axis, 0, 0, tiled=True)  32.9 us
    all_to_all x1, blocking collectives, all_reduce_a2a(): chunks = lax.all_to_all(rows_in, axes, 0, 0, tiled=True)  27.4 us
    all_to_all x2, starting transfers between devices, gather_tiles(): return lax.all_to_all(copies, axis, 0, 0, tiled=True)  19.9 us
    all_to_all x1, waiting for transfers between devices, all_reduce_a2a(): return lax.all_to_all(copies, axes, 0, 0, tiled=True).astype(jnp.float32)  15 us
    pallas_call x1, Pallas kernels, attend_gkv(): pl.pallas_call(_gkv_kernel, out_shape=outs, scratch_shapes=[pltpu.VMEM(k....  14.8 us
    pallas_call x1, Pallas kernels, attend_gq(): pl.pallas_call(_gq_kernel, out_shape=outs, scratch_shapes=[pltpu.VMEM(q.s...  12 us
    ppermute x4, starting transfers between devices, from_neighbour(): return lax.ppermute(array, axis, pairs)  12 us
    pallas_call x1, Pallas kernels, attend_fwd(): pl.pallas_call(_fwd_kernel, out_shape=jax.ShapeDtypeStruct(q.shape, jnp.b...  8.98 us
  transfers between devices with their start and end apart: 7, of which 4 were waited for; matrix products, arithmetic and copies ran while one was open for 11% of the time, Pallas kernels for 6%

profile of v7, /device:TPU:0, one launch (start us, length us, event | category | flops | bytes accessed | tf_op | source)
XLA Modules:
  0.0 213.1 jit_solution(13863892157493662693)
XLA Ops:
  1.4 2.0 fusion.12
  3.4 2.3 %collective-permute-start = (bf16[1024,256]{1,0:T(8,128)(2,1)}, bf16[1024,256]{1,0:T(8,128)(2,1)}, u32[]{:S(2)}, u32[]{:S(2)}) collective-permute-start(bf16[1024,256]{1,0:T(8,128)(2,1)} %fusion.12), channel_id=1, source_target_pairs={{0,8},{8,16},{16,24},{24,32},{32,40},{40,48},{48,56},{56,64},{64,7... | collective-permute-start | bytes 1572872 | tf_op jit(solution)/shard_map/ppermute | solution.py:109
  7.0 7.1 %collective-permute-start.2 = (bf16[1024,256]{1,0:T(8,128)(2,1)}, bf16[1024,256]{1,0:T(8,128)(2,1)}, u32[]{:S(2)}, u32[]{:S(2)}) collective-permute-start(bf16[1024,256]{1,0:T(8,128)(2,1)} %fusion.12), channel_id=1, source_target_pairs={{0,1},{1,2},{2,3},{3,4},{4,5},{5,6},{6,7},{8,9},{9,10},{10,11},{11... | collective-permute-start | bytes 1572872 | tf_op jit(solution)/shard_map/ppermute | solution.py:109
  15.4 3.1 %fusion.5 = bf16[8,5,128,128]{3,2,0,1:T(8,128)(2,1)} fusion(s32[1,1,8,5,128,128]{5,4,3,2,1,0:T(8,128)} %param.13), kind=kLoop, calls=%fused_computation.11 | loop fusion | flops 655360 | bytes 3932160 | tf_op jit(solution)/shard_map/convert.7
  18.5 1.8 reduce_sum.84
  21.2 1.4 fusion.22
  22.7 7.1 %collective-permute-done.3 = bf16[1024,256]{1,0:T(8,128)(2,1)} collective-permute-done((bf16[1024,256]{1,0:T(8,128)(2,1)}, bf16[1024,256]{1,0:T(8,128)(2,1)}, u32[]{:S(2)}, u32[]{:S(2)}) %collective-permute-start.3) | collective-permute-done | bytes 524320 | tf_op jit(solution)/shard_map/ppermute | solution.py:109
  29.7 1.4 fusion.39
  31.2 1.3 fusion.40
  32.5 1.3 convolution_add_fusion.1
  33.9 1.6 fusion.6
  37.0 1.5 broadcast_in_dim.10
  38.5 15.9 %all-to-all-start = ((bf16[8,512,256]{2,1,0:T(8,128)(2,1)}), bf16[8,512,256]{2,1,0:T(8,128)(2,1)S(1)}, u32[]{:S(2)}, u32[]{:S(2)}) async-start(bf16[8,512,256]{2,1,0:T(8,128)(2,1)} %broadcast_in_dim.10), calls=%async_computation | async-start | bytes 4194304 | tf_op jit(solution)/shard_map/all_to_all | solution.py:115
  58.2 25.0 %all-to-all-done = bf16[8,512,256]{2,1,0:T(8,128)(2,1)S(1)} async-done(((bf16[8,512,256]{2,1,0:T(8,128)(2,1)}), bf16[8,512,256]{2,1,0:T(8,128)(2,1)S(1)}, u32[]{:S(2)}, u32[]{:S(2)}) %all-to-all-start) | async-done | bytes 2097184 | tf_op jit(solution)/shard_map/all_to_all | solution.py:115
  83.2 1.8 convolution_convert_fusion
  85.0 2.8 %fusion.60 = (bf16[4096,256]{1,0:T(8,128)(2,1)}, bf16[4096,256]{1,0:T(8,128)(2,1)}, bf16[4096,256]{1,0:T(8,128)(2,1)}) fusion(bf16[4096,768]{1,0:T(8,128)(2,1)S(1)} %convolution_convert_fusion), kind=kLoop, calls=%fused_computation.90 | loop fusion | bytes 12582912 | tf_op jit(solution)/shard_map/slice | solution.py:212
  87.8 9.0 %shard_map.171 = bf16[512,256]{1,0:T(8,128)(2,1)} custom-call(bf16[512,256]{1,0:T(8,128)(2,1)} %get-tuple-element.30.q_ref, bf16[4096,256]{1,0:T(8,128)(2,1)} %get-tuple-element.22.k_ref, bf16[4096,256]{1,0:T(8,128)(2,1)} %get-tuple-element.21.v_ref), custom_call_target="tpu_custom_call" | custom-call | tf_op jit(solution)/shard_map/pallas_call | solution.py:88
  100.0 1.5 broadcast_in_dim.11
  101.4 3.9 %all-to-all-start.1 = ((bf16[8,512,256]{2,1,0:T(8,128)(2,1)}), bf16[8,512,256]{2,1,0:T(8,128)(2,1)S(1)}, u32[]{:S(2)}, u32[]{:S(2)}) async-start(bf16[8,512,256]{2,1,0:T(8,128)(2,1)} %broadcast_in_dim.11), calls=%async_computation.1 | async-start | bytes 4194304 | tf_op jit(solution)/shard_map/all_to_all | solution.py:115
  106.9 1.6 copy.31
  109.3 12.0 %shard_map.172 = (f32[256,256]{1,0:T(8,128)}, f32[512,256]{1,0:T(8,128)}) custom-call(bf16[512,256]{1,0:T(8,128)(2,1)} %get-tuple-element.30.q_ref, bf16[512,256]{1,0:T(8,128)(2,1)} %copy-done.10, bf16[4096,256]{1,0:T(8,128)(2,1)} %get-tuple-element.22.k_ref, bf16[4096,256]{1,0:T(8,128)(2,1)} %get-tuple-element.21.v_ref, ...), custom_call_target="tpu_custom_call" | custom-call | tf_op jit(solution)/shard_map/pallas_call | solution.py:94
  121.3 2.0 copy.29
  123.3 1.7 fusion.56
  125.1 7.9 %all-to-all-done.1 = bf16[8,512,256]{2,1,0:T(8,128)(2,1)S(1)} async-done(((bf16[8,512,256]{2,1,0:T(8,128)(2,1)}), bf16[8,512,256]{2,1,0:T(8,128)(2,1)S(1)}, u32[]{:S(2)}, u32[]{:S(2)}) %all-to-all-start.1) | async-done | bytes 2097184 | tf_op jit(solution)/shard_map/all_to_all | solution.py:115
  134.3 14.8 %shard_map.173 = (f32[256,256]{1,0:T(8,128)}, f32[256,256]{1,0:T(8,128)}, f32[512,256]{1,0:T(8,128)}) custom-call(bf16[4096,256]{1,0:T(8,128)(2,1)} %get-tuple-element.20.q_ref, bf16[4096,256]{1,0:T(8,128)(2,1)} %bitcast.103, bf16[512,256]{1,0:T(8,128)(2,1)} %get-tuple-element.29.k_ref, bf16[512,256]{1,0:T(8,128)(2,1)} %get-tuple-element.28.v_ref, ...), custom_call_target="tpu_custom_call" | custom-call | tf_op jit(solution)/shard_map/pallas_call | solution.py:101
  149.1 2.2 %copy.32 = f32[512,256]{0,1:T(8,128)} copy(f32[512,256]{1,0:T(8,128)} %get-tuple-element.13) | data formatting | bytes 1048576 | tf_op jit(solution)/shard_map/pallas_call | solution.py:101
  151.3 1.4 fusion.24
  153.3 3.4 %fusion.8 = f32[256,256]{1,0:T(8,128)} fusion(bf16[1024,256]{1,0:T(8,128)(2,1)} %bitcast.109, f32[1024,256]{1,0:T(8,128)} %copy-done.11, f32[1024]{0:T(1024)S(1)} %copy-done.17, s32[1,1,512,1024]{3,2,1,0:T(8,128)S(1)} %copy-done.7, f32[256,512]{1,0:T(8,128)S(1)} %get-tuple-element.32, f32[512]{0:T(512)} %copy-done.23, f32[512]{0:T(512)} %broadcast_multiply_fusion, ...), kind=kOutput, calls=%fused_computation.15 | convolution fusion | flops 407109632 | bytes 5520384 | tf_op jit(solution)/shard_map/gh,ge->he/dot_general | solution.py:249
  156.7 4.7 %concatenate.7 = f32[1344,256]{1,0:T(8,128)S(1)} concatenate(f32[256,256]{1,0:T(8,128)} %fusion.8, f32[256,256]{1,0:T(8,128)} %get-tuple-element.14, f32[256,256]{1,0:T(8,128)} %get-tuple-element.15, f32[256,256]{1,0:T(8,128)} %get-tuple-element.16, f32[256,256]{1,0:T(8,128)S(1)} %copy-done.9, f32[1,256]{1,0:T(1,128)} %bitcast.111, f32[63,256]{1,0:T(8,128)S(1)} %broadcast_in_dim.13), dimensions={0} | concatenate | bytes 2752512 | tf_op jit(solution)/shard_map/concatenate | solution.py:256
  161.6 27.4 %all_to_all.20 = f32[128,21,128]{2,1,0:T(8,128)S(1)} all-to-all(f32[128,21,128]{2,1,0:T(8,128)S(1)} %reshape.142), channel_id=1, replica_groups=mesh['row'=16,'col'=8] {'row','col'}, dimensions={0} | all-to-all | bytes 2752512 | tf_op jit(solution)/shard_map/all_to_all | solution.py:124
  190.1 5.4 %all-to-all-start.3 = ((bf16[128,21,128]{2,1,0:T(8,128)(2,1)}), bf16[128,21,128]{2,1,0:T(8,128)(2,1)S(1)}, u32[]{:S(2)}, u32[]{:S(2)}) async-start(bf16[128,21,128]{2,1,0:T(8,128)(2,1)} %broadcast_in_dim.14), calls=%async_computation.3 | async-start | bytes 1572864 | tf_op jit(solution)/shard_map/all_to_all | solution.py:127
  196.1 15.0 %all-to-all-done.3 = bf16[128,21,128]{2,1,0:T(8,128)(2,1)S(1)} async-done(((bf16[128,21,128]{2,1,0:T(8,128)(2,1)}), bf16[128,21,128]{2,1,0:T(8,128)(2,1)S(1)}, u32[]{:S(2)}, u32[]{:S(2)}) %all-to-all-start.3) | async-done | bytes 688160 | tf_op jit(solution)/shard_map/all_to_all | solution.py:127
  (89 shorter events, 19.3 us)
Async XLA Ops:
  0.6 96.1 %copy-start = (bf16[256,256]{1,0:T(8,128)(2,1)S(1)}, bf16[256,256]{1,0:T(8,128)(2,1)}, u32[]{:S(2)}) copy-start(bf16[256,256]{1,0:T(8,128)(2,1)} %param.21) | copy-start | bytes 393220
  1.3 34.4 %copy-start.16 = (f32[1024]{0:T(1024)}, f32[1024]{0:T(1024)S(1)}, u32[]{:S(2)}) copy-start(f32[1024]{0:T(1024)S(1)} %fusion.52) | copy-start | bytes 12292
  3.4 17.6 %copy-start.1 = (s32[1,1,8,5,128,128]{5,4,3,2,1,0:T(8,128)S(1)}, s32[1,1,8,5,128,128]{5,4,3,2,1,0:T(8,128)}, u32[]{:S(2)}) copy-start(s32[1,1,8,5,128,128]{5,4,3,2,1,0:T(8,128)} %param.13) | copy-start | bytes 7864324
  3.4 29.1 %collective-permute-start = (bf16[1024,256]{1,0:T(8,128)(2,1)}, bf16[1024,256]{1,0:T(8,128)(2,1)}, u32[]{:S(2)}, u32[]{:S(2)}) collective-permute-start(bf16[1024,256]{1,0:T(8,128)(2,1)} %fusion.12), channel_id=1, source_target_pairs={{0,8},{8,16},{16,24},{24,32},{32,40},{40,48},{48,56},{56,64},{64,7... | collective-permute-start | bytes 1572872 | tf_op jit(solution)/shard_map/ppermute | solution.py:109
  5.7 24.0 %collective-permute-start.3 = (bf16[1024,256]{1,0:T(8,128)(2,1)}, bf16[1024,256]{1,0:T(8,128)(2,1)}, u32[]{:S(2)}, u32[]{:S(2)}) collective-permute-start(bf16[1024,256]{1,0:T(8,128)(2,1)} %fusion.12), channel_id=1, source_target_pairs={{1,0},{2,1},{3,2},{4,3},{5,4},{6,5},{7,6},{9,8},{10,9},{11,10},{12... | collective-permute-start | bytes 1572872 | tf_op jit(solution)/shard_map/ppermute | solution.py:109
  7.0 24.1 %collective-permute-start.2 = (bf16[1024,256]{1,0:T(8,128)(2,1)}, bf16[1024,256]{1,0:T(8,128)(2,1)}, u32[]{:S(2)}, u32[]{:S(2)}) collective-permute-start(bf16[1024,256]{1,0:T(8,128)(2,1)} %fusion.12), channel_id=1, source_target_pairs={{0,1},{1,2},{2,3},{3,4},{4,5},{5,6},{6,7},{8,9},{9,10},{10,11},{11... | collective-permute-start | bytes 1572872 | tf_op jit(solution)/shard_map/ppermute | solution.py:109
  14.1 19.8 %collective-permute-start.1 = (bf16[1024,256]{1,0:T(8,128)(2,1)}, bf16[1024,256]{1,0:T(8,128)(2,1)}, u32[]{:S(2)}, u32[]{:S(2)}) collective-permute-start(bf16[1024,256]{1,0:T(8,128)(2,1)} %fusion.12), channel_id=1, source_target_pairs={{8,0},{16,8},{24,16},{32,24},{40,32},{48,40},{56,48},{64,56},{72,6... | collective-permute-start | bytes 1572872 | tf_op jit(solution)/shard_map/ppermute | solution.py:109
  18.5 2.8 %copy-start.5 = (bf16[1,1,1024,256]{3,2,1,0:T(8,128)(2,1)S(1)}, bf16[1,1,1024,256]{3,2,1,0:T(8,128)(2,1)}, u32[]{:S(2)}) copy-start(bf16[1,1,1024,256]{3,2,1,0:T(8,128)(2,1)} %param.12) | copy-start | bytes 1572868
  20.3 15.4 %copy-start.23 = (f32[512]{0:T(512)}, f32[512]{0:T(512)S(1)}, u32[]{:S(2)}) copy-start(f32[512]{0:T(512)S(1)} %convert_add_fusion.2) | copy-start | bytes 6148
  21.2 9.9 %copy-start.3 = (bf16[8,5,128,128]{3,2,0,1:T(8,128)(2,1)S(1)}, bf16[8,5,128,128]{3,2,0,1:T(8,128)(2,1)}, u32[]{:S(2)}) copy-start(bf16[8,5,128,128]{3,2,0,1:T(8,128)(2,1)} %fusion.5) | copy-start | bytes 3932164
  33.8 1.6 copy-start.15
  33.9 1.9 copy-start.6
  35.4 1.2 copy-start.12
  35.8 1.1 copy-start.11
  38.5 15.9 %copy-start.24 = (bf16[256]{0:T(256)(128)(2,1)S(1)}, bf16[256]{0:T(256)(128)(2,1)}, u32[]{:S(2)}) copy-start(bf16[256]{0:T(256)(128)(2,1)} %param.22) | copy-start | bytes 1540
  38.5 16.5 %copy-start.13 = (bf16[256,256]{1,0:T(8,128)(2,1)S(1)}, bf16[256,256]{1,0:T(8,128)(2,1)}, u32[]{:S(2)}) copy-start(bf16[256,256]{1,0:T(8,128)(2,1)} %param.18) | copy-start | bytes 393220
  38.5 44.7 %all-to-all-start = ((bf16[8,512,256]{2,1,0:T(8,128)(2,1)}), bf16[8,512,256]{2,1,0:T(8,128)(2,1)S(1)}, u32[]{:S(2)}, u32[]{:S(2)}) async-start(bf16[8,512,256]{2,1,0:T(8,128)(2,1)} %broadcast_in_dim.10), calls=%async_computation | async-start | bytes 4194304 | tf_op jit(solution)/shard_map/all_to_all | solution.py:115
  87.8 10.2 %copy-start.22 = (f32[1,1,512]{2,1,0:T(1,128)S(1)}, f32[1,1,512]{2,1,0:T(1,128)}, u32[]{:S(2)}) copy-start(f32[1,1,512]{2,1,0:T(1,128)} %param.23) | copy-start | bytes 6148
  87.8 10.2 %copy-start.18 = (f32[256]{0:T(256)S(1)}, f32[256]{0:T(256)}, u32[]{:S(2)}) copy-start(f32[256]{0:T(256)} %convert_element_type.148) | copy-start | bytes 3076
  98.9 2.6 %copy-start.21 = (f32[512]{0:T(512)}, f32[512]{0:T(512)S(1)}, u32[]{:S(2)}) copy-start(f32[512]{0:T(512)S(1)} %broadcast_multiply_fusion.1) | copy-start | bytes 6148
  99.2 0.7 copy-start.10
  101.4 4.7 %copy-start.14 = (bf16[256,256]{1,0:T(8,128)(2,1)S(1)}, bf16[256,256]{1,0:T(8,128)(2,1)}, u32[]{:S(2)}) copy-start(bf16[256,256]{1,0:T(8,128)(2,1)} %param.19) | copy-start | bytes 393220
  101.4 31.5 %all-to-all-start.1 = ((bf16[8,512,256]{2,1,0:T(8,128)(2,1)}), bf16[8,512,256]{2,1,0:T(8,128)(2,1)S(1)}, u32[]{:S(2)}, u32[]{:S(2)}) async-start(bf16[8,512,256]{2,1,0:T(8,128)(2,1)} %broadcast_in_dim.11), calls=%async_computation.1 | async-start | bytes 4194304 | tf_op jit(solution)/shard_map/all_to_all | solution.py:115
  109.3 14.1 %copy-start.4 = (bf16[512,256]{1,0:T(8,128)(2,1)S(1)}, bf16[512,256]{1,0:T(8,128)(2,1)}, u32[]{:S(2)}) copy-start(bf16[512,256]{1,0:T(8,128)(2,1)} %shard_map.171) | copy-start | bytes 786436
  133.0 1.3 copy-start.2
  134.3 17.0 %copy-start.19 = (f32[256]{0:T(256)S(1)}, f32[256]{0:T(256)}, u32[]{:S(2)}) copy-start(f32[256]{0:T(256)} %convert_element_type.148) | copy-start | bytes 3076
  149.1 4.2 %copy-start.7 = (s32[1,1,512,1024]{3,2,1,0:T(8,128)S(1)}, s32[1,1,512,1024]{3,2,1,0:T(8,128)}, u32[]{:S(2)}) copy-start(s32[1,1,512,1024]{3,2,1,0:T(8,128)} %param.15) | copy-start | bytes 6291460
  149.1 4.2 %copy-start.8 = (f32[512,256]{0,1:T(8,128)S(1)}, f32[512,256]{0,1:T(8,128)}, u32[]{:S(2)}) copy-start(f32[512,256]{0,1:T(8,128)} %copy.29) | copy-start | bytes 1572868
  149.1 4.2 %copy-start.17 = (f32[1024]{0:T(1024)S(1)}, f32[1024]{0:T(1024)}, u32[]{:S(2)}) copy-start(f32[1024]{0:T(1024)} %copy-done.16) | copy-start | bytes 12292
  153.3 3.4 %copy-start.9 = (f32[256,256]{1,0:T(8,128)S(1)}, f32[256,256]{1,0:T(8,128)}, u32[]{:S(2)}) copy-start(f32[256,256]{1,0:T(8,128)} %fusion.56) | copy-start | bytes 786436
  188.9 6.6 %copy-start.20 = (f32[512]{0:T(512)S(1)}, f32[512]{0:T(512)}, u32[]{:S(2)}) copy-start(f32[512]{0:T(512)} %get-tuple-element.18) | copy-start | bytes 6148
  190.1 21.1 %all-to-all-start.3 = ((bf16[128,21,128]{2,1,0:T(8,128)(2,1)}), bf16[128,21,128]{2,1,0:T(8,128)(2,1)S(1)}, u32[]{:S(2)}, u32[]{:S(2)}) async-start(bf16[128,21,128]{2,1,0:T(8,128)(2,1)} %broadcast_in_dim.14), calls=%async_computation.3 | async-start | bytes 1572864 | tf_op jit(solution)/shard_map/all_to_all | solution.py:127

commit v8 on v4

--- a/solution.py
+++ b/solution.py
@@ -28,7 +28,8 @@
 def _half_tanh(q, k):
     return jnp.tanh(_nt(q, k) * (0.5 / math.sqrt(HD)) - 0.5 * SHIFT)
 
-def _fwd_kernel(q_ref, k_ref, v_ref, o_ref, acc_ref):
+def _fwd_kernel(q_ref, k_ref, v_ref, tok_ref, gval_ref, sw_ref, wo_ref, wot_ref,
+                att_ref, mixed_ref, gproj_ref, gattn_ref, acc_ref):
     blocks = k_ref.shape[0] // KB
     acc_ref[...] = jnp.zeros_like(acc_ref)
     def step(j, carry):
@@ -40,7 +41,19 @@
             acc_ref[:, cols] += _nn(w, v_ref[rows, cols])
         return carry
     lax.fori_loop(0, blocks, step, 0)
-    o_ref[...] = acc_ref[...].astype(o_ref.dtype)
+    attended = acc_ref[...].astype(jnp.bfloat16)
+    att_ref[...] = attended
+    proj = _nn(attended, wo_ref[...])
+    pscale = lax.rsqrt(jnp.mean(proj * proj, axis=-1, keepdims=True) + EPS)
+    pnormed = proj * pscale
+    mixed_ref[...] = tok_ref[...].astype(jnp.float32) + pnormed
+    grad_mixed = gval_ref[...] * sw_ref[...].astype(jnp.float32)
+    grad_proj = pscale * (grad_mixed - pnormed * jnp.mean(grad_mixed * pnormed, axis=-1, keepdims=True))
+    grad_proj = grad_proj.astype(jnp.bfloat16)
+    gproj_ref[...] = grad_proj
+    grad_attn = _nn(grad_proj, wot_ref[...]).astype(jnp.bfloat16)
+    for c in range(gattn_ref.shape[0]):
+        gattn_ref[c] = grad_attn
 
 def _gq_kernel(q_ref, g_ref, k_ref, v_ref, o_ref, acc_ref):
     blocks = k_ref.shape[0] // KB
@@ -79,9 +92,13 @@
     dk_ref[...] = acck_ref[...].astype(dk_ref.dtype)
     dv_ref[...] = accv_ref[...].astype(dv_ref.dtype)
 
-def attend_fwd(q, k_all, v_all):
-    return pl.pallas_call(_fwd_kernel, out_shape=jax.ShapeDtypeStruct(q.shape, jnp.bfloat16),
-        scratch_shapes=[pltpu.VMEM(q.shape, jnp.float32)])(q, k_all, v_all)
+def attend_fwd(q, k_all, v_all, tokens, grad_value, w_score, w_out, copies):
+    bf16, f32 = jnp.bfloat16, jnp.float32
+    outs = (jax.ShapeDtypeStruct(q.shape, bf16), jax.ShapeDtypeStruct(q.shape, f32),
+            jax.ShapeDtypeStruct(q.shape, bf16), jax.ShapeDtypeStruct((copies,) + q.shape, bf16))
+    return pl.pallas_call(_fwd_kernel, out_shape=outs,
+        scratch_shapes=[pltpu.VMEM(q.shape, f32)])(
+            q, k_all, v_all, tokens, grad_value, w_score.reshape(1, -1), w_out, w_out.T)
 
 def attend_gq(q, g, k_all, v_all):
     return pl.pallas_call(_gq_kernel, out_shape=jax.ShapeDtypeStruct(q.shape, jnp.bfloat16),
@@ -207,21 +224,20 @@
     key_own = qkv_own[:, H:2 * H]
     value_own = qkv_own[:, 2 * H:]
 
-    attended = attend_fwd(query_own, key_all, value_all)
-    proj = jnp.dot(attended, w_out, preferred_element_type=jnp.float32)
-    pnormed, pscale = rms_forward(proj)
-    mixed = tokens.astype(jnp.float32) + pnormed
     score_w = w_score.astype(jnp.float32)
-    value_out = token_live[:, 0] * jnp.sum(mixed * score_w, axis=1)
     loss_weight = 1.0 / math.sqrt(lax.axis_size("row") * lax.axis_size("col") * NT)
     grad_value = token_live[:, 0] * cotangent[0, 0] * loss_weight
+    attended, mixed, grad_proj, grad_attn_copies = attend_fwd(
+        query_own, key_all, value_all, tokens, grad_value[:, None], w_score, w_out,
+        lax.axis_size("col"),
+    )
+    value_out = token_live[:, 0] * jnp.sum(mixed * score_w, axis=1)
     g_score = jnp.sum(mixed * grad_value[:, None], axis=0)
     grad_mixed = grad_value[:, None] * score_w
-    grad_proj = rms_backward(grad_mixed, pnormed, pscale).astype(jnp.bfloat16)
     g_out = jnp.einsum("nh,ne->he", attended, grad_proj, preferred_element_type=jnp.float32)
-    grad_attn = jnp.dot(grad_proj, w_out.T, preferred_element_type=jnp.float32).astype(jnp.bfloat16)
-
-    grad_attn_all = gather_tiles(grad_attn, "col").reshape(-1, H)
+    grad_attn = grad_attn_copies[0]
+
+    grad_attn_all = lax.all_to_all(grad_attn_copies, "col", 0, 0, tiled=True).reshape(-1, H)
 
     grad_query = attend_gq(query_own, grad_attn, key_all, value_all)
     grad_key, grad_val = attend_gkv(query_all, grad_attn_all, key_own, value_own)

time: 214 us -> 212 us (level)
  matrix products: 27.7 us -> 24.3 us
    all_to_all x2 -> x1, waiting for transfers between devices: 35.2 us -> 24.3 us  [gather_tiles(): return lax.all_to_all(copies, axis, 0, 0, tiled=True)]
    all_to_all x0 -> x1, waiting for transfers between devices: none -> 9.4 us  [body(): lax.all_to_all(grad_attn_copies, 'col', 0, 0, tiled=True).reshape(-1, H)]
    all_to_all x0 -> x1, starting transfers between devices: none -> 3.92 us  [body(): lax.all_to_all(grad_attn_copies, 'col', 0, 0, tiled=True).reshape(-1, H)]
    all_to_all x2 -> x1, starting transfers between devices: 19.7 us -> 15.9 us  [gather_tiles(): return lax.all_to_all(copies, axis, 0, 0, tiled=True)]
  transfers between devices with their start and end apart: 7 -> 7, of which waited for: 4 -> 4; matrix products, arithmetic and copies ran while one was open for 10% -> 11% of each run, Pallas kernels for 5% -> 5%
where the time goes in v8:
time: 212 us; the launch traced here: 211 us
  waiting for transfers between devices  55.8 us (26%)
  starting transfers between devices  37.3 us (18%)
  Pallas kernels  36.3 us (17%)
  blocking collectives  27.4 us (13%)
  matrix products  24.3 us (11%)
  local copies, waits for them, and re-layouts  17 us (8%)
  other arithmetic  10.3 us (5%)
  between operations  2.44 us (1%)
    all_to_all x1, blocking collectives, all_reduce_a2a(): chunks = lax.all_to_all(rows_in, axes, 0, 0, tiled=True)  27.4 us
    all_to_all x1, waiting for transfers between devices, gather_tiles(): return lax.all_to_all(copies, axis, 0, 0, tiled=True)  24.3 us
    all_to_all x1, starting transfers between devices, gather_tiles(): return lax.all_to_all(copies, axis, 0, 0, tiled=True)  15.9 us
    all_to_all x1, waiting for transfers between devices, all_reduce_a2a(): return lax.all_to_all(copies, axes, 0, 0, tiled=True).astype(jnp.float32)  15 us
    pallas_call x1, Pallas kernels, attend_gkv(): pl.pallas_call(_gkv_kernel, out_shape=(sh, sh), scratch_shapes=[pltpu.VME...  14.1 us
    ppermute x4, starting transfers between devices, from_neighbour(): return lax.ppermute(array, axis, pairs)  12 us
    pallas_call x1, Pallas kernels, attend_gq(): pl.pallas_call(_gq_kernel, out_shape=jax.ShapeDtypeStruct(q.shape, jnp.bf...  11.6 us
    pallas_call x1, Pallas kernels, attend_fwd(): pl.pallas_call(_fwd_kernel, out_shape=outs, scratch_shapes=[pltpu.VMEM(q....  10.6 us
  transfers between devices with their start and end apart: 7, of which 4 were waited for; matrix products, arithmetic and copies ran while one was open for 11% of the time, Pallas kernels for 5%

profile of v8, /device:TPU:0, one launch (start us, length us, event | category | flops | bytes accessed | tf_op | source)
XLA Modules:
  0.0 210.7 jit_solution(3511881897217875567)
XLA Ops:
  1.3 2.1 fusion.13
  3.4 2.4 %collective-permute-start = (bf16[1024,256]{1,0:T(8,128)(2,1)}, bf16[1024,256]{1,0:T(8,128)(2,1)}, u32[]{:S(2)}, u32[]{:S(2)}) collective-permute-start(bf16[1024,256]{1,0:T(8,128)(2,1)} %fusion.13), channel_id=1, source_target_pairs={{0,8},{8,16},{16,24},{24,32},{32,40},{40,48},{48,56},{56,64},{64,7... | collective-permute-start | bytes 1572872 | tf_op jit(solution)/shard_map/ppermute | solution.py:116
  7.0 7.1 %collective-permute-start.2 = (bf16[1024,256]{1,0:T(8,128)(2,1)}, bf16[1024,256]{1,0:T(8,128)(2,1)}, u32[]{:S(2)}, u32[]{:S(2)}) collective-permute-start(bf16[1024,256]{1,0:T(8,128)(2,1)} %fusion.13), channel_id=1, source_target_pairs={{0,1},{1,2},{2,3},{3,4},{4,5},{5,6},{6,7},{8,9},{9,10},{10,11},{11... | collective-permute-start | bytes 1572872 | tf_op jit(solution)/shard_map/ppermute | solution.py:116
  15.4 3.1 %fusion.5 = bf16[8,5,128,128]{3,2,0,1:T(8,128)(2,1)} fusion(s32[1,1,8,5,128,128]{5,4,3,2,1,0:T(8,128)} %param.13), kind=kLoop, calls=%fused_computation.11 | loop fusion | flops 655360 | bytes 3932160 | tf_op jit(solution)/shard_map/convert.7
  18.5 1.8 reduce_sum.66
  21.3 1.4 fusion.18
  22.7 7.0 %collective-permute-done.3 = bf16[1024,256]{1,0:T(8,128)(2,1)} collective-permute-done((bf16[1024,256]{1,0:T(8,128)(2,1)}, bf16[1024,256]{1,0:T(8,128)(2,1)}, u32[]{:S(2)}, u32[]{:S(2)}) %collective-permute-start.3) | collective-permute-done | bytes 524320 | tf_op jit(solution)/shard_map/ppermute | solution.py:116
  29.7 1.4 fusion.35
  31.2 1.3 fusion.36
  32.5 1.3 convolution_add_fusion.1
  33.9 1.5 fusion.6
  37.9 1.5 broadcast_in_dim.8
  39.4 15.9 %all-to-all-start = ((bf16[8,512,256]{2,1,0:T(8,128)(2,1)}), bf16[8,512,256]{2,1,0:T(8,128)(2,1)S(1)}, u32[]{:S(2)}, u32[]{:S(2)}) async-start(bf16[8,512,256]{2,1,0:T(8,128)(2,1)} %broadcast_in_dim.8), calls=%async_computation | async-start | bytes 4194304 | tf_op jit(solution)/shard_map/all_to_all | solution.py:122
  59.8 24.3 %all-to-all-done = bf16[8,512,256]{2,1,0:T(8,128)(2,1)S(1)} async-done(((bf16[8,512,256]{2,1,0:T(8,128)(2,1)}), bf16[8,512,256]{2,1,0:T(8,128)(2,1)S(1)}, u32[]{:S(2)}, u32[]{:S(2)}) %all-to-all-start) | async-done | bytes 2097184 | tf_op jit(solution)/shard_map/all_to_all | solution.py:122
  84.0 1.8 convolution_convert_fusion
  85.8 2.8 %fusion.51 = (bf16[4096,256]{1,0:T(8,128)(2,1)}, bf16[4096,256]{1,0:T(8,128)(2,1)}, bf16[4096,256]{1,0:T(8,128)(2,1)}) fusion(bf16[4096,768]{1,0:T(8,128)(2,1)S(1)} %convolution_convert_fusion), kind=kLoop, calls=%fused_computation.82 | loop fusion | bytes 12582912 | tf_op jit(solution)/shard_map/slice | solution.py:219
  88.6 10.6 %shard_map.171 = (bf16[512,256]{1,0:T(8,128)(2,1)}, f32[512,256]{1,0:T(8,128)}, bf16[512,256]{1,0:T(8,128)(2,1)}, bf16[8,512,256]{2,1,0:T(8,128)(2,1)}) custom-call(bf16[512,256]{1,0:T(8,128)(2,1)} %get-tuple-element.31.q_ref, bf16[4096,256]{1,0:T(8,128)(2,1)} %get-tuple-element.23.k_ref, bf16[4096,256]{1,0:T(8,128)(2,1)} %get-tuple-element.22.v_ref, ...), custom_call_target="tpu_custom_call" | custom-call | tf_op jit(solution)/shard_map/pallas_call | solution.py:99
  99.2 3.9 %all-to-all-start.1 = ((bf16[8,512,256]{2,1,0:T(8,128)(2,1)}), bf16[8,512,256]{2,1,0:T(8,128)(2,1)S(1)}, u32[]{:S(2)}, u32[]{:S(2)}) async-start(bf16[8,512,256]{2,1,0:T(8,128)(2,1)} %get-tuple-element.14), calls=%async_computation.1 | async-start | bytes 4194304 | tf_op jit(solution)/shard_map/all_to_all | solution.py:240
  103.2 1.7 slice_bitcast_fusion.10.g_ref
  104.9 11.6 %shard_map.172 = bf16[512,256]{1,0:T(8,128)(2,1)} custom-call(bf16[512,256]{1,0:T(8,128)(2,1)} %get-tuple-element.31.q_ref, bf16[512,256]{1,0:T(8,128)(2,1)} %slice_bitcast_fusion.10.g_ref, bf16[4096,256]{1,0:T(8,128)(2,1)} %get-tuple-element.23.k_ref, bf16[4096,256]{1,0:T(8,128)(2,1)} %get-tuple-element.22.v_ref), custom_call_target="tpu_custom_call" | custom-call | tf_op jit(solution)/shard_map/pallas_call | solution.py:104
  118.5 1.9 fusion.59
  121.3 9.4 %all-to-all-done.1 = bf16[8,512,256]{2,1,0:T(8,128)(2,1)S(1)} async-done(((bf16[8,512,256]{2,1,0:T(8,128)(2,1)}), bf16[8,512,256]{2,1,0:T(8,128)(2,1)S(1)}, u32[]{:S(2)}, u32[]{:S(2)}) %all-to-all-start.1) | async-done | bytes 2097184 | tf_op jit(solution)/shard_map/all_to_all | solution.py:240
  130.7 1.3 copy-done.4
  132.0 14.1 %shard_map.173 = (bf16[512,256]{1,0:T(8,128)(2,1)}, bf16[512,256]{1,0:T(8,128)(2,1)}) custom-call(bf16[4096,256]{1,0:T(8,128)(2,1)} %get-tuple-element.21.q_ref, bf16[4096,256]{1,0:T(8,128)(2,1)} %bitcast.113, bf16[512,256]{1,0:T(8,128)(2,1)} %get-tuple-element.30.k_ref, bf16[512,256]{1,0:T(8,128)(2,1)} %get-tuple-element.29.v_ref), custom_call_target="tpu_custom_call" | custom-call | tf_op jit(solution)/shard_map/pallas_call | solution.py:109
  146.2 2.0 fusion.58
  148.2 1.9 fusion.57
  150.1 1.4 convolution_add_fusion.3
  153.2 3.5 %fusion.8 = f32[256,256]{1,0:T(8,128)} fusion(bf16[1024,256]{1,0:T(8,128)(2,1)} %bitcast.117, f32[1024,256]{1,0:T(8,128)} %copy-done.15, f32[1024]{0:T(1024)S(1)} %fusion.46, s32[1,1,512,1024]{3,2,1,0:T(8,128)S(1)} %copy-done.11, f32[512,256]{1,0:T(8,128)} %get-tuple-element.35, f32[256,512]{0,1:T(8,128)S(1)} %copy-done.9, f32[512]{0:T(512)} %copy-done.29, ...), kind=kOutput, calls=%fused_computation.15 | convolution fusion | flops 406585344 | bytes 4990976 | tf_op jit(solution)/shard_map/gh,ge->he/dot_general | solution.py:257
  156.8 2.2 %concatenate.7 = f32[1344,256]{1,0:T(8,128)S(1)} concatenate(f32[256,256]{1,0:T(8,128)} %fusion.8, f32[256,256]{1,0:T(8,128)S(1)} %fusion.56, f32[256,256]{1,0:T(8,128)} %fusion.57, f32[256,256]{1,0:T(8,128)S(1)} %copy-done.13, f32[256,256]{1,0:T(8,128)S(1)} %copy-done.12, f32[1,256]{1,0:T(1,128)S(1)} %bitcast.121, f32[63,256]{1,0:T(8,128)S(1)} %broadcast_in_dim.10), dimensions={0} | concatenate | bytes 2752512 | tf_op jit(solution)/shard_map/concatenate | solution.py:264
  159.2 27.4 %all_to_all.20 = f32[128,21,128]{2,1,0:T(8,128)S(1)} all-to-all(f32[128,21,128]{2,1,0:T(8,128)S(1)} %reshape.145), channel_id=1, replica_groups=mesh['row'=16,'col'=8] {'row','col'}, dimensions={0} | all-to-all | bytes 2752512 | tf_op jit(solution)/shard_map/all_to_all | solution.py:131
  187.7 5.4 %all-to-all-start.3 = ((bf16[128,21,128]{2,1,0:T(8,128)(2,1)}), bf16[128,21,128]{2,1,0:T(8,128)(2,1)S(1)}, u32[]{:S(2)}, u32[]{:S(2)}) async-start(bf16[128,21,128]{2,1,0:T(8,128)(2,1)} %broadcast_in_dim.11), calls=%async_computation.3 | async-start | bytes 1572864 | tf_op jit(solution)/shard_map/all_to_all | solution.py:134
  193.7 15.0 %all-to-all-done.3 = bf16[128,21,128]{2,1,0:T(8,128)(2,1)S(1)} async-done(((bf16[128,21,128]{2,1,0:T(8,128)(2,1)}), bf16[128,21,128]{2,1,0:T(8,128)(2,1)S(1)}, u32[]{:S(2)}, u32[]{:S(2)}) %all-to-all-start.3) | async-done | bytes 688160 | tf_op jit(solution)/shard_map/all_to_all | solution.py:134
  (102 shorter events, 18.2 us)
Async XLA Ops:
  0.6 34.8 %copy-start = (bf16[256,256]{1,0:T(8,128)(2,1)S(1)}, bf16[256,256]{1,0:T(8,128)(2,1)}, u32[]{:S(2)}) copy-start(bf16[256,256]{1,0:T(8,128)(2,1)} %param.17) | copy-start | bytes 393220
  3.4 17.6 %copy-start.3 = (s32[1,1,8,5,128,128]{5,4,3,2,1,0:T(8,128)S(1)}, s32[1,1,8,5,128,128]{5,4,3,2,1,0:T(8,128)}, u32[]{:S(2)}) copy-start(s32[1,1,8,5,128,128]{5,4,3,2,1,0:T(8,128)} %param.13) | copy-start | bytes 7864324
  3.4 29.1 %collective-permute-start = (bf16[1024,256]{1,0:T(8,128)(2,1)}, bf16[1024,256]{1,0:T(8,128)(2,1)}, u32[]{:S(2)}, u32[]{:S(2)}) collective-permute-start(bf16[1024,256]{1,0:T(8,128)(2,1)} %fusion.13), channel_id=1, source_target_pairs={{0,8},{8,16},{16,24},{24,32},{32,40},{40,48},{48,56},{56,64},{64,7... | collective-permute-start | bytes 1572872 | tf_op jit(solution)/shard_map/ppermute | solution.py:116
  5.7 24.0 %collective-permute-start.3 = (bf16[1024,256]{1,0:T(8,128)(2,1)}, bf16[1024,256]{1,0:T(8,128)(2,1)}, u32[]{:S(2)}, u32[]{:S(2)}) collective-permute-start(bf16[1024,256]{1,0:T(8,128)(2,1)} %fusion.13), channel_id=1, source_target_pairs={{1,0},{2,1},{3,2},{4,3},{5,4},{6,5},{7,6},{9,8},{10,9},{11,10},{12... | collective-permute-start | bytes 1572872 | tf_op jit(solution)/shard_map/ppermute | solution.py:116
  7.0 24.1 %collective-permute-start.2 = (bf16[1024,256]{1,0:T(8,128)(2,1)}, bf16[1024,256]{1,0:T(8,128)(2,1)}, u32[]{:S(2)}, u32[]{:S(2)}) collective-permute-start(bf16[1024,256]{1,0:T(8,128)(2,1)} %fusion.13), channel_id=1, source_target_pairs={{0,1},{1,2},{2,3},{3,4},{4,5},{5,6},{6,7},{8,9},{9,10},{10,11},{11... | collective-permute-start | bytes 1572872 | tf_op jit(solution)/shard_map/ppermute | solution.py:116
  14.1 19.7 %collective-permute-start.1 = (bf16[1024,256]{1,0:T(8,128)(2,1)}, bf16[1024,256]{1,0:T(8,128)(2,1)}, u32[]{:S(2)}, u32[]{:S(2)}) collective-permute-start(bf16[1024,256]{1,0:T(8,128)(2,1)} %fusion.13), channel_id=1, source_target_pairs={{8,0},{16,8},{24,16},{32,24},{40,32},{48,40},{56,48},{64,56},{72,6... | collective-permute-start | bytes 1572872 | tf_op jit(solution)/shard_map/ppermute | solution.py:116
  20.3 15.4 %copy-start.29 = (f32[512]{0:T(512)}, f32[512]{0:T(512)S(1)}, u32[]{:S(2)}) copy-start(f32[512]{0:T(512)S(1)} %convert_add_fusion.1) | copy-start | bytes 6148
  21.2 9.9 %copy-start.5 = (bf16[8,5,128,128]{3,2,0,1:T(8,128)(2,1)S(1)}, bf16[8,5,128,128]{3,2,0,1:T(8,128)(2,1)}, u32[]{:S(2)}) copy-start(bf16[8,5,128,128]{3,2,0,1:T(8,128)(2,1)} %fusion.5) | copy-start | bytes 3932164
  37.8 20.6 %copy-start.1 = (bf16[512,256]{1,0:T(8,128)(2,1)}, bf16[512,256]{1,0:T(8,128)(2,1)S(1)}, u32[]{:S(2)}) copy-start(bf16[512,256]{1,0:T(8,128)(2,1)S(1)} %fusion.19.tok_ref) | copy-start | bytes 786436
  39.3 16.0 %copy-start.24 = (f32[1,1,512]{2,1,0:T(1,128)S(1)}, f32[1,1,512]{2,1,0:T(1,128)}, u32[]{:S(2)}) copy-start(f32[1,1,512]{2,1,0:T(1,128)} %param.23) | copy-start | bytes 6148
  39.3 16.1 %copy-start.16 = (bf16[256,256]{1,0:T(8,128)(2,1)S(1)}, bf16[256,256]{1,0:T(8,128)(2,1)}, u32[]{:S(2)}) copy-start(bf16[256,256]{1,0:T(8,128)(2,1)} %wo_ref.1) | copy-start | bytes 393220
  39.3 16.9 %copy-start.30 = (bf16[256]{0:T(256)(128)(2,1)S(1)}, bf16[256]{0:T(256)(128)(2,1)}, u32[]{:S(2)}) copy-start(bf16[256]{0:T(256)(128)(2,1)} %param.22) | copy-start | bytes 1540
  39.3 17.4 %copy-start.21 = (bf16[256,256]{1,0:T(8,128)(2,1)S(1)}, bf16[256,256]{1,0:T(8,128)(2,1)}, u32[]{:S(2)}) copy-start(bf16[256,256]{1,0:T(8,128)(2,1)} %param.18) | copy-start | bytes 393220
  39.3 18.4 %copy-start.17 = (bf16[256,256]{1,0:T(8,128)(2,1)S(1)}, bf16[256,256]{1,0:T(8,128)(2,1)}, u32[]{:S(2)}) copy-start(bf16[256,256]{1,0:T(8,128)(2,1)} %param.20) | copy-start | bytes 393220
  39.4 44.7 %all-to-all-start = ((bf16[8,512,256]{2,1,0:T(8,128)(2,1)}), bf16[8,512,256]{2,1,0:T(8,128)(2,1)S(1)}, u32[]{:S(2)}, u32[]{:S(2)}) async-start(bf16[8,512,256]{2,1,0:T(8,128)(2,1)} %broadcast_in_dim.8), calls=%async_computation | async-start | bytes 4194304 | tf_op jit(solution)/shard_map/all_to_all | solution.py:122
  99.2 3.9 %copy-start.31 = (bf16[256]{0:T(256)(128)(2,1)S(1)}, bf16[256]{0:T(256)(128)(2,1)}, u32[]{:S(2)}) copy-start(bf16[256]{0:T(256)(128)(2,1)} %param.22) | copy-start | bytes 1540
  99.2 4.0 %copy-start.25 = (f32[1,1,512]{2,1,0:T(1,128)S(1)}, f32[1,1,512]{2,1,0:T(1,128)}, u32[]{:S(2)}) copy-start(f32[1,1,512]{2,1,0:T(1,128)} %param.23) | copy-start | bytes 6148
  99.2 31.5 %all-to-all-start.1 = ((bf16[8,512,256]{2,1,0:T(8,128)(2,1)}), bf16[8,512,256]{2,1,0:T(8,128)(2,1)S(1)}, u32[]{:S(2)}, u32[]{:S(2)}) async-start(bf16[8,512,256]{2,1,0:T(8,128)(2,1)} %get-tuple-element.14), calls=%async_computation.1 | async-start | bytes 4194304 | tf_op jit(solution)/shard_map/all_to_all | solution.py:240
  103.2 13.3 %copy-start.28 = (f32[256]{0:T(256)}, f32[256]{0:T(256)S(1)}, u32[]{:S(2)}) copy-start(f32[256]{0:T(256)S(1)} %convert_element_type.135) | copy-start | bytes 3076
  104.9 11.6 %copy-start.20 = (f32[512,256]{1,0:T(8,128)S(1)}, f32[512,256]{1,0:T(8,128)}, u32[]{:S(2)}) copy-start(f32[512,256]{1,0:T(8,128)} %get-tuple-element.13) | copy-start | bytes 1572868
  104.9 12.4 %copy-start.2 = (bf16[512,256]{1,0:T(8,128)(2,1)S(1)}, bf16[512,256]{1,0:T(8,128)(2,1)}, u32[]{:S(2)}) copy-start(bf16[512,256]{1,0:T(8,128)(2,1)} %copy-done.1) | copy-start | bytes 786436
  104.9 13.6 %copy-start.23 = (bf16[512,256]{1,0:T(8,128)(2,1)S(1)}, bf16[512,256]{1,0:T(8,128)(2,1)}, u32[]{:S(2)}) copy-start(bf16[512,256]{1,0:T(8,128)(2,1)} %get-tuple-element.17) | copy-start | bytes 786436
  116.4 4.0 %copy-start.6 = (bf16[512,256]{1,0:T(8,128)(2,1)S(1)}, bf16[512,256]{1,0:T(8,128)(2,1)}, u32[]{:S(2)}) copy-start(bf16[512,256]{1,0:T(8,128)(2,1)} %shard_map.172) | copy-start | bytes 786436
  116.4 4.0 %copy-start.22 = (bf16[256,256]{1,0:T(8,128)(2,1)S(1)}, bf16[256,256]{1,0:T(8,128)(2,1)}, u32[]{:S(2)}) copy-start(bf16[256,256]{1,0:T(8,128)(2,1)} %param.18) | copy-start | bytes 393220
  146.1 5.3 %copy-start.9 = (f32[256,512]{0,1:T(8,128)S(1)}, f32[256,512]{0,1:T(8,128)}, u32[]{:S(2)}) copy-start(f32[256,512]{0,1:T(8,128)} %copy-done.8) | copy-start | bytes 1572868
  146.1 5.3 %copy-start.14 = (bf16[512,256]{1,0:T(8,128)(2,1)S(1)}, bf16[512,256]{1,0:T(8,128)(2,1)}, u32[]{:S(2)}) copy-start(bf16[512,256]{1,0:T(8,128)(2,1)} %get-tuple-element.16) | copy-start | bytes 786436
  146.1 5.3 %copy-start.18 = (bf16[256,256]{1,0:T(8,128)(2,1)S(1)}, bf16[256,256]{1,0:T(8,128)(2,1)}, u32[]{:S(2)}) copy-start(bf16[256,256]{1,0:T(8,128)(2,1)} %param.20) | copy-start | bytes 393220
  153.2 3.6 %copy-start.12 = (f32[256,256]{1,0:T(8,128)S(1)}, f32[256,256]{1,0:T(8,128)}, u32[]{:S(2)}) copy-start(f32[256,256]{1,0:T(8,128)} %fusion.59) | copy-start | bytes 786436
  153.2 3.6 %copy-start.13 = (f32[256,256]{1,0:T(8,128)S(1)}, f32[256,256]{1,0:T(8,128)}, u32[]{:S(2)}) copy-start(f32[256,256]{1,0:T(8,128)} %fusion.58) | copy-start | bytes 786436
  153.2 3.6 %copy-start.27 = (f32[256]{0:T(256)S(1)}, f32[256]{0:T(256)}, u32[]{:S(2)}) copy-start(f32[256]{0:T(256)} %get-tuple-element.19) | copy-start | bytes 3076
  186.5 6.6 %copy-start.26 = (f32[512]{0:T(512)S(1)}, f32[512]{0:T(512)}, u32[]{:S(2)}) copy-start(f32[512]{0:T(512)} %get-tuple-element.20) | copy-start | bytes 6148
  187.7 21.1 %all-to-all-start.3 = ((bf16[128,21,128]{2,1,0:T(8,128)(2,1)}), bf16[128,21,128]{2,1,0:T(8,128)(2,1)S(1)}, u32[]{:S(2)}, u32[]{:S(2)}) async-start(bf16[128,21,128]{2,1,0:T(8,128)(2,1)} %broadcast_in_dim.11), calls=%async_computation.3 | async-start | bytes 1572864 | tf_op jit(solution)/shard_map/all_to_all | solution.py:134
  (7 other events, 12.1 us)

commit v9 on v8

--- a/solution.py
+++ b/solution.py
@@ -64,7 +64,7 @@
             cols = slice(h * HD, (h + 1) * HD)
             k = k_ref[rows, cols]
             t = _half_tanh(q_ref[:, cols], k)
-            dp = _nt(g_ref[:, cols], v_ref[rows, cols])
+            dp = _nt(g_ref[0, :, cols], v_ref[rows, cols])
             ds = (dp * (1.0 - t * t) * (0.25 / math.sqrt(HD))).astype(jnp.bfloat16)
             acc_ref[:, cols] += _nn(ds, k)
         return carry
@@ -235,11 +235,10 @@
     g_score = jnp.sum(mixed * grad_value[:, None], axis=0)
     grad_mixed = grad_value[:, None] * score_w
     g_out = jnp.einsum("nh,ne->he", attended, grad_proj, preferred_element_type=jnp.float32)
-    grad_attn = grad_attn_copies[0]
 
     grad_attn_all = lax.all_to_all(grad_attn_copies, "col", 0, 0, tiled=True).reshape(-1, H)
 
-    grad_query = attend_gq(query_own, grad_attn, key_all, value_all)
+    grad_query = attend_gq(query_own, grad_attn_copies, key_all, value_all)
     grad_key, grad_val = attend_gkv(query_all, grad_attn_all, key_own, value_own)
 
     g_query = jnp.einsum("nh,ne->he", tokens, grad_query, preferred_element_type=jnp.float32)

time: 212 us -> 212 us (level)
  transfers between devices with their start and end apart: 7 -> 7, of which waited for: 4 -> 4; matrix products, arithmetic and copies ran while one was open for 11% -> 10% of each run, Pallas kernels for 5% -> 6%
where the time goes in v9:
time: 212 us; the launch traced here: 211 us
  waiting for transfers between devices  56.8 us (27%)
  starting transfers between devices  37.3 us (18%)
  Pallas kernels  36.8 us (17%)
  blocking collectives  27.4 us (13%)
  matrix products  24.3 us (11%)
  local copies, waits for them, and re-layouts  15.4 us (7%)
  other arithmetic  10.3 us (5%)
  between operations  2.46 us (1%)
    all_to_all x1, blocking collectives, all_reduce_a2a(): chunks = lax.all_to_all(rows_in, axes, 0, 0, tiled=True)  27.4 us
    all_to_all x1, waiting for transfers between devices, gather_tiles(): return lax.all_to_all(copies, axis, 0, 0, tiled=True)  24.3 us
    all_to_all x1, starting transfers between devices, gather_tiles(): return lax.all_to_all(copies, axis, 0, 0, tiled=True)  15.9 us
    all_to_all x1, waiting for transfers between devices, all_reduce_a2a(): return lax.all_to_all(copies, axes, 0, 0, tiled=True).astype(jnp.float32)  15 us
    pallas_call x1, Pallas kernels, attend_gkv(): pl.pallas_call(_gkv_kernel, out_shape=(sh, sh), scratch_shapes=[pltpu.VME...  14.1 us
    pallas_call x1, Pallas kernels, attend_gq(): pl.pallas_call(_gq_kernel, out_shape=jax.ShapeDtypeStruct(q.shape, jnp.bf...  12.1 us
    ppermute x4, starting transfers between devices, from_neighbour(): return lax.ppermute(array, axis, pairs)  12 us
    pallas_call x1, Pallas kernels, attend_fwd(): pl.pallas_call(_fwd_kernel, out_shape=outs, scratch_shapes=[pltpu.VMEM(q....  10.6 us
  transfers between devices with their start and end apart: 7, of which 4 were waited for; matrix products, arithmetic and copies ran while one was open for 10% of the time, Pallas kernels for 6%

profile of v9, /device:TPU:0, one launch (start us, length us, event | category | flops | bytes accessed | tf_op | source)
XLA Modules:
  0.0 210.7 jit_solution(9434457265878428722)
XLA Ops:
  1.3 2.1 fusion.13
  3.4 2.4 %collective-permute-start = (bf16[1024,256]{1,0:T(8,128)(2,1)}, bf16[1024,256]{1,0:T(8,128)(2,1)}, u32[]{:S(2)}, u32[]{:S(2)}) collective-permute-start(bf16[1024,256]{1,0:T(8,128)(2,1)} %fusion.13), channel_id=1, source_target_pairs={{0,8},{8,16},{16,24},{24,32},{32,40},{40,48},{48,56},{56,64},{64,7... | collective-permute-start | bytes 1572872 | tf_op jit(solution)/shard_map/ppermute | solution.py:116
  5.7 1.3 collective-permute-start.3
  7.0 7.1 %collective-permute-start.2 = (bf16[1024,256]{1,0:T(8,128)(2,1)}, bf16[1024,256]{1,0:T(8,128)(2,1)}, u32[]{:S(2)}, u32[]{:S(2)}) collective-permute-start(bf16[1024,256]{1,0:T(8,128)(2,1)} %fusion.13), channel_id=1, source_target_pairs={{0,1},{1,2},{2,3},{3,4},{4,5},{5,6},{6,7},{8,9},{9,10},{10,11},{11... | collective-permute-start | bytes 1572872 | tf_op jit(solution)/shard_map/ppermute | solution.py:116
  15.4 3.1 %fusion.5 = bf16[8,5,128,128]{3,2,0,1:T(8,128)(2,1)} fusion(s32[1,1,8,5,128,128]{5,4,3,2,1,0:T(8,128)} %param.13), kind=kLoop, calls=%fused_computation.11 | loop fusion | flops 655360 | bytes 3932160 | tf_op jit(solution)/shard_map/convert.7
  18.5 1.8 reduce_sum.66
  21.3 1.4 fusion.18
  22.7 7.0 %collective-permute-done.3 = bf16[1024,256]{1,0:T(8,128)(2,1)} collective-permute-done((bf16[1024,256]{1,0:T(8,128)(2,1)}, bf16[1024,256]{1,0:T(8,128)(2,1)}, u32[]{:S(2)}, u32[]{:S(2)}) %collective-permute-start.3) | collective-permute-done | bytes 524320 | tf_op jit(solution)/shard_map/ppermute | solution.py:116
  29.7 1.4 fusion.35
  31.2 1.3 fusion.36
  32.5 1.3 convolution_add_fusion.1
  33.9 1.5 fusion.6
  37.9 1.5 broadcast_in_dim.8
  39.4 15.9 %all-to-all-start = ((bf16[8,512,256]{2,1,0:T(8,128)(2,1)}), bf16[8,512,256]{2,1,0:T(8,128)(2,1)S(1)}, u32[]{:S(2)}, u32[]{:S(2)}) async-start(bf16[8,512,256]{2,1,0:T(8,128)(2,1)} %broadcast_in_dim.8), calls=%async_computation | async-start | bytes 4194304 | tf_op jit(solution)/shard_map/all_to_all | solution.py:122
  59.8 24.3 %all-to-all-done = bf16[8,512,256]{2,1,0:T(8,128)(2,1)S(1)} async-done(((bf16[8,512,256]{2,1,0:T(8,128)(2,1)}), bf16[8,512,256]{2,1,0:T(8,128)(2,1)S(1)}, u32[]{:S(2)}, u32[]{:S(2)}) %all-to-all-start) | async-done | bytes 2097184 | tf_op jit(solution)/shard_map/all_to_all | solution.py:122
  84.0 1.8 convolution_convert_fusion
  85.8 2.8 %fusion.51 = (bf16[4096,256]{1,0:T(8,128)(2,1)}, bf16[4096,256]{1,0:T(8,128)(2,1)}, bf16[4096,256]{1,0:T(8,128)(2,1)}) fusion(bf16[4096,768]{1,0:T(8,128)(2,1)S(1)} %convolution_convert_fusion), kind=kLoop, calls=%fused_computation.81 | loop fusion | bytes 12582912 | tf_op jit(solution)/shard_map/slice | solution.py:219
  88.6 10.6 %shard_map.171 = (bf16[512,256]{1,0:T(8,128)(2,1)}, f32[512,256]{1,0:T(8,128)}, bf16[512,256]{1,0:T(8,128)(2,1)}, bf16[8,512,256]{2,1,0:T(8,128)(2,1)}) custom-call(bf16[512,256]{1,0:T(8,128)(2,1)} %get-tuple-element.31.q_ref, bf16[4096,256]{1,0:T(8,128)(2,1)} %get-tuple-element.23.k_ref, bf16[4096,256]{1,0:T(8,128)(2,1)} %get-tuple-element.22.v_ref, ...), custom_call_target="tpu_custom_call" | custom-call | tf_op jit(solution)/shard_map/pallas_call | solution.py:99
  99.2 3.9 %all-to-all-start.1 = ((bf16[8,512,256]{2,1,0:T(8,128)(2,1)}), bf16[8,512,256]{2,1,0:T(8,128)(2,1)S(1)}, u32[]{:S(2)}, u32[]{:S(2)}) async-start(bf16[8,512,256]{2,1,0:T(8,128)(2,1)} %get-tuple-element.14.g_ref), calls=%async_computation.1 | async-start | bytes 4194304 | tf_op jit(solution)/shard_map/all_to_all | solution.py:239
  103.2 12.1 %shard_map.172 = bf16[512,256]{1,0:T(8,128)(2,1)} custom-call(bf16[512,256]{1,0:T(8,128)(2,1)} %get-tuple-element.31.q_ref, bf16[8,512,256]{2,1,0:T(8,128)(2,1)} %get-tuple-element.14.g_ref, bf16[4096,256]{1,0:T(8,128)(2,1)} %get-tuple-element.23.k_ref, bf16[4096,256]{1,0:T(8,128)(2,1)} %get-tuple-element.22.v_ref), custom_call_target="tpu_custom_call" | custom-call | tf_op jit(solution)/shard_map/pallas_call | solution.py:104
  117.4 1.9 fusion.59
  120.3 10.4 %all-to-all-done.1 = bf16[8,512,256]{2,1,0:T(8,128)(2,1)S(1)} async-done(((bf16[8,512,256]{2,1,0:T(8,128)(2,1)}), bf16[8,512,256]{2,1,0:T(8,128)(2,1)S(1)}, u32[]{:S(2)}, u32[]{:S(2)}) %all-to-all-start.1) | async-done | bytes 2097184 | tf_op jit(solution)/shard_map/all_to_all | solution.py:239
  130.7 1.3 copy-done.4
  132.0 14.1 %shard_map.173 = (bf16[512,256]{1,0:T(8,128)(2,1)}, bf16[512,256]{1,0:T(8,128)(2,1)}) custom-call(bf16[4096,256]{1,0:T(8,128)(2,1)} %get-tuple-element.21.q_ref, bf16[4096,256]{1,0:T(8,128)(2,1)} %bitcast.111, bf16[512,256]{1,0:T(8,128)(2,1)} %get-tuple-element.30.k_ref, bf16[512,256]{1,0:T(8,128)(2,1)} %get-tuple-element.29.v_ref), custom_call_target="tpu_custom_call" | custom-call | tf_op jit(solution)/shard_map/pallas_call | solution.py:109
  146.2 2.0 fusion.58
  148.2 1.9 fusion.57
  150.1 1.4 convolution_add_fusion.3
  153.2 3.5 %fusion.8 = f32[256,256]{1,0:T(8,128)} fusion(bf16[1024,256]{1,0:T(8,128)(2,1)} %bitcast.115, f32[1024,256]{1,0:T(8,128)} %copy-done.15, f32[1024]{0:T(1024)S(1)} %fusion.46, s32[1,1,512,1024]{3,2,1,0:T(8,128)S(1)} %copy-done.11, f32[512,256]{1,0:T(8,128)} %get-tuple-element.35, f32[256,512]{0,1:T(8,128)S(1)} %copy-done.9, f32[512]{0:T(512)} %copy-done.29, ...), kind=kOutput, calls=%fused_computation.15 | convolution fusion | flops 406585344 | bytes 4990976 | tf_op jit(solution)/shard_map/gh,ge->he/dot_general | solution.py:256
  156.8 2.2 %concatenate.7 = f32[1344,256]{1,0:T(8,128)S(1)} concatenate(f32[256,256]{1,0:T(8,128)} %fusion.8, f32[256,256]{1,0:T(8,128)S(1)} %fusion.56, f32[256,256]{1,0:T(8,128)} %fusion.57, f32[256,256]{1,0:T(8,128)S(1)} %copy-done.13, f32[256,256]{1,0:T(8,128)S(1)} %copy-done.12, f32[1,256]{1,0:T(1,128)S(1)} %bitcast.119, f32[63,256]{1,0:T(8,128)S(1)} %broadcast_in_dim.10), dimensions={0} | concatenate | bytes 2752512 | tf_op jit(solution)/shard_map/concatenate | solution.py:263
  159.2 27.4 %all_to_all.20 = f32[128,21,128]{2,1,0:T(8,128)S(1)} all-to-all(f32[128,21,128]{2,1,0:T(8,128)S(1)} %reshape.145), channel_id=1, replica_groups=mesh['row'=16,'col'=8] {'row','col'}, dimensions={0} | all-to-all | bytes 2752512 | tf_op jit(solution)/shard_map/all_to_all | solution.py:131
  187.7 5.4 %all-to-all-start.3 = ((bf16[128,21,128]{2,1,0:T(8,128)(2,1)}), bf16[128,21,128]{2,1,0:T(8,128)(2,1)S(1)}, u32[]{:S(2)}, u32[]{:S(2)}) async-start(bf16[128,21,128]{2,1,0:T(8,128)(2,1)} %broadcast_in_dim.11), calls=%async_computation.3 | async-start | bytes 1572864 | tf_op jit(solution)/shard_map/all_to_all | solution.py:134
  193.7 15.0 %all-to-all-done.3 = bf16[128,21,128]{2,1,0:T(8,128)(2,1)S(1)} async-done(((bf16[128,21,128]{2,1,0:T(8,128)(2,1)}), bf16[128,21,128]{2,1,0:T(8,128)(2,1)S(1)}, u32[]{:S(2)}, u32[]{:S(2)}) %all-to-all-start.3) | async-done | bytes 688160 | tf_op jit(solution)/shard_map/all_to_all | solution.py:134
  (101 shorter events, 16.9 us)
Async XLA Ops:
  0.6 34.8 %copy-start = (bf16[256,256]{1,0:T(8,128)(2,1)S(1)}, bf16[256,256]{1,0:T(8,128)(2,1)}, u32[]{:S(2)}) copy-start(bf16[256,256]{1,0:T(8,128)(2,1)} %param.17) | copy-start | bytes 393220
  3.4 17.6 %copy-start.3 = (s32[1,1,8,5,128,128]{5,4,3,2,1,0:T(8,128)S(1)}, s32[1,1,8,5,128,128]{5,4,3,2,1,0:T(8,128)}, u32[]{:S(2)}) copy-start(s32[1,1,8,5,128,128]{5,4,3,2,1,0:T(8,128)} %param.13) | copy-start | bytes 7864324
  3.4 29.1 %collective-permute-start = (bf16[1024,256]{1,0:T(8,128)(2,1)}, bf16[1024,256]{1,0:T(8,128)(2,1)}, u32[]{:S(2)}, u32[]{:S(2)}) collective-permute-start(bf16[1024,256]{1,0:T(8,128)(2,1)} %fusion.13), channel_id=1, source_target_pairs={{0,8},{8,16},{16,24},{24,32},{32,40},{40,48},{48,56},{56,64},{64,7... | collective-permute-start | bytes 1572872 | tf_op jit(solution)/shard_map/ppermute | solution.py:116
  5.7 24.0 %collective-permute-start.3 = (bf16[1024,256]{1,0:T(8,128)(2,1)}, bf16[1024,256]{1,0:T(8,128)(2,1)}, u32[]{:S(2)}, u32[]{:S(2)}) collective-permute-start(bf16[1024,256]{1,0:T(8,128)(2,1)} %fusion.13), channel_id=1, source_target_pairs={{1,0},{2,1},{3,2},{4,3},{5,4},{6,5},{7,6},{9,8},{10,9},{11,10},{12... | collective-permute-start | bytes 1572872 | tf_op jit(solution)/shard_map/ppermute | solution.py:116
  7.0 24.1 %collective-permute-start.2 = (bf16[1024,256]{1,0:T(8,128)(2,1)}, bf16[1024,256]{1,0:T(8,128)(2,1)}, u32[]{:S(2)}, u32[]{:S(2)}) collective-permute-start(bf16[1024,256]{1,0:T(8,128)(2,1)} %fusion.13), channel_id=1, source_target_pairs={{0,1},{1,2},{2,3},{3,4},{4,5},{5,6},{6,7},{8,9},{9,10},{10,11},{11... | collective-permute-start | bytes 1572872 | tf_op jit(solution)/shard_map/ppermute | solution.py:116
  14.1 19.7 %collective-permute-start.1 = (bf16[1024,256]{1,0:T(8,128)(2,1)}, bf16[1024,256]{1,0:T(8,128)(2,1)}, u32[]{:S(2)}, u32[]{:S(2)}) collective-permute-start(bf16[1024,256]{1,0:T(8,128)(2,1)} %fusion.13), channel_id=1, source_target_pairs={{8,0},{16,8},{24,16},{32,24},{40,32},{48,40},{56,48},{64,56},{72,6... | collective-permute-start | bytes 1572872 | tf_op jit(solution)/shard_map/ppermute | solution.py:116
  20.3 15.4 %copy-start.29 = (f32[512]{0:T(512)}, f32[512]{0:T(512)S(1)}, u32[]{:S(2)}) copy-start(f32[512]{0:T(512)S(1)} %convert_add_fusion.1) | copy-start | bytes 6148
  21.2 9.9 %copy-start.5 = (bf16[8,5,128,128]{3,2,0,1:T(8,128)(2,1)S(1)}, bf16[8,5,128,128]{3,2,0,1:T(8,128)(2,1)}, u32[]{:S(2)}) copy-start(bf16[8,5,128,128]{3,2,0,1:T(8,128)(2,1)} %fusion.5) | copy-start | bytes 3932164
  37.8 20.6 %copy-start.1 = (bf16[512,256]{1,0:T(8,128)(2,1)}, bf16[512,256]{1,0:T(8,128)(2,1)S(1)}, u32[]{:S(2)}) copy-start(bf16[512,256]{1,0:T(8,128)(2,1)S(1)} %fusion.19.tok_ref) | copy-start | bytes 786436
  39.3 16.0 %copy-start.24 = (f32[1,1,512]{2,1,0:T(1,128)S(1)}, f32[1,1,512]{2,1,0:T(1,128)}, u32[]{:S(2)}) copy-start(f32[1,1,512]{2,1,0:T(1,128)} %param.23) | copy-start | bytes 6148
  39.3 16.1 %copy-start.16 = (bf16[256,256]{1,0:T(8,128)(2,1)S(1)}, bf16[256,256]{1,0:T(8,128)(2,1)}, u32[]{:S(2)}) copy-start(bf16[256,256]{1,0:T(8,128)(2,1)} %wo_ref.1) | copy-start | bytes 393220
  39.3 16.9 %copy-start.30 = (bf16[256]{0:T(256)(128)(2,1)S(1)}, bf16[256]{0:T(256)(128)(2,1)}, u32[]{:S(2)}) copy-start(bf16[256]{0:T(256)(128)(2,1)} %param.22) | copy-start | bytes 1540
  39.3 17.4 %copy-start.21 = (bf16[256,256]{1,0:T(8,128)(2,1)S(1)}, bf16[256,256]{1,0:T(8,128)(2,1)}, u32[]{:S(2)}) copy-start(bf16[256,256]{1,0:T(8,128)(2,1)} %param.18) | copy-start | bytes 393220
  39.3 18.4 %copy-start.17 = (bf16[256,256]{1,0:T(8,128)(2,1)S(1)}, bf16[256,256]{1,0:T(8,128)(2,1)}, u32[]{:S(2)}) copy-start(bf16[256,256]{1,0:T(8,128)(2,1)} %param.20) | copy-start | bytes 393220
  39.4 44.7 %all-to-all-start = ((bf16[8,512,256]{2,1,0:T(8,128)(2,1)}), bf16[8,512,256]{2,1,0:T(8,128)(2,1)S(1)}, u32[]{:S(2)}, u32[]{:S(2)}) async-start(bf16[8,512,256]{2,1,0:T(8,128)(2,1)} %broadcast_in_dim.8), calls=%async_computation | async-start | bytes 4194304 | tf_op jit(solution)/shard_map/all_to_all | solution.py:122
  99.2 3.9 %copy-start.31 = (bf16[256]{0:T(256)(128)(2,1)S(1)}, bf16[256]{0:T(256)(128)(2,1)}, u32[]{:S(2)}) copy-start(bf16[256]{0:T(256)(128)(2,1)} %param.22) | copy-start | bytes 1540
  99.2 4.0 %copy-start.25 = (f32[1,1,512]{2,1,0:T(1,128)S(1)}, f32[1,1,512]{2,1,0:T(1,128)}, u32[]{:S(2)}) copy-start(f32[1,1,512]{2,1,0:T(1,128)} %param.23) | copy-start | bytes 6148
  99.2 31.5 %all-to-all-start.1 = ((bf16[8,512,256]{2,1,0:T(8,128)(2,1)}), bf16[8,512,256]{2,1,0:T(8,128)(2,1)S(1)}, u32[]{:S(2)}, u32[]{:S(2)}) async-start(bf16[8,512,256]{2,1,0:T(8,128)(2,1)} %get-tuple-element.14.g_ref), calls=%async_computation.1 | async-start | bytes 4194304 | tf_op jit(solution)/shard_map/all_to_all | solution.py:239
  103.2 12.2 %copy-start.28 = (f32[256]{0:T(256)}, f32[256]{0:T(256)S(1)}, u32[]{:S(2)}) copy-start(f32[256]{0:T(256)S(1)} %convert_element_type.135) | copy-start | bytes 3076
  103.2 12.2 %copy-start.20 = (f32[512,256]{1,0:T(8,128)S(1)}, f32[512,256]{1,0:T(8,128)}, u32[]{:S(2)}) copy-start(f32[512,256]{1,0:T(8,128)} %get-tuple-element.13) | copy-start | bytes 1572868
  103.2 13.0 %copy-start.2 = (bf16[512,256]{1,0:T(8,128)(2,1)S(1)}, bf16[512,256]{1,0:T(8,128)(2,1)}, u32[]{:S(2)}) copy-start(bf16[512,256]{1,0:T(8,128)(2,1)} %copy-done.1) | copy-start | bytes 786436
  103.2 14.2 %copy-start.23 = (bf16[512,256]{1,0:T(8,128)(2,1)S(1)}, bf16[512,256]{1,0:T(8,128)(2,1)}, u32[]{:S(2)}) copy-start(bf16[512,256]{1,0:T(8,128)(2,1)} %get-tuple-element.17) | copy-start | bytes 786436
  115.3 4.0 %copy-start.6 = (bf16[512,256]{1,0:T(8,128)(2,1)S(1)}, bf16[512,256]{1,0:T(8,128)(2,1)}, u32[]{:S(2)}) copy-start(bf16[512,256]{1,0:T(8,128)(2,1)} %shard_map.172) | copy-start | bytes 786436
  115.3 4.0 %copy-start.22 = (bf16[256,256]{1,0:T(8,128)(2,1)S(1)}, bf16[256,256]{1,0:T(8,128)(2,1)}, u32[]{:S(2)}) copy-start(bf16[256,256]{1,0:T(8,128)(2,1)} %param.18) | copy-start | bytes 393220
  146.1 5.3 %copy-start.9 = (f32[256,512]{0,1:T(8,128)S(1)}, f32[256,512]{0,1:T(8,128)}, u32[]{:S(2)}) copy-start(f32[256,512]{0,1:T(8,128)} %copy-done.8) | copy-start | bytes 1572868
  146.1 5.3 %copy-start.14 = (bf16[512,256]{1,0:T(8,128)(2,1)S(1)}, bf16[512,256]{1,0:T(8,128)(2,1)}, u32[]{:S(2)}) copy-start(bf16[512,256]{1,0:T(8,128)(2,1)} %get-tuple-element.16) | copy-start | bytes 786436
  146.1 5.3 %copy-start.18 = (bf16[256,256]{1,0:T(8,128)(2,1)S(1)}, bf16[256,256]{1,0:T(8,128)(2,1)}, u32[]{:S(2)}) copy-start(bf16[256,256]{1,0:T(8,128)(2,1)} %param.20) | copy-start | bytes 393220
  153.2 3.6 %copy-start.12 = (f32[256,256]{1,0:T(8,128)S(1)}, f32[256,256]{1,0:T(8,128)}, u32[]{:S(2)}) copy-start(f32[256,256]{1,0:T(8,128)} %fusion.59) | copy-start | bytes 786436
  153.2 3.6 %copy-start.13 = (f32[256,256]{1,0:T(8,128)S(1)}, f32[256,256]{1,0:T(8,128)}, u32[]{:S(2)}) copy-start(f32[256,256]{1,0:T(8,128)} %fusion.58) | copy-start | bytes 786436
  153.2 3.6 %copy-start.27 = (f32[256]{0:T(256)S(1)}, f32[256]{0:T(256)}, u32[]{:S(2)}) copy-start(f32[256]{0:T(256)} %get-tuple-element.19) | copy-start | bytes 3076
  186.5 6.6 %copy-start.26 = (f32[512]{0:T(512)S(1)}, f32[512]{0:T(512)}, u32[]{:S(2)}) copy-start(f32[512]{0:T(512)} %get-tuple-element.20) | copy-start | bytes 6148
  187.7 21.1 %all-to-all-start.3 = ((bf16[128,21,128]{2,1,0:T(8,128)(2,1)}), bf16[128,21,128]{2,1,0:T(8,128)(2,1)S(1)}, u32[]{:S(2)}, u32[]{:S(2)}) async-start(bf16[128,21,128]{2,1,0:T(8,128)(2,1)} %broadcast_in_dim.11), calls=%async_computation.3 | async-start | bytes 1572864 | tf_op jit(solution)/shard_map/all_to_all | solution.py:134
  (7 other events, 12.1 us)

commit v10 on v9

--- a/solution.py
+++ b/solution.py
@@ -28,17 +28,17 @@
 def _half_tanh(q, k):
     return jnp.tanh(_nt(q, k) * (0.5 / math.sqrt(HD)) - 0.5 * SHIFT)
 
-def _fwd_kernel(q_ref, k_ref, v_ref, tok_ref, gval_ref, sw_ref, wo_ref, wot_ref,
+def _fwd_kernel(q_ref, kv_ref, tok_ref, gval_ref, sw_ref, wo_ref, wot_ref,
                 att_ref, mixed_ref, gproj_ref, gattn_ref, acc_ref):
-    blocks = k_ref.shape[0] // KB
+    blocks = kv_ref.shape[0] // KB
     acc_ref[...] = jnp.zeros_like(acc_ref)
     def step(j, carry):
         rows = pl.ds(pl.multiple_of(j * KB, KB), KB)
         for h in range(HEADS):
             cols = slice(h * HD, (h + 1) * HD)
-            t = _half_tanh(q_ref[:, cols], k_ref[rows, cols])
+            t = _half_tanh(q_ref[:, cols], kv_ref[rows, cols])
             w = (0.5 * t + 0.5).astype(jnp.bfloat16)
-            acc_ref[:, cols] += _nn(w, v_ref[rows, cols])
+            acc_ref[:, cols] += _nn(w, kv_ref[rows, pl.ds(H + h * HD, HD)])
         return carry
     lax.fori_loop(0, blocks, step, 0)
     attended = acc_ref[...].astype(jnp.bfloat16)
@@ -55,16 +55,16 @@
     for c in range(gattn_ref.shape[0]):
         gattn_ref[c] = grad_attn
 
-def _gq_kernel(q_ref, g_ref, k_ref, v_ref, o_ref, acc_ref):
-    blocks = k_ref.shape[0] // KB
+def _gq_kernel(q_ref, g_ref, kv_ref, o_ref, acc_ref):
+    blocks = kv_ref.shape[0] // KB
     acc_ref[...] = jnp.zeros_like(acc_ref)
     def step(j, carry):
         rows = pl.ds(pl.multiple_of(j * KB, KB), KB)
         for h in range(HEADS):
             cols = slice(h * HD, (h + 1) * HD)
-            k = k_ref[rows, cols]
+            k = kv_ref[rows, cols]
             t = _half_tanh(q_ref[:, cols], k)
-            dp = _nt(g_ref[0, :, cols], v_ref[rows, cols])
+            dp = _nt(g_ref[0, :, cols], kv_ref[rows, pl.ds(H + h * HD, HD)])
             ds = (dp * (1.0 - t * t) * (0.25 / math.sqrt(HD))).astype(jnp.bfloat16)
             acc_ref[:, cols] += _nn(ds, k)
         return carry
@@ -92,17 +92,17 @@
     dk_ref[...] = acck_ref[...].astype(dk_ref.dtype)
     dv_ref[...] = accv_ref[...].astype(dv_ref.dtype)
 
-def attend_fwd(q, k_all, v_all, tokens, grad_value, w_score, w_out, copies):
+def attend_fwd(q, kv_all, tokens, grad_value, w_score, w_out, copies):
     bf16, f32 = jnp.bfloat16, jnp.float32
     outs = (jax.ShapeDtypeStruct(q.shape, bf16), jax.ShapeDtypeStruct(q.shape, f32),
             jax.ShapeDtypeStruct(q.shape, bf16), jax.ShapeDtypeStruct((copies,) + q.shape, bf16))
     return pl.pallas_call(_fwd_kernel, out_shape=outs,
         scratch_shapes=[pltpu.VMEM(q.shape, f32)])(
-            q, k_all, v_all, tokens, grad_value, w_score.reshape(1, -1), w_out, w_out.T)
-
-def attend_gq(q, g, k_all, v_all):
+            q, kv_all, tokens, grad_value, w_score.reshape(1, -1), w_out, w_out.T)
+
+def attend_gq(q, g, kv_all):
     return pl.pallas_call(_gq_kernel, out_shape=jax.ShapeDtypeStruct(q.shape, jnp.bfloat16),
-        scratch_shapes=[pltpu.VMEM(q.shape, jnp.float32)])(q, g, k_all, v_all)
+        scratch_shapes=[pltpu.VMEM(q.shape, jnp.float32)])(q, g, kv_all)
 
 def attend_gkv(q_all, g_all, k, v):
     sh = jax.ShapeDtypeStruct(k.shape, jnp.bfloat16)
@@ -214,11 +214,10 @@
     tokens = (token_live * normed).astype(jnp.bfloat16)
 
     tokens_all = gather_tiles(tokens, "col").reshape(-1, H)
-    w_qkv = jnp.concatenate([w_query, w_key, w_value], axis=1)
-    qkv_all = project(tokens_all, w_qkv)
-    query_all = qkv_all[:, :H]
-    key_all = qkv_all[:, H:2 * H]
-    value_all = qkv_all[:, 2 * H:]
+    w_kv = jnp.concatenate([w_key, w_value], axis=1)
+    kv_all = project(tokens_all, w_kv)
+    query_all = project(tokens_all, w_query)
+    w_qkv = jnp.concatenate([w_query, w_kv], axis=1)
     qkv_own = project(tokens, w_qkv)
     query_own = qkv_own[:, :H]
     key_own = qkv_own[:, H:2 * H]
@@ -228,7 +227,7 @@
     loss_weight = 1.0 / math.sqrt(lax.axis_size("row") * lax.axis_size("col") * NT)
     grad_value = token_live[:, 0] * cotangent[0, 0] * loss_weight
     attended, mixed, grad_proj, grad_attn_copies = attend_fwd(
-        query_own, key_all, value_all, tokens, grad_value[:, None], w_score, w_out,
+        query_own, kv_all, tokens, grad_value[:, None], w_score, w_out,
         lax.axis_size("col"),
     )
     value_out = token_live[:, 0] * jnp.sum(mixed * score_w, axis=1)
@@ -238,7 +237,7 @@
 
     grad_attn_all = lax.all_to_all(grad_attn_copies, "col", 0, 0, tiled=True).reshape(-1, H)
 
-    grad_query = attend_gq(query_own, grad_attn_copies, key_all, value_all)
+    grad_query = attend_gq(query_own, grad_attn_copies, kv_all)
     grad_key, grad_val = attend_gkv(query_all, grad_attn_all, key_own, value_own)
 
     g_query = jnp.einsum("nh,ne->he", tokens, grad_query, preferred_element_type=jnp.float32)

time: 212 us -> 201 us (0.948)
  local copies, waits for them, and re-layouts: 15.4 us -> 8.51 us
  other arithmetic: 10.3 us -> 7.92 us
  waiting for transfers between devices: 56.8 us -> 54.5 us
    dot_general x2 -> x3, matrix products: 2.16 us -> 5.61 us  [project(): jnp.dot(rows_in, weight_mat, preferred_element_type=jnp.float32)]
    slice x1 -> x0, local copies, waits for them, and re-layouts: 2.79 us -> none  [body(): query_all = qkv_all[:, :H]]
    unnamed x67 -> x57, local copies, waits for them, and re-layouts: 4.18 us -> 2.05 us
where the time goes in v10:
time: 201 us
  waiting for transfers between devices  54.5 us (27%)
  starting transfers between devices  38.1 us (19%)
  Pallas kernels  36.9 us (18%)
  blocking collectives  28.6 us (14%)
  matrix products  23.5 us (12%)
  local copies, waits for them, and re-layouts  8.51 us (4%)
  other arithmetic  7.92 us (4%)
  between operations  2.65 us (1%)
    all_to_all x1, blocking collectives, all_reduce_a2a(): chunks = lax.all_to_all(rows_in, axes, 0, 0, tiled=True)  28.6 us
    all_to_all x1, waiting for transfers between devices, gather_tiles(): return lax.all_to_all(copies, axis, 0, 0, tiled=True)  24.1 us
    all_to_all x1, starting transfers between devices, gather_tiles(): return lax.all_to_all(copies, axis, 0, 0, tiled=True)  16.7 us
    all_to_all x1, waiting for transfers between devices, all_reduce_a2a(): return lax.all_to_all(copies, axes, 0, 0, tiled=True).astype(jnp.float32)  15 us
    pallas_call x1, Pallas kernels, attend_gkv(): pl.pallas_call(_gkv_kernel, out_shape=(sh, sh), scratch_shapes=[pltpu.VME...  14.1 us
    pallas_call x1, Pallas kernels, attend_gq(): pl.pallas_call(_gq_kernel, out_shape=jax.ShapeDtypeStruct(q.shape, jnp.bf...  12.1 us
    ppermute x4, starting transfers between devices, from_neighbour(): return lax.ppermute(array, axis, pairs)  11.5 us
    pallas_call x1, Pallas kernels, attend_fwd(): pl.pallas_call(_fwd_kernel, out_shape=outs, scratch_shapes=[pltpu.VMEM(q....  10.6 us
  transfers between devices with their start and end apart: 7, of which 4 were waited for; matrix products, arithmetic and copies ran while one was open for 10% of the time, Pallas kernels for 6%

profile of v10, /device:TPU:0, one launch (start us, length us, event | category | flops | bytes accessed | tf_op | source)
XLA Modules:
  0.0 200.7 jit_solution(4153906333826520921)
XLA Ops:
  1.5 2.1 %fusion.13 = bf16[1024,256]{1,0:T(8,128)(2,1)} fusion(f32[1024]{0:T(1024)S(1)} %fusion.54, bf16[1,1,1024,256]{3,2,1,0:T(8,128)(2,1)} %param.12), kind=kLoop, calls=%fused_computation.24 | loop fusion | flops 786432 | bytes 1052672 | tf_op jit(solution)/shard_map/convert_element_type | solution.py:185
  3.5 1.3 collective-permute-start.3
  4.8 6.9 %collective-permute-start.2 = (bf16[1024,256]{1,0:T(8,128)(2,1)}, bf16[1024,256]{1,0:T(8,128)(2,1)}, u32[]{:S(2)}, u32[]{:S(2)}) collective-permute-start(bf16[1024,256]{1,0:T(8,128)(2,1)} %fusion.13), channel_id=1, source_target_pairs={{0,1},{1,2},{2,3},{3,4},{4,5},{5,6},{6,7},{8,9},{9,10},{10,11},{11... | collective-permute-start | bytes 1572872 | tf_op jit(solution)/shard_map/ppermute | solution.py:116
  11.7 2.1 %collective-permute-start = (bf16[1024,256]{1,0:T(8,128)(2,1)}, bf16[1024,256]{1,0:T(8,128)(2,1)}, u32[]{:S(2)}, u32[]{:S(2)}) collective-permute-start(bf16[1024,256]{1,0:T(8,128)(2,1)} %fusion.13), channel_id=1, source_target_pairs={{0,8},{8,16},{16,24},{24,32},{32,40},{40,48},{48,56},{56,64},{64,7... | collective-permute-start | bytes 1572872 | tf_op jit(solution)/shard_map/ppermute | solution.py:116
  13.8 1.3 collective-permute-start.1
  15.1 1.8 reduce_sum.66
  16.9 1.3 fusion.5
  19.2 1.4 fusion.18
  20.7 7.0 %collective-permute-done.3 = bf16[1024,256]{1,0:T(8,128)(2,1)} collective-permute-done((bf16[1024,256]{1,0:T(8,128)(2,1)}, bf16[1024,256]{1,0:T(8,128)(2,1)}, u32[]{:S(2)}, u32[]{:S(2)}) %collective-permute-start.3) | collective-permute-done | bytes 524320 | tf_op jit(solution)/shard_map/ppermute | solution.py:116
  27.7 1.4 fusion.40
  29.1 1.3 fusion.41
  30.4 1.3 convolution_add_fusion.1
  31.8 1.5 fusion.6
  35.8 1.5 broadcast_in_dim.8
  37.3 16.7 %all-to-all-start = ((bf16[8,512,256]{2,1,0:T(8,128)(2,1)}), bf16[8,512,256]{2,1,0:T(8,128)(2,1)S(1)}, u32[]{:S(2)}, u32[]{:S(2)}) async-start(bf16[8,512,256]{2,1,0:T(8,128)(2,1)} %broadcast_in_dim.8), calls=%async_computation | async-start | bytes 4194304 | tf_op jit(solution)/shard_map/all_to_all | solution.py:122
  57.5 24.1 %all-to-all-done = bf16[8,512,256]{2,1,0:T(8,128)(2,1)S(1)} async-done(((bf16[8,512,256]{2,1,0:T(8,128)(2,1)}), bf16[8,512,256]{2,1,0:T(8,128)(2,1)S(1)}, u32[]{:S(2)}, u32[]{:S(2)}) %all-to-all-start) | async-done | bytes 2097184 | tf_op jit(solution)/shard_map/all_to_all | solution.py:122
  81.6 3.2 %convolution_convert_fusion.kv_ref = bf16[4096,512]{1,0:T(8,128)(2,1)} fusion(bf16[4096,256]{1,0:T(8,128)(2,1)S(1)} %bitcast.110, bf16[256,256]{1,0:T(8,128)(2,1)S(1)} %copy-done.12, bf16[256,256]{1,0:T(8,128)(2,1)S(1)} %copy-done.16), kind=kOutput, calls=%fused_computation | convolution fusion | flops 1076363264 | bytes 6553600 | tf_op jit(solution)/shard_map/dot_general | solution.py:166
  84.8 10.6 %shard_map.171 = (bf16[512,256]{1,0:T(8,128)(2,1)}, f32[512,256]{1,0:T(8,128)}, bf16[512,256]{1,0:T(8,128)(2,1)}, bf16[8,512,256]{2,1,0:T(8,128)(2,1)}) custom-call(bf16[512,256]{1,0:T(8,128)(2,1)} %get-tuple-element.28.q_ref, bf16[4096,512]{1,0:T(8,128)(2,1)} %convolution_convert_fusion.kv_ref, bf16[512,256]{1,0:T(8,128)(2,1)} %copy-done.2, ...), custom_call_target="tpu_custom_call" | custom-call | tf_op jit(solution)/shard_map/pallas_call | solution.py:99
  95.4 4.5 %all-to-all-start.1 = ((bf16[8,512,256]{2,1,0:T(8,128)(2,1)}), bf16[8,512,256]{2,1,0:T(8,128)(2,1)}, u32[]{:S(2)}, u32[]{:S(2)}) async-start(bf16[8,512,256]{2,1,0:T(8,128)(2,1)} %get-tuple-element.14.g_ref), calls=%async_computation.1 | async-start | bytes 4194304 | tf_op jit(solution)/shard_map/all_to_all | solution.py:238
  100.0 12.1 %shard_map.172 = bf16[512,256]{1,0:T(8,128)(2,1)} custom-call(bf16[512,256]{1,0:T(8,128)(2,1)} %get-tuple-element.28.q_ref, bf16[8,512,256]{2,1,0:T(8,128)(2,1)} %get-tuple-element.14.g_ref, bf16[4096,512]{1,0:T(8,128)(2,1)} %convolution_convert_fusion.kv_ref), custom_call_target="tpu_custom_call" | custom-call | tf_op jit(solution)/shard_map/pallas_call | solution.py:104
  112.9 1.2 fusion.65
  114.1 1.3 fusion.68
  116.4 2.0 %convolution_convert_fusion.1.q_ref = bf16[4096,256]{1,0:T(8,128)(2,1)} fusion(bf16[4096,256]{1,0:T(8,128)(2,1)S(1)} %bitcast.111, bf16[256,256]{1,0:T(8,128)(2,1)S(1)} %copy-done.15), kind=kOutput, calls=%fused_computation.1 | convolution fusion | flops 537919488 | bytes 4325376 | tf_op jit(solution)/shard_map/dot_general | solution.py:166
  118.4 8.4 %all-to-all-done.1 = bf16[8,512,256]{2,1,0:T(8,128)(2,1)} async-done(((bf16[8,512,256]{2,1,0:T(8,128)(2,1)}), bf16[8,512,256]{2,1,0:T(8,128)(2,1)}, u32[]{:S(2)}, u32[]{:S(2)}) %all-to-all-start.1) | async-done | bytes 2097184 | tf_op jit(solution)/shard_map/all_to_all | solution.py:238
  126.8 14.1 %shard_map.173 = (bf16[512,256]{1,0:T(8,128)(2,1)}, bf16[512,256]{1,0:T(8,128)(2,1)}) custom-call(bf16[4096,256]{1,0:T(8,128)(2,1)} %convolution_convert_fusion.1.q_ref, bf16[4096,256]{1,0:T(8,128)(2,1)} %bitcast.24.g_ref, bf16[512,256]{1,0:T(8,128)(2,1)} %get-tuple-element.27.k_ref, bf16[512,256]{1,0:T(8,128)(2,1)} %get-tuple-element.26.v_ref), custom_call_target="tpu_custom_call" | custom-call | tf_op jit(solution)/shard_map/pallas_call | solution.py:109
  141.0 1.3 fusion.66
  142.3 1.2 convolution_add_fusion.3
  144.2 3.2 %fusion.8 = f32[256,256]{1,0:T(8,128)S(1)} fusion(bf16[1024,256]{1,0:T(8,128)(2,1)} %bitcast.115, f32[1024,256]{1,0:T(8,128)} %copy-done.11, f32[1024]{0:T(1024)S(1)} %fusion.54, s32[1,1,512,1024]{3,2,1,0:T(8,128)} %param.15, f32[512,256]{1,0:T(8,128)S(1)} %get-tuple-element.32, f32[256,512]{0,1:T(8,128)S(1)} %copy-done.8, f32[512]{0:T(512)S(1)} %copy-done.26, ...), kind=kOutput, calls=%fused_computation.16 | convolution fusion | flops 406585344 | bytes 4990976 | tf_op jit(solution)/shard_map/gh,ge->he/dot_general | solution.py:255
  148.0 28.6 %all_to_all.20 = f32[128,21,128]{2,1,0:T(8,128)S(1)} all-to-all(f32[128,21,128]{2,1,0:T(8,128)S(1)} %reshape.145), channel_id=1, replica_groups=mesh['row'=16,'col'=8] {'row','col'}, dimensions={0} | all-to-all | bytes 2752512 | tf_op jit(solution)/shard_map/all_to_all | solution.py:131
  177.7 5.4 %all-to-all-start.3 = ((bf16[128,21,128]{2,1,0:T(8,128)(2,1)}), bf16[128,21,128]{2,1,0:T(8,128)(2,1)S(1)}, u32[]{:S(2)}, u32[]{:S(2)}) async-start(bf16[128,21,128]{2,1,0:T(8,128)(2,1)} %broadcast_in_dim.11), calls=%async_computation.3 | async-start | bytes 1572864 | tf_op jit(solution)/shard_map/all_to_all | solution.py:134
  183.7 15.0 %all-to-all-done.3 = bf16[128,21,128]{2,1,0:T(8,128)(2,1)S(1)} async-done(((bf16[128,21,128]{2,1,0:T(8,128)(2,1)}), bf16[128,21,128]{2,1,0:T(8,128)(2,1)S(1)}, u32[]{:S(2)}, u32[]{:S(2)}) %all-to-all-start.3) | async-done | bytes 688160 | tf_op jit(solution)/shard_map/all_to_all | solution.py:134
  199.0 1.1 fusion.61
  (90 shorter events, 11.8 us)
Async XLA Ops:
  0.6 32.7 %copy-start = (bf16[256,256]{1,0:T(8,128)(2,1)S(1)}, bf16[256,256]{1,0:T(8,128)(2,1)}, u32[]{:S(2)}) copy-start(bf16[256,256]{1,0:T(8,128)(2,1)} %param.17) | copy-start | bytes 393220
  0.6 16.2 %copy-start.1 = (s32[1,1,8,5,128,128]{5,4,3,2,1,0:T(8,128)S(1)}, s32[1,1,8,5,128,128]{5,4,3,2,1,0:T(8,128)}, u32[]{:S(2)}) copy-start(s32[1,1,8,5,128,128]{5,4,3,2,1,0:T(8,128)} %param.13) | copy-start | bytes 7864324
  3.5 24.1 %collective-permute-start.3 = (bf16[1024,256]{1,0:T(8,128)(2,1)}, bf16[1024,256]{1,0:T(8,128)(2,1)}, u32[]{:S(2)}, u32[]{:S(2)}) collective-permute-start(bf16[1024,256]{1,0:T(8,128)(2,1)} %fusion.13), channel_id=1, source_target_pairs={{1,0},{2,1},{3,2},{4,3},{5,4},{6,5},{7,6},{9,8},{10,9},{11,10},{12... | collective-permute-start | bytes 1572872 | tf_op jit(solution)/shard_map/ppermute | solution.py:116
  4.8 24.2 %collective-permute-start.2 = (bf16[1024,256]{1,0:T(8,128)(2,1)}, bf16[1024,256]{1,0:T(8,128)(2,1)}, u32[]{:S(2)}, u32[]{:S(2)}) collective-permute-start(bf16[1024,256]{1,0:T(8,128)(2,1)} %fusion.13), channel_id=1, source_target_pairs={{0,1},{1,2},{2,3},{3,4},{4,5},{5,6},{6,7},{8,9},{9,10},{10,11},{11... | collective-permute-start | bytes 1572872 | tf_op jit(solution)/shard_map/ppermute | solution.py:116
  11.7 18.7 %collective-permute-start = (bf16[1024,256]{1,0:T(8,128)(2,1)}, bf16[1024,256]{1,0:T(8,128)(2,1)}, u32[]{:S(2)}, u32[]{:S(2)}) collective-permute-start(bf16[1024,256]{1,0:T(8,128)(2,1)} %fusion.13), channel_id=1, source_target_pairs={{0,8},{8,16},{16,24},{24,32},{32,40},{40,48},{48,56},{56,64},{64,7... | collective-permute-start | bytes 1572872 | tf_op jit(solution)/shard_map/ppermute | solution.py:116
  13.8 18.0 %collective-permute-start.1 = (bf16[1024,256]{1,0:T(8,128)(2,1)}, bf16[1024,256]{1,0:T(8,128)(2,1)}, u32[]{:S(2)}, u32[]{:S(2)}) collective-permute-start(bf16[1024,256]{1,0:T(8,128)(2,1)} %fusion.13), channel_id=1, source_target_pairs={{8,0},{16,8},{24,16},{32,24},{40,32},{48,40},{56,48},{64,56},{72,6... | collective-permute-start | bytes 1572872 | tf_op jit(solution)/shard_map/ppermute | solution.py:116
  16.8 16.8 %copy-start.25 = (f32[512]{0:T(512)}, f32[512]{0:T(512)S(1)}, u32[]{:S(2)}) copy-start(f32[512]{0:T(512)S(1)} %convert_add_fusion.1) | copy-start | bytes 6148
  19.1 9.9 %copy-start.4 = (bf16[8,5,128,128]{3,2,0,1:T(8,128)(2,1)S(1)}, bf16[8,5,128,128]{3,2,0,1:T(8,128)(2,1)}, u32[]{:S(2)}) copy-start(bf16[8,5,128,128]{3,2,0,1:T(8,128)(2,1)} %fusion.5) | copy-start | bytes 3932164
  31.8 1.9 copy-start.9
  33.3 1.1 copy-start.19
  35.8 20.4 %copy-start.2 = (bf16[512,256]{1,0:T(8,128)(2,1)}, bf16[512,256]{1,0:T(8,128)(2,1)S(1)}, u32[]{:S(2)}) copy-start(bf16[512,256]{1,0:T(8,128)(2,1)S(1)} %fusion.19.tok_ref) | copy-start | bytes 786436
  37.2 16.7 %copy-start.21 = (f32[1,1,512]{2,1,0:T(1,128)S(1)}, f32[1,1,512]{2,1,0:T(1,128)}, u32[]{:S(2)}) copy-start(f32[1,1,512]{2,1,0:T(1,128)} %param.23) | copy-start | bytes 6148
  37.2 16.9 %copy-start.27 = (bf16[256]{0:T(256)(128)(2,1)S(1)}, bf16[256]{0:T(256)(128)(2,1)}, u32[]{:S(2)}) copy-start(bf16[256]{0:T(256)(128)(2,1)} %param.22) | copy-start | bytes 1540
  37.2 17.4 %copy-start.18 = (bf16[256,256]{1,0:T(8,128)(2,1)S(1)}, bf16[256,256]{1,0:T(8,128)(2,1)}, u32[]{:S(2)}) copy-start(bf16[256,256]{1,0:T(8,128)(2,1)} %wo_ref.1) | copy-start | bytes 393220
  37.2 19.0 %copy-start.12 = (bf16[256,256]{1,0:T(8,128)(2,1)S(1)}, bf16[256,256]{1,0:T(8,128)(2,1)}, u32[]{:S(2)}) copy-start(bf16[256,256]{1,0:T(8,128)(2,1)} %param.20) | copy-start | bytes 393220
  37.2 19.0 %copy-start.14 = (bf16[256,256]{1,0:T(8,128)(2,1)S(1)}, bf16[256,256]{1,0:T(8,128)(2,1)}, u32[]{:S(2)}) copy-start(bf16[256,256]{1,0:T(8,128)(2,1)} %param.18) | copy-start | bytes 393220
  37.3 18.9 %copy-start.16 = (bf16[256,256]{1,0:T(8,128)(2,1)S(1)}, bf16[256,256]{1,0:T(8,128)(2,1)}, u32[]{:S(2)}) copy-start(bf16[256,256]{1,0:T(8,128)(2,1)} %param.19) | copy-start | bytes 393220
  37.3 44.3 %all-to-all-start = ((bf16[8,512,256]{2,1,0:T(8,128)(2,1)}), bf16[8,512,256]{2,1,0:T(8,128)(2,1)S(1)}, u32[]{:S(2)}, u32[]{:S(2)}) async-start(bf16[8,512,256]{2,1,0:T(8,128)(2,1)} %broadcast_in_dim.8), calls=%async_computation | async-start | bytes 4194304 | tf_op jit(solution)/shard_map/all_to_all | solution.py:122
  95.4 31.4 %all-to-all-start.1 = ((bf16[8,512,256]{2,1,0:T(8,128)(2,1)}), bf16[8,512,256]{2,1,0:T(8,128)(2,1)}, u32[]{:S(2)}, u32[]{:S(2)}) async-start(bf16[8,512,256]{2,1,0:T(8,128)(2,1)} %get-tuple-element.14.g_ref), calls=%async_computation.1 | async-start | bytes 4194304 | tf_op jit(solution)/shard_map/all_to_all | solution.py:238
  99.9 12.2 %copy-start.24 = (f32[256]{0:T(256)}, f32[256]{0:T(256)S(1)}, u32[]{:S(2)}) copy-start(f32[256]{0:T(256)S(1)} %convert_element_type.138) | copy-start | bytes 3076
  100.0 12.1 %copy-start.20 = (f32[512,256]{1,0:T(8,128)S(1)}, f32[512,256]{1,0:T(8,128)}, u32[]{:S(2)}) copy-start(f32[512,256]{1,0:T(8,128)} %get-tuple-element.13) | copy-start | bytes 1572868
  100.0 12.9 %copy-start.3 = (bf16[512,256]{1,0:T(8,128)(2,1)S(1)}, bf16[512,256]{1,0:T(8,128)(2,1)}, u32[]{:S(2)}) copy-start(bf16[512,256]{1,0:T(8,128)(2,1)} %copy-done.2) | copy-start | bytes 786436
  112.1 3.3 %copy-start.5 = (bf16[512,256]{1,0:T(8,128)(2,1)S(1)}, bf16[512,256]{1,0:T(8,128)(2,1)}, u32[]{:S(2)}) copy-start(bf16[512,256]{1,0:T(8,128)(2,1)} %shard_map.172) | copy-start | bytes 786436
  112.1 3.4 %copy-start.15 = (bf16[256,256]{1,0:T(8,128)(2,1)S(1)}, bf16[256,256]{1,0:T(8,128)(2,1)}, u32[]{:S(2)}) copy-start(bf16[256,256]{1,0:T(8,128)(2,1)} %param.18) | copy-start | bytes 393220
  126.8 15.5 %copy-start.17 = (bf16[256,256]{1,0:T(8,128)(2,1)S(1)}, bf16[256,256]{1,0:T(8,128)(2,1)}, u32[]{:S(2)}) copy-start(bf16[256,256]{1,0:T(8,128)(2,1)} %param.19) | copy-start | bytes 393220
  140.9 2.6 %copy-start.10 = (bf16[512,256]{1,0:T(8,128)(2,1)S(1)}, bf16[512,256]{1,0:T(8,128)(2,1)}, u32[]{:S(2)}) copy-start(bf16[512,256]{1,0:T(8,128)(2,1)} %get-tuple-element.16) | copy-start | bytes 786436
  140.9 2.8 %copy-start.8 = (f32[256,512]{0,1:T(8,128)S(1)}, f32[256,512]{0,1:T(8,128)}, u32[]{:S(2)}) copy-start(f32[256,512]{0,1:T(8,128)} %copy-done.7) | copy-start | bytes 1572868
  141.0 2.8 %copy-start.13 = (bf16[256,256]{1,0:T(8,128)(2,1)S(1)}, bf16[256,256]{1,0:T(8,128)(2,1)}, u32[]{:S(2)}) copy-start(bf16[256,256]{1,0:T(8,128)(2,1)} %param.20) | copy-start | bytes 393220
  142.3 1.9 copy-start.26
  144.2 3.3 %copy-start.23 = (f32[256]{0:T(256)S(1)}, f32[256]{0:T(256)}, u32[]{:S(2)}) copy-start(f32[256]{0:T(256)} %get-tuple-element.19) | copy-start | bytes 3076
  176.5 6.6 %copy-start.22 = (f32[512]{0:T(512)S(1)}, f32[512]{0:T(512)}, u32[]{:S(2)}) copy-start(f32[512]{0:T(512)} %get-tuple-element.20) | copy-start | bytes 6148
  177.7 21.1 %all-to-all-start.3 = ((bf16[128,21,128]{2,1,0:T(8,128)(2,1)}), bf16[128,21,128]{2,1,0:T(8,128)(2,1)S(1)}, u32[]{:S(2)}, u32[]{:S(2)}) async-start(bf16[128,21,128]{2,1,0:T(8,128)(2,1)} %broadcast_in_dim.11), calls=%async_computation.3 | async-start | bytes 1572864 | tf_op jit(solution)/shard_map/all_to_all | solution.py:134
  (3 other events, 2.9 us)

commit v11 on v10

--- a/solution.py
+++ b/solution.py
@@ -17,7 +17,7 @@
 
 EPS = 1e-06
 SHIFT = math.log(NT)
-KB = 1024
+KB = 2048
 
 def _nt(a, b):
     return lax.dot_general(a, b, (((1,), (1,)), ((), ())), preferred_element_type=jnp.float32)

time: 201 us -> 201 us (level)
  no operation moved by 1% of the time
where the time goes in v11:
time: 201 us; the launch traced here: 200 us
  waiting for transfers between devices  54.6 us (27%)
  starting transfers between devices  38.1 us (19%)
  Pallas kernels  36.4 us (18%)
  blocking collectives  28.6 us (14%)
  matrix products  23.5 us (12%)
  local copies, waits for them, and re-layouts  8.51 us (4%)
  other arithmetic  7.92 us (4%)
  between operations  2.65 us (1%)
    all_to_all x1, blocking collectives, all_reduce_a2a(): chunks = lax.all_to_all(rows_in, axes, 0, 0, tiled=True)  28.6 us
    all_to_all x1, waiting for transfers between devices, gather_tiles(): return lax.all_to_all(copies, axis, 0, 0, tiled=True)  24.1 us
    all_to_all x1, starting transfers between devices, gather_tiles(): return lax.all_to_all(copies, axis, 0, 0, tiled=True)  16.7 us
    all_to_all x1, waiting for transfers between devices, all_reduce_a2a(): return lax.all_to_all(copies, axes, 0, 0, tiled=True).astype(jnp.float32)  15 us
    pallas_call x1, Pallas kernels, attend_gkv(): pl.pallas_call(_gkv_kernel, out_shape=(sh, sh), scratch_shapes=[pltpu.VME...  14.2 us
    pallas_call x1, Pallas kernels, attend_gq(): pl.pallas_call(_gq_kernel, out_shape=jax.ShapeDtypeStruct(q.shape, jnp.bf...  12 us
    ppermute x4, starting transfers between devices, from_neighbour(): return lax.ppermute(array, axis, pairs)  11.5 us
    pallas_call x1, Pallas kernels, attend_fwd(): pl.pallas_call(_fwd_kernel, out_shape=outs, scratch_shapes=[pltpu.VMEM(q....  10.1 us
  transfers between devices with their start and end apart: 7, of which 4 were waited for; matrix products, arithmetic and copies ran while one was open for 10% of the time, Pallas kernels for 6%

profile of v11, /device:TPU:0, one launch (start us, length us, event | category | flops | bytes accessed | tf_op | source)
XLA Modules:
  0.0 200.3 jit_solution(5536223953426254730)
XLA Ops:
  1.5 2.1 %fusion.13 = bf16[1024,256]{1,0:T(8,128)(2,1)} fusion(f32[1024]{0:T(1024)S(1)} %fusion.54, bf16[1,1,1024,256]{3,2,1,0:T(8,128)(2,1)} %param.12), kind=kLoop, calls=%fused_computation.24 | loop fusion | flops 786432 | bytes 1052672 | tf_op jit(solution)/shard_map/convert_element_type | solution.py:185
  3.5 1.3 collective-permute-start.3
  4.8 6.9 %collective-permute-start.2 = (bf16[1024,256]{1,0:T(8,128)(2,1)}, bf16[1024,256]{1,0:T(8,128)(2,1)}, u32[]{:S(2)}, u32[]{:S(2)}) collective-permute-start(bf16[1024,256]{1,0:T(8,128)(2,1)} %fusion.13), channel_id=1, source_target_pairs={{0,1},{1,2},{2,3},{3,4},{4,5},{5,6},{6,7},{8,9},{9,10},{10,11},{11... | collective-permute-start | bytes 1572872 | tf_op jit(solution)/shard_map/ppermute | solution.py:116
  11.7 2.1 %collective-permute-start = (bf16[1024,256]{1,0:T(8,128)(2,1)}, bf16[1024,256]{1,0:T(8,128)(2,1)}, u32[]{:S(2)}, u32[]{:S(2)}) collective-permute-start(bf16[1024,256]{1,0:T(8,128)(2,1)} %fusion.13), channel_id=1, source_target_pairs={{0,8},{8,16},{16,24},{24,32},{32,40},{40,48},{48,56},{56,64},{64,7... | collective-permute-start | bytes 1572872 | tf_op jit(solution)/shard_map/ppermute | solution.py:116
  13.8 1.3 collective-permute-start.1
  15.1 1.8 reduce_sum.66
  16.9 1.3 fusion.5
  19.2 1.4 fusion.18
  20.7 7.0 %collective-permute-done.3 = bf16[1024,256]{1,0:T(8,128)(2,1)} collective-permute-done((bf16[1024,256]{1,0:T(8,128)(2,1)}, bf16[1024,256]{1,0:T(8,128)(2,1)}, u32[]{:S(2)}, u32[]{:S(2)}) %collective-permute-start.3) | collective-permute-done | bytes 524320 | tf_op jit(solution)/shard_map/ppermute | solution.py:116
  27.7 1.4 fusion.40
  29.1 1.3 fusion.41
  30.4 1.3 convolution_add_fusion.1
  31.8 1.5 fusion.6
  35.8 1.5 broadcast_in_dim.8
  37.3 16.7 %all-to-all-start = ((bf16[8,512,256]{2,1,0:T(8,128)(2,1)}), bf16[8,512,256]{2,1,0:T(8,128)(2,1)S(1)}, u32[]{:S(2)}, u32[]{:S(2)}) async-start(bf16[8,512,256]{2,1,0:T(8,128)(2,1)} %broadcast_in_dim.8), calls=%async_computation | async-start | bytes 4194304 | tf_op jit(solution)/shard_map/all_to_all | solution.py:122
  57.5 24.1 %all-to-all-done = bf16[8,512,256]{2,1,0:T(8,128)(2,1)S(1)} async-done(((bf16[8,512,256]{2,1,0:T(8,128)(2,1)}), bf16[8,512,256]{2,1,0:T(8,128)(2,1)S(1)}, u32[]{:S(2)}, u32[]{:S(2)}) %all-to-all-start) | async-done | bytes 2097184 | tf_op jit(solution)/shard_map/all_to_all | solution.py:122
  81.6 3.2 %convolution_convert_fusion.kv_ref = bf16[4096,512]{1,0:T(8,128)(2,1)} fusion(bf16[4096,256]{1,0:T(8,128)(2,1)S(1)} %bitcast.110, bf16[256,256]{1,0:T(8,128)(2,1)S(1)} %copy-done.12, bf16[256,256]{1,0:T(8,128)(2,1)S(1)} %copy-done.16), kind=kOutput, calls=%fused_computation | convolution fusion | flops 1076363264 | bytes 6553600 | tf_op jit(solution)/shard_map/dot_general | solution.py:166
  84.8 10.1 %shard_map.171 = (bf16[512,256]{1,0:T(8,128)(2,1)}, f32[512,256]{1,0:T(8,128)}, bf16[512,256]{1,0:T(8,128)(2,1)}, bf16[8,512,256]{2,1,0:T(8,128)(2,1)}) custom-call(bf16[512,256]{1,0:T(8,128)(2,1)} %get-tuple-element.28.q_ref, bf16[4096,512]{1,0:T(8,128)(2,1)} %convolution_convert_fusion.kv_ref, bf16[512,256]{1,0:T(8,128)(2,1)} %copy-done.2, ...), custom_call_target="tpu_custom_call" | custom-call | tf_op jit(solution)/shard_map/pallas_call | solution.py:99
  94.9 4.5 %all-to-all-start.1 = ((bf16[8,512,256]{2,1,0:T(8,128)(2,1)}), bf16[8,512,256]{2,1,0:T(8,128)(2,1)}, u32[]{:S(2)}, u32[]{:S(2)}) async-start(bf16[8,512,256]{2,1,0:T(8,128)(2,1)} %get-tuple-element.14.g_ref), calls=%async_computation.1 | async-start | bytes 4194304 | tf_op jit(solution)/shard_map/all_to_all | solution.py:238
  99.5 12.0 %shard_map.172 = bf16[512,256]{1,0:T(8,128)(2,1)} custom-call(bf16[512,256]{1,0:T(8,128)(2,1)} %get-tuple-element.28.q_ref, bf16[8,512,256]{2,1,0:T(8,128)(2,1)} %get-tuple-element.14.g_ref, bf16[4096,512]{1,0:T(8,128)(2,1)} %convolution_convert_fusion.kv_ref), custom_call_target="tpu_custom_call" | custom-call | tf_op jit(solution)/shard_map/pallas_call | solution.py:104
  112.3 1.2 fusion.65
  113.6 1.3 fusion.68
  115.8 2.1 %convolution_convert_fusion.1.q_ref = bf16[4096,256]{1,0:T(8,128)(2,1)} fusion(bf16[4096,256]{1,0:T(8,128)(2,1)S(1)} %bitcast.111, bf16[256,256]{1,0:T(8,128)(2,1)S(1)} %copy-done.15), kind=kOutput, calls=%fused_computation.1 | convolution fusion | flops 537919488 | bytes 4325376 | tf_op jit(solution)/shard_map/dot_general | solution.py:166
  117.9 8.4 %all-to-all-done.1 = bf16[8,512,256]{2,1,0:T(8,128)(2,1)} async-done(((bf16[8,512,256]{2,1,0:T(8,128)(2,1)}), bf16[8,512,256]{2,1,0:T(8,128)(2,1)}, u32[]{:S(2)}, u32[]{:S(2)}) %all-to-all-start.1) | async-done | bytes 2097184 | tf_op jit(solution)/shard_map/all_to_all | solution.py:238
  126.3 14.2 %shard_map.173 = (bf16[512,256]{1,0:T(8,128)(2,1)}, bf16[512,256]{1,0:T(8,128)(2,1)}) custom-call(bf16[4096,256]{1,0:T(8,128)(2,1)} %convolution_convert_fusion.1.q_ref, bf16[4096,256]{1,0:T(8,128)(2,1)} %bitcast.24.g_ref, bf16[512,256]{1,0:T(8,128)(2,1)} %get-tuple-element.27.k_ref, bf16[512,256]{1,0:T(8,128)(2,1)} %get-tuple-element.26.v_ref), custom_call_target="tpu_custom_call" | custom-call | tf_op jit(solution)/shard_map/pallas_call | solution.py:109
  140.5 1.3 fusion.66
  141.9 1.2 convolution_add_fusion.3
  143.8 3.2 %fusion.8 = f32[256,256]{1,0:T(8,128)S(1)} fusion(bf16[1024,256]{1,0:T(8,128)(2,1)} %bitcast.115, f32[1024,256]{1,0:T(8,128)} %copy-done.11, f32[1024]{0:T(1024)S(1)} %fusion.54, s32[1,1,512,1024]{3,2,1,0:T(8,128)} %param.15, f32[512,256]{1,0:T(8,128)S(1)} %get-tuple-element.32, f32[256,512]{0,1:T(8,128)S(1)} %copy-done.8, f32[512]{0:T(512)S(1)} %copy-done.26, ...), kind=kOutput, calls=%fused_computation.16 | convolution fusion | flops 406585344 | bytes 4990976 | tf_op jit(solution)/shard_map/gh,ge->he/dot_general | solution.py:255
  147.5 28.6 %all_to_all.20 = f32[128,21,128]{2,1,0:T(8,128)S(1)} all-to-all(f32[128,21,128]{2,1,0:T(8,128)S(1)} %reshape.145), channel_id=1, replica_groups=mesh['row'=16,'col'=8] {'row','col'}, dimensions={0} | all-to-all | bytes 2752512 | tf_op jit(solution)/shard_map/all_to_all | solution.py:131
  177.3 5.4 %all-to-all-start.3 = ((bf16[128,21,128]{2,1,0:T(8,128)(2,1)}), bf16[128,21,128]{2,1,0:T(8,128)(2,1)S(1)}, u32[]{:S(2)}, u32[]{:S(2)}) async-start(bf16[128,21,128]{2,1,0:T(8,128)(2,1)} %broadcast_in_dim.11), calls=%async_computation.3 | async-start | bytes 1572864 | tf_op jit(solution)/shard_map/all_to_all | solution.py:134
  183.3 15.0 %all-to-all-done.3 = bf16[128,21,128]{2,1,0:T(8,128)(2,1)S(1)} async-done(((bf16[128,21,128]{2,1,0:T(8,128)(2,1)}), bf16[128,21,128]{2,1,0:T(8,128)(2,1)S(1)}, u32[]{:S(2)}, u32[]{:S(2)}) %all-to-all-start.3) | async-done | bytes 688160 | tf_op jit(solution)/shard_map/all_to_all | solution.py:134
  198.6 1.1 fusion.61
  (90 shorter events, 11.8 us)
Async XLA Ops:
  0.6 32.7 %copy-start = (bf16[256,256]{1,0:T(8,128)(2,1)S(1)}, bf16[256,256]{1,0:T(8,128)(2,1)}, u32[]{:S(2)}) copy-start(bf16[256,256]{1,0:T(8,128)(2,1)} %param.17) | copy-start | bytes 393220
  0.6 16.2 %copy-start.1 = (s32[1,1,8,5,128,128]{5,4,3,2,1,0:T(8,128)S(1)}, s32[1,1,8,5,128,128]{5,4,3,2,1,0:T(8,128)}, u32[]{:S(2)}) copy-start(s32[1,1,8,5,128,128]{5,4,3,2,1,0:T(8,128)} %param.13) | copy-start | bytes 7864324
  3.5 24.1 %collective-permute-start.3 = (bf16[1024,256]{1,0:T(8,128)(2,1)}, bf16[1024,256]{1,0:T(8,128)(2,1)}, u32[]{:S(2)}, u32[]{:S(2)}) collective-permute-start(bf16[1024,256]{1,0:T(8,128)(2,1)} %fusion.13), channel_id=1, source_target_pairs={{1,0},{2,1},{3,2},{4,3},{5,4},{6,5},{7,6},{9,8},{10,9},{11,10},{12... | collective-permute-start | bytes 1572872 | tf_op jit(solution)/shard_map/ppermute | solution.py:116
  4.8 24.2 %collective-permute-start.2 = (bf16[1024,256]{1,0:T(8,128)(2,1)}, bf16[1024,256]{1,0:T(8,128)(2,1)}, u32[]{:S(2)}, u32[]{:S(2)}) collective-permute-start(bf16[1024,256]{1,0:T(8,128)(2,1)} %fusion.13), channel_id=1, source_target_pairs={{0,1},{1,2},{2,3},{3,4},{4,5},{5,6},{6,7},{8,9},{9,10},{10,11},{11... | collective-permute-start | bytes 1572872 | tf_op jit(solution)/shard_map/ppermute | solution.py:116
  11.7 18.7 %collective-permute-start = (bf16[1024,256]{1,0:T(8,128)(2,1)}, bf16[1024,256]{1,0:T(8,128)(2,1)}, u32[]{:S(2)}, u32[]{:S(2)}) collective-permute-start(bf16[1024,256]{1,0:T(8,128)(2,1)} %fusion.13), channel_id=1, source_target_pairs={{0,8},{8,16},{16,24},{24,32},{32,40},{40,48},{48,56},{56,64},{64,7... | collective-permute-start | bytes 1572872 | tf_op jit(solution)/shard_map/ppermute | solution.py:116
  13.8 18.0 %collective-permute-start.1 = (bf16[1024,256]{1,0:T(8,128)(2,1)}, bf16[1024,256]{1,0:T(8,128)(2,1)}, u32[]{:S(2)}, u32[]{:S(2)}) collective-permute-start(bf16[1024,256]{1,0:T(8,128)(2,1)} %fusion.13), channel_id=1, source_target_pairs={{8,0},{16,8},{24,16},{32,24},{40,32},{48,40},{56,48},{64,56},{72,6... | collective-permute-start | bytes 1572872 | tf_op jit(solution)/shard_map/ppermute | solution.py:116
  16.8 16.8 %copy-start.25 = (f32[512]{0:T(512)}, f32[512]{0:T(512)S(1)}, u32[]{:S(2)}) copy-start(f32[512]{0:T(512)S(1)} %convert_add_fusion.1) | copy-start | bytes 6148
  19.1 9.9 %copy-start.4 = (bf16[8,5,128,128]{3,2,0,1:T(8,128)(2,1)S(1)}, bf16[8,5,128,128]{3,2,0,1:T(8,128)(2,1)}, u32[]{:S(2)}) copy-start(bf16[8,5,128,128]{3,2,0,1:T(8,128)(2,1)} %fusion.5) | copy-start | bytes 3932164
  31.8 1.9 copy-start.9
  33.3 1.1 copy-start.19
  35.8 20.4 %copy-start.2 = (bf16[512,256]{1,0:T(8,128)(2,1)}, bf16[512,256]{1,0:T(8,128)(2,1)S(1)}, u32[]{:S(2)}) copy-start(bf16[512,256]{1,0:T(8,128)(2,1)S(1)} %fusion.19.tok_ref) | copy-start | bytes 786436
  37.2 16.7 %copy-start.21 = (f32[1,1,512]{2,1,0:T(1,128)S(1)}, f32[1,1,512]{2,1,0:T(1,128)}, u32[]{:S(2)}) copy-start(f32[1,1,512]{2,1,0:T(1,128)} %param.23) | copy-start | bytes 6148
  37.2 16.9 %copy-start.27 = (bf16[256]{0:T(256)(128)(2,1)S(1)}, bf16[256]{0:T(256)(128)(2,1)}, u32[]{:S(2)}) copy-start(bf16[256]{0:T(256)(128)(2,1)} %param.22) | copy-start | bytes 1540
  37.2 17.4 %copy-start.18 = (bf16[256,256]{1,0:T(8,128)(2,1)S(1)}, bf16[256,256]{1,0:T(8,128)(2,1)}, u32[]{:S(2)}) copy-start(bf16[256,256]{1,0:T(8,128)(2,1)} %wo_ref.1) | copy-start | bytes 393220
  37.2 19.0 %copy-start.12 = (bf16[256,256]{1,0:T(8,128)(2,1)S(1)}, bf16[256,256]{1,0:T(8,128)(2,1)}, u32[]{:S(2)}) copy-start(bf16[256,256]{1,0:T(8,128)(2,1)} %param.20) | copy-start | bytes 393220
  37.2 19.0 %copy-start.14 = (bf16[256,256]{1,0:T(8,128)(2,1)S(1)}, bf16[256,256]{1,0:T(8,128)(2,1)}, u32[]{:S(2)}) copy-start(bf16[256,256]{1,0:T(8,128)(2,1)} %param.18) | copy-start | bytes 393220
  37.3 18.9 %copy-start.16 = (bf16[256,256]{1,0:T(8,128)(2,1)S(1)}, bf16[256,256]{1,0:T(8,128)(2,1)}, u32[]{:S(2)}) copy-start(bf16[256,256]{1,0:T(8,128)(2,1)} %param.19) | copy-start | bytes 393220
  37.3 44.3 %all-to-all-start = ((bf16[8,512,256]{2,1,0:T(8,128)(2,1)}), bf16[8,512,256]{2,1,0:T(8,128)(2,1)S(1)}, u32[]{:S(2)}, u32[]{:S(2)}) async-start(bf16[8,512,256]{2,1,0:T(8,128)(2,1)} %broadcast_in_dim.8), calls=%async_computation | async-start | bytes 4194304 | tf_op jit(solution)/shard_map/all_to_all | solution.py:122
  94.9 31.4 %all-to-all-start.1 = ((bf16[8,512,256]{2,1,0:T(8,128)(2,1)}), bf16[8,512,256]{2,1,0:T(8,128)(2,1)}, u32[]{:S(2)}, u32[]{:S(2)}) async-start(bf16[8,512,256]{2,1,0:T(8,128)(2,1)} %get-tuple-element.14.g_ref), calls=%async_computation.1 | async-start | bytes 4194304 | tf_op jit(solution)/shard_map/all_to_all | solution.py:238
  99.4 12.1 %copy-start.24 = (f32[256]{0:T(256)}, f32[256]{0:T(256)S(1)}, u32[]{:S(2)}) copy-start(f32[256]{0:T(256)S(1)} %convert_element_type.138) | copy-start | bytes 3076
  99.5 12.1 %copy-start.20 = (f32[512,256]{1,0:T(8,128)S(1)}, f32[512,256]{1,0:T(8,128)}, u32[]{:S(2)}) copy-start(f32[512,256]{1,0:T(8,128)} %get-tuple-element.13) | copy-start | bytes 1572868
  99.5 12.9 %copy-start.3 = (bf16[512,256]{1,0:T(8,128)(2,1)S(1)}, bf16[512,256]{1,0:T(8,128)(2,1)}, u32[]{:S(2)}) copy-start(bf16[512,256]{1,0:T(8,128)(2,1)} %copy-done.2) | copy-start | bytes 786436
  111.5 3.4 %copy-start.5 = (bf16[512,256]{1,0:T(8,128)(2,1)S(1)}, bf16[512,256]{1,0:T(8,128)(2,1)}, u32[]{:S(2)}) copy-start(bf16[512,256]{1,0:T(8,128)(2,1)} %shard_map.172) | copy-start | bytes 786436
  111.5 3.4 %copy-start.15 = (bf16[256,256]{1,0:T(8,128)(2,1)S(1)}, bf16[256,256]{1,0:T(8,128)(2,1)}, u32[]{:S(2)}) copy-start(bf16[256,256]{1,0:T(8,128)(2,1)} %param.18) | copy-start | bytes 393220
  126.3 15.5 %copy-start.17 = (bf16[256,256]{1,0:T(8,128)(2,1)S(1)}, bf16[256,256]{1,0:T(8,128)(2,1)}, u32[]{:S(2)}) copy-start(bf16[256,256]{1,0:T(8,128)(2,1)} %param.19) | copy-start | bytes 393220
  140.5 2.6 %copy-start.10 = (bf16[512,256]{1,0:T(8,128)(2,1)S(1)}, bf16[512,256]{1,0:T(8,128)(2,1)}, u32[]{:S(2)}) copy-start(bf16[512,256]{1,0:T(8,128)(2,1)} %get-tuple-element.16) | copy-start | bytes 786436
  140.5 2.8 %copy-start.8 = (f32[256,512]{0,1:T(8,128)S(1)}, f32[256,512]{0,1:T(8,128)}, u32[]{:S(2)}) copy-start(f32[256,512]{0,1:T(8,128)} %copy-done.7) | copy-start | bytes 1572868
  140.5 2.8 %copy-start.13 = (bf16[256,256]{1,0:T(8,128)(2,1)S(1)}, bf16[256,256]{1,0:T(8,128)(2,1)}, u32[]{:S(2)}) copy-start(bf16[256,256]{1,0:T(8,128)(2,1)} %param.20) | copy-start | bytes 393220
  141.8 1.9 copy-start.26
  143.8 3.3 %copy-start.23 = (f32[256]{0:T(256)S(1)}, f32[256]{0:T(256)}, u32[]{:S(2)}) copy-start(f32[256]{0:T(256)} %get-tuple-element.19) | copy-start | bytes 3076
  176.1 6.6 %copy-start.22 = (f32[512]{0:T(512)S(1)}, f32[512]{0:T(512)}, u32[]{:S(2)}) copy-start(f32[512]{0:T(512)} %get-tuple-element.20) | copy-start | bytes 6148
  177.3 21.1 %all-to-all-start.3 = ((bf16[128,21,128]{2,1,0:T(8,128)(2,1)}), bf16[128,21,128]{2,1,0:T(8,128)(2,1)S(1)}, u32[]{:S(2)}, u32[]{:S(2)}) async-start(bf16[128,21,128]{2,1,0:T(8,128)(2,1)} %broadcast_in_dim.11), calls=%async_computation.3 | async-start | bytes 1572864 | tf_op jit(solution)/shard_map/all_to_all | solution.py:134
  (3 other events, 2.9 us)

commit v12 on v10

--- a/solution.py
+++ b/solution.py
@@ -71,7 +71,7 @@
     lax.fori_loop(0, blocks, step, 0)
     o_ref[...] = acc_ref[...].astype(o_ref.dtype)
 
-def _gkv_kernel(q_ref, g_ref, k_ref, v_ref, dk_ref, dv_ref, acck_ref, accv_ref):
+def _gkv_kernel(q_ref, g_ref, k_ref, v_ref, tt_ref, dk_ref, dv_ref, gk_ref, gv_ref, acck_ref, accv_ref):
     blocks = q_ref.shape[0] // KB
     acck_ref[...] = jnp.zeros_like(acck_ref)
     accv_ref[...] = jnp.zeros_like(accv_ref)
@@ -89,8 +89,12 @@
             accv_ref[:, cols] += _nn(w, g)
         return carry
     lax.fori_loop(0, blocks, step, 0)
-    dk_ref[...] = acck_ref[...].astype(dk_ref.dtype)
-    dv_ref[...] = accv_ref[...].astype(dv_ref.dtype)
+    grad_key = acck_ref[...].astype(jnp.bfloat16)
+    grad_val = accv_ref[...].astype(jnp.bfloat16)
+    dk_ref[...] = grad_key
+    dv_ref[...] = grad_val
+    gk_ref[...] = _nn(tt_ref[...], grad_key)
+    gv_ref[...] = _nn(tt_ref[...], grad_val)
 
 def attend_fwd(q, kv_all, tokens, grad_value, w_score, w_out, copies):
     bf16, f32 = jnp.bfloat16, jnp.float32
@@ -104,10 +108,12 @@
     return pl.pallas_call(_gq_kernel, out_shape=jax.ShapeDtypeStruct(q.shape, jnp.bfloat16),
         scratch_shapes=[pltpu.VMEM(q.shape, jnp.float32)])(q, g, kv_all)
 
-def attend_gkv(q_all, g_all, k, v):
+def attend_gkv(q_all, g_all, k, v, tokens_t):
     sh = jax.ShapeDtypeStruct(k.shape, jnp.bfloat16)
-    return pl.pallas_call(_gkv_kernel, out_shape=(sh, sh),
-        scratch_shapes=[pltpu.VMEM(k.shape, jnp.float32), pltpu.VMEM(k.shape, jnp.float32)],)(q_all, g_all, k, v)
+    gw = jax.ShapeDtypeStruct((H, H), jnp.float32)
+    return pl.pallas_call(_gkv_kernel, out_shape=(sh, sh, gw, gw),
+        scratch_shapes=[pltpu.VMEM(k.shape, jnp.float32), pltpu.VMEM(k.shape, jnp.float32)],
+        )(q_all, g_all, k, v, tokens_t)
 
 
 def from_neighbour(array, axis, step):
@@ -238,11 +244,11 @@
     grad_attn_all = lax.all_to_all(grad_attn_copies, "col", 0, 0, tiled=True).reshape(-1, H)
 
     grad_query = attend_gq(query_own, grad_attn_copies, kv_all)
-    grad_key, grad_val = attend_gkv(query_all, grad_attn_all, key_own, value_own)
+    grad_key, grad_val, g_key, g_value = attend_gkv(
+        query_all, grad_attn_all, key_own, value_own, tokens.T
+    )
 
     g_query = jnp.einsum("nh,ne->he", tokens, grad_query, preferred_element_type=jnp.float32)
-    g_key = jnp.einsum("nh,ne->he", tokens, grad_key, preferred_element_type=jnp.float32)
-    g_value = jnp.einsum("nh,ne->he", tokens, grad_val, preferred_element_type=jnp.float32)
     grad_tokens = grad_mixed + jnp.dot(grad_query, w_query.T, preferred_element_type=jnp.float32)
     grad_tokens = grad_tokens + jnp.dot(grad_key, w_key.T, preferred_element_type=jnp.float32)
     grad_tokens = grad_tokens + jnp.dot(grad_val, w_value.T, preferred_element_type=jnp.float32)

time: 201 us -> 207 us (1.030)
  waiting for transfers between devices: 54.5 us -> 47.6 us
  local copies, waits for them, and re-layouts: 8.51 us -> 13.2 us
  matrix products: 23.5 us -> 27.6 us
  other arithmetic: 7.92 us -> 11.9 us
    all_to_all x1, waiting for transfers between devices: 8.37 us -> 2.81 us  [body(): lax.all_to_all(grad_attn_copies, 'col', 0, 0, tiled=True).reshape(-1, H)]
    pallas_call x0 -> x1, local copies, waits for them, and re-layouts: none -> 2.08 us  [attend_fwd(): pl.pallas_call(_fwd_kernel, out_shape=outs, scratch_shapes=[pltpu.VMEM(q....]
  transfers between devices with their start and end apart: 7 -> 7, of which waited for: 4 -> 4; matrix products, arithmetic and copies ran while one was open for 10% -> 15% of each run, Pallas kernels for 6% -> 6%
where the time goes in v12:
time: 207 us; the launch traced here: 206 us
  waiting for transfers between devices  47.6 us (23%)
  starting transfers between devices  38 us (18%)
  Pallas kernels  37.2 us (18%)
  blocking collectives  28.2 us (14%)
  matrix products  27.6 us (13%)
  local copies, waits for them, and re-layouts  13.2 us (6%)
  other arithmetic  11.9 us (6%)
  between operations  2.36 us (1%)
    all_to_all x1, blocking collectives, all_reduce_a2a(): chunks = lax.all_to_all(rows_in, axes, 0, 0, tiled=True)  28.2 us
    all_to_all x1, waiting for transfers between devices, gather_tiles(): return lax.all_to_all(copies, axis, 0, 0, tiled=True)  22.7 us
    all_to_all x1, starting transfers between devices, gather_tiles(): return lax.all_to_all(copies, axis, 0, 0, tiled=True)  15.9 us
    all_to_all x1, waiting for transfers between devices, all_reduce_a2a(): return lax.all_to_all(copies, axes, 0, 0, tiled=True).astype(jnp.float32)  15 us
    pallas_call x1, Pallas kernels, attend_gkv(): pl.pallas_call(_gkv_kernel, out_shape=(sh, sh, gw, gw), scratch_shapes=[p...  14.5 us
    pallas_call x1, Pallas kernels, attend_gq(): pl.pallas_call(_gq_kernel, out_shape=jax.ShapeDtypeStruct(q.shape, jnp.bf...  12 us
    ppermute x4, starting transfers between devices, from_neighbour(): return lax.ppermute(array, axis, pairs)  12 us
    pallas_call x1, Pallas kernels, attend_fwd(): pl.pallas_call(_fwd_kernel, out_shape=outs, scratch_shapes=[pltpu.VMEM(q....  10.6 us
  transfers between devices with their start and end apart: 7, of which 4 were waited for; matrix products, arithmetic and copies ran while one was open for 15% of the time, Pallas kernels for 6%

profile of v12, /device:TPU:0, one launch (start us, length us, event | category | flops | bytes accessed | tf_op | source)
XLA Modules:
  0.0 206.1 jit_solution(17968978932208923552)
XLA Ops:
  1.3 2.0 fusion.13
  3.4 2.3 %collective-permute-start = (bf16[1024,256]{1,0:T(8,128)(2,1)}, bf16[1024,256]{1,0:T(8,128)(2,1)}, u32[]{:S(2)}, u32[]{:S(2)}) collective-permute-start(bf16[1024,256]{1,0:T(8,128)(2,1)} %fusion.13), channel_id=1, source_target_pairs={{0,8},{8,16},{16,24},{24,32},{32,40},{40,48},{48,56},{56,64},{64,7... | collective-permute-start | bytes 1572872 | tf_op jit(solution)/shard_map/ppermute | solution.py:122
  7.0 7.1 %collective-permute-start.2 = (bf16[1024,256]{1,0:T(8,128)(2,1)}, bf16[1024,256]{1,0:T(8,128)(2,1)}, u32[]{:S(2)}, u32[]{:S(2)}) collective-permute-start(bf16[1024,256]{1,0:T(8,128)(2,1)} %fusion.13), channel_id=1, source_target_pairs={{0,1},{1,2},{2,3},{3,4},{4,5},{5,6},{6,7},{8,9},{9,10},{10,11},{11... | collective-permute-start | bytes 1572872 | tf_op jit(solution)/shard_map/ppermute | solution.py:122
  15.4 3.1 %fusion.5 = bf16[8,5,128,128]{3,2,0,1:T(8,128)(2,1)} fusion(s32[1,1,8,5,128,128]{5,4,3,2,1,0:T(8,128)} %param.13), kind=kLoop, calls=%fused_computation.12 | loop fusion | flops 655360 | bytes 3932160 | tf_op jit(solution)/shard_map/convert.7
  18.5 1.8 reduce_sum.66
  21.2 1.4 fusion.18
  22.7 7.1 %collective-permute-done.3 = bf16[1024,256]{1,0:T(8,128)(2,1)} collective-permute-done((bf16[1024,256]{1,0:T(8,128)(2,1)}, bf16[1024,256]{1,0:T(8,128)(2,1)}, u32[]{:S(2)}, u32[]{:S(2)}) %collective-permute-start.3) | collective-permute-done | bytes 524320 | tf_op jit(solution)/shard_map/ppermute | solution.py:122
  29.7 1.4 fusion.40
  33.9 1.6 fusion.6
  37.0 1.5 broadcast_in_dim.8
  38.5 15.9 %all-to-all-start = ((bf16[8,512,256]{2,1,0:T(8,128)(2,1)}), bf16[8,512,256]{2,1,0:T(8,128)(2,1)S(1)}, u32[]{:S(2)}, u32[]{:S(2)}) async-start(bf16[8,512,256]{2,1,0:T(8,128)(2,1)} %broadcast_in_dim.8), calls=%async_computation | async-start | bytes 4194304 | tf_op jit(solution)/shard_map/all_to_all | solution.py:128
  54.6 1.7 copy.28
  58.3 1.4 convolution_convert_fusion.2
  60.5 22.7 %all-to-all-done = bf16[8,512,256]{2,1,0:T(8,128)(2,1)S(1)} async-done(((bf16[8,512,256]{2,1,0:T(8,128)(2,1)}), bf16[8,512,256]{2,1,0:T(8,128)(2,1)S(1)}, u32[]{:S(2)}, u32[]{:S(2)}) %all-to-all-start) | async-done | bytes 2097184 | tf_op jit(solution)/shard_map/all_to_all | solution.py:128
  83.2 3.2 %convolution_convert_fusion.kv_ref = bf16[4096,512]{1,0:T(8,128)(2,1)} fusion(bf16[4096,256]{1,0:T(8,128)(2,1)S(1)} %bitcast.106, bf16[256,256]{1,0:T(8,128)(2,1)S(1)} %copy-done.11, bf16[256,256]{1,0:T(8,128)(2,1)S(1)} %copy-done.13), kind=kOutput, calls=%fused_computation | convolution fusion | flops 1076363264 | bytes 6553600 | tf_op jit(solution)/shard_map/dot_general | solution.py:172
  86.4 10.6 %shard_map.171 = (bf16[512,256]{1,0:T(8,128)(2,1)}, f32[512,256]{1,0:T(8,128)}, bf16[512,256]{1,0:T(8,128)(2,1)}, bf16[8,512,256]{2,1,0:T(8,128)(2,1)}) custom-call(bf16[512,256]{1,0:T(8,128)(2,1)} %get-tuple-element.32.q_ref, bf16[4096,512]{1,0:T(8,128)(2,1)} %convolution_convert_fusion.kv_ref, bf16[512,256]{1,0:T(8,128)(2,1)} %copy-done.3, ...), custom_call_target="tpu_custom_call" | custom-call | tf_op jit(solution)/shard_map/pallas_call | solution.py:103
  97.1 4.7 %all-to-all-start.1 = ((bf16[8,512,256]{2,1,0:T(8,128)(2,1)}), bf16[8,512,256]{2,1,0:T(8,128)(2,1)}, u32[]{:S(2)}, u32[]{:S(2)}) async-start(bf16[8,512,256]{2,1,0:T(8,128)(2,1)} %get-tuple-element.16.g_ref), calls=%async_computation.1 | async-start | bytes 4194304 | tf_op jit(solution)/shard_map/all_to_all | solution.py:244
  102.6 12.0 %shard_map.172 = bf16[512,256]{1,0:T(8,128)(2,1)} custom-call(bf16[512,256]{1,0:T(8,128)(2,1)} %get-tuple-element.32.q_ref, bf16[8,512,256]{2,1,0:T(8,128)(2,1)} %get-tuple-element.16.g_ref, bf16[4096,512]{1,0:T(8,128)(2,1)} %convolution_convert_fusion.kv_ref), custom_call_target="tpu_custom_call" | custom-call | tf_op jit(solution)/shard_map/pallas_call | solution.py:108
  114.6 2.1 %copy.30 = f32[512,256]{0,1:T(8,128)} copy(f32[512,256]{1,0:T(8,128)} %get-tuple-element.15) | data formatting | bytes 1048576 | tf_op jit(solution)/shard_map/pallas_call | solution.py:103
  116.7 1.8 multiply_reduce_fusion
  119.7 2.0 fusion.66
  121.7 2.0 convolution_add_fusion.4
  123.6 3.0 %convolution_convert_fusion.1.q_ref = bf16[4096,256]{1,0:T(8,128)(2,1)} fusion(bf16[4096,256]{1,0:T(8,128)(2,1)S(1)} %bitcast.107, bf16[256,256]{1,0:T(8,128)(2,1)} %param.18), kind=kOutput, calls=%fused_computation.1 | convolution fusion | flops 537919488 | bytes 4325376 | tf_op jit(solution)/shard_map/dot_general | solution.py:172
  126.6 2.8 %all-to-all-done.1 = bf16[8,512,256]{2,1,0:T(8,128)(2,1)} async-done(((bf16[8,512,256]{2,1,0:T(8,128)(2,1)}), bf16[8,512,256]{2,1,0:T(8,128)(2,1)}, u32[]{:S(2)}, u32[]{:S(2)}) %all-to-all-start.1) | async-done | bytes 2097184 | tf_op jit(solution)/shard_map/all_to_all | solution.py:244
  129.4 14.5 %shard_map.173 = (bf16[512,256]{1,0:T(8,128)(2,1)}, bf16[512,256]{1,0:T(8,128)(2,1)}, f32[256,256]{1,0:T(8,128)}, f32[256,256]{1,0:T(8,128)}) custom-call(bf16[4096,256]{1,0:T(8,128)(2,1)} %convolution_convert_fusion.1.q_ref, bf16[4096,256]{1,0:T(8,128)(2,1)} %bitcast.24.g_ref, bf16[512,256]{1,0:T(8,128)(2,1)} %get-tuple-element.31.k_ref, ...), custom_call_target="tpu_custom_call" | custom-call | tf_op jit(solution)/shard_map/pallas_call | solution.py:114
  143.9 1.4 convolution_add_fusion.3
  145.3 2.1 %fusion.20 = (f32[512]{0:T(512)S(1)}, f32[512,256]{0,1:T(8,128)}) fusion(f32[256,512]{1,0:T(8,128)S(1)} %get-tuple-element.34, f32[512]{0:T(512)S(1)} %add_rsqrt_fusion, f32[512,256]{0,1:T(8,128)S(1)} %convolution_add_fusion.3, bf16[512,256]{1,0:T(8,128)(2,1)} %get-tuple-element.18, bf16[256,256]{1,0:T(8,128)(2,1)} %param.20, f32[512]{0:T(512)S(1)} %fusion.55), kind=kOutput, calls=%fused_computation.37 | convolution fusion | flops 67763712 | bytes 1972224 | tf_op jit(solution)/shard_map/dot_general | solution.py:254
  148.0 3.3 %fusion.8 = f32[256,256]{1,0:T(8,128)} fusion(bf16[1024,256]{1,0:T(8,128)(2,1)} %bitcast.111, f32[1024,256]{1,0:T(8,128)} %copy-done.10, f32[1024]{0:T(1024)S(1)} %fusion.54, s32[1,1,512,1024]{3,2,1,0:T(8,128)S(1)} %copy-done.7, f32[512,256]{0,1:T(8,128)} %get-tuple-element.36, f32[256,512]{1,0:T(8,128)S(1)} %get-tuple-element.34, f32[512]{0:T(512)} %copy-done.21, ...), kind=kOutput, calls=%fused_computation.16 | convolution fusion | flops 406585344 | bytes 4990976 | tf_op jit(solution)/shard_map/gh,ge->he/dot_general | solution.py:261
  151.3 2.2 %concatenate.12 = f32[1344,256]{1,0:T(8,128)S(1)} concatenate(f32[256,256]{1,0:T(8,128)} %fusion.8, f32[256,256]{1,0:T(8,128)S(1)} %fusion.65, f32[256,256]{1,0:T(8,128)S(1)} %copy-done.15, f32[256,256]{1,0:T(8,128)} %get-tuple-element.20, f32[256,256]{1,0:T(8,128)S(1)} %copy-done.9, f32[1,256]{1,0:T(1,128)S(1)} %bitcast.115, f32[63,256]{1,0:T(8,128)S(1)} %broadcast_in_dim.10), dimensions={0} | concatenate | bytes 2752512 | tf_op jit(solution)/shard_map/concatenate | solution.py:268
  153.7 28.2 %all_to_all.20 = f32[128,21,128]{2,1,0:T(8,128)S(1)} all-to-all(f32[128,21,128]{2,1,0:T(8,128)S(1)} %reshape.145), channel_id=1, replica_groups=mesh['row'=16,'col'=8] {'row','col'}, dimensions={0} | all-to-all | bytes 2752512 | tf_op jit(solution)/shard_map/all_to_all | solution.py:137
  183.1 5.4 %all-to-all-start.3 = ((bf16[128,21,128]{2,1,0:T(8,128)(2,1)}), bf16[128,21,128]{2,1,0:T(8,128)(2,1)S(1)}, u32[]{:S(2)}, u32[]{:S(2)}) async-start(bf16[128,21,128]{2,1,0:T(8,128)(2,1)} %broadcast_in_dim.11), calls=%async_computation.3 | async-start | bytes 1572864 | tf_op jit(solution)/shard_map/all_to_all | solution.py:140
  189.1 15.0 %all-to-all-done.3 = bf16[128,21,128]{2,1,0:T(8,128)(2,1)S(1)} async-done(((bf16[128,21,128]{2,1,0:T(8,128)(2,1)}), bf16[128,21,128]{2,1,0:T(8,128)(2,1)S(1)}, u32[]{:S(2)}, u32[]{:S(2)}) %all-to-all-start.3) | async-done | bytes 688160 | tf_op jit(solution)/shard_map/all_to_all | solution.py:140
  (81 shorter events, 16.5 us)
Async XLA Ops:
  0.6 34.8 %copy-start = (bf16[256,256]{1,0:T(8,128)(2,1)S(1)}, bf16[256,256]{1,0:T(8,128)(2,1)}, u32[]{:S(2)}) copy-start(bf16[256,256]{1,0:T(8,128)(2,1)} %param.17) | copy-start | bytes 393220
  3.4 17.6 %copy-start.1 = (s32[1,1,8,5,128,128]{5,4,3,2,1,0:T(8,128)S(1)}, s32[1,1,8,5,128,128]{5,4,3,2,1,0:T(8,128)}, u32[]{:S(2)}) copy-start(s32[1,1,8,5,128,128]{5,4,3,2,1,0:T(8,128)} %param.13) | copy-start | bytes 7864324
  3.4 29.1 %collective-permute-start = (bf16[1024,256]{1,0:T(8,128)(2,1)}, bf16[1024,256]{1,0:T(8,128)(2,1)}, u32[]{:S(2)}, u32[]{:S(2)}) collective-permute-start(bf16[1024,256]{1,0:T(8,128)(2,1)} %fusion.13), channel_id=1, source_target_pairs={{0,8},{8,16},{16,24},{24,32},{32,40},{40,48},{48,56},{56,64},{64,7... | collective-permute-start | bytes 1572872 | tf_op jit(solution)/shard_map/ppermute | solution.py:122
  5.7 24.0 %collective-permute-start.3 = (bf16[1024,256]{1,0:T(8,128)(2,1)}, bf16[1024,256]{1,0:T(8,128)(2,1)}, u32[]{:S(2)}, u32[]{:S(2)}) collective-permute-start(bf16[1024,256]{1,0:T(8,128)(2,1)} %fusion.13), channel_id=1, source_target_pairs={{1,0},{2,1},{3,2},{4,3},{5,4},{6,5},{7,6},{9,8},{10,9},{11,10},{12... | collective-permute-start | bytes 1572872 | tf_op jit(solution)/shard_map/ppermute | solution.py:122
  7.0 24.1 %collective-permute-start.2 = (bf16[1024,256]{1,0:T(8,128)(2,1)}, bf16[1024,256]{1,0:T(8,128)(2,1)}, u32[]{:S(2)}, u32[]{:S(2)}) collective-permute-start(bf16[1024,256]{1,0:T(8,128)(2,1)} %fusion.13), channel_id=1, source_target_pairs={{0,1},{1,2},{2,3},{3,4},{4,5},{5,6},{6,7},{8,9},{9,10},{10,11},{11... | collective-permute-start | bytes 1572872 | tf_op jit(solution)/shard_map/ppermute | solution.py:122
  14.1 19.8 %collective-permute-start.1 = (bf16[1024,256]{1,0:T(8,128)(2,1)}, bf16[1024,256]{1,0:T(8,128)(2,1)}, u32[]{:S(2)}, u32[]{:S(2)}) collective-permute-start(bf16[1024,256]{1,0:T(8,128)(2,1)} %fusion.13), channel_id=1, source_target_pairs={{8,0},{16,8},{24,16},{32,24},{40,32},{48,40},{56,48},{64,56},{72,6... | collective-permute-start | bytes 1572872 | tf_op jit(solution)/shard_map/ppermute | solution.py:122
  18.5 2.8 %copy-start.5 = (bf16[1,1,1024,256]{3,2,1,0:T(8,128)(2,1)S(1)}, bf16[1,1,1024,256]{3,2,1,0:T(8,128)(2,1)}, u32[]{:S(2)}) copy-start(bf16[1,1,1024,256]{3,2,1,0:T(8,128)(2,1)} %param.12) | copy-start | bytes 1572868
  20.3 15.4 %copy-start.21 = (f32[512]{0:T(512)}, f32[512]{0:T(512)S(1)}, u32[]{:S(2)}) copy-start(f32[512]{0:T(512)S(1)} %convert_add_fusion.1) | copy-start | bytes 6148
  21.2 9.9 %copy-start.2 = (bf16[8,5,128,128]{3,2,0,1:T(8,128)(2,1)S(1)}, bf16[8,5,128,128]{3,2,0,1:T(8,128)(2,1)}, u32[]{:S(2)}) copy-start(bf16[8,5,128,128]{3,2,0,1:T(8,128)(2,1)} %fusion.5) | copy-start | bytes 3932164
  33.8 1.9 copy-start.6
  35.4 1.2 copy-start.14
  35.7 1.1 copy-start.10
  37.0 1.5 copy-start.3
  38.5 16.0 %copy-start.16 = (f32[1,1,512]{2,1,0:T(1,128)S(1)}, f32[1,1,512]{2,1,0:T(1,128)}, u32[]{:S(2)}) copy-start(f32[1,1,512]{2,1,0:T(1,128)} %param.23) | copy-start | bytes 6148
  38.5 19.7 %copy-start.11 = (bf16[256,256]{1,0:T(8,128)(2,1)S(1)}, bf16[256,256]{1,0:T(8,128)(2,1)}, u32[]{:S(2)}) copy-start(bf16[256,256]{1,0:T(8,128)(2,1)} %param.20) | copy-start | bytes 393220
  38.5 19.7 %copy-start.12 = (bf16[256,256]{1,0:T(8,128)(2,1)S(1)}, bf16[256,256]{1,0:T(8,128)(2,1)}, u32[]{:S(2)}) copy-start(bf16[256,256]{1,0:T(8,128)(2,1)} %param.18) | copy-start | bytes 393220
  38.5 44.7 %all-to-all-start = ((bf16[8,512,256]{2,1,0:T(8,128)(2,1)}), bf16[8,512,256]{2,1,0:T(8,128)(2,1)S(1)}, u32[]{:S(2)}, u32[]{:S(2)}) async-start(bf16[8,512,256]{2,1,0:T(8,128)(2,1)} %broadcast_in_dim.8), calls=%async_computation | async-start | bytes 4194304 | tf_op jit(solution)/shard_map/all_to_all | solution.py:128
  58.3 25.0 %copy-start.13 = (bf16[256,256]{1,0:T(8,128)(2,1)S(1)}, bf16[256,256]{1,0:T(8,128)(2,1)}, u32[]{:S(2)}) copy-start(bf16[256,256]{1,0:T(8,128)(2,1)} %param.19) | copy-start | bytes 393220
  97.1 4.7 %copy-start.22 = (bf16[256]{0:T(256)(128)(2,1)S(1)}, bf16[256]{0:T(256)(128)(2,1)}, u32[]{:S(2)}) copy-start(bf16[256]{0:T(256)(128)(2,1)} %param.22) | copy-start | bytes 1540
  97.1 4.7 %copy-start.17 = (f32[1,1,512]{2,1,0:T(1,128)S(1)}, f32[1,1,512]{2,1,0:T(1,128)}, u32[]{:S(2)}) copy-start(f32[1,1,512]{2,1,0:T(1,128)} %param.23) | copy-start | bytes 6148
  97.1 32.4 %all-to-all-start.1 = ((bf16[8,512,256]{2,1,0:T(8,128)(2,1)}), bf16[8,512,256]{2,1,0:T(8,128)(2,1)}, u32[]{:S(2)}, u32[]{:S(2)}) async-start(bf16[8,512,256]{2,1,0:T(8,128)(2,1)} %get-tuple-element.16.g_ref), calls=%async_computation.1 | async-start | bytes 4194304 | tf_op jit(solution)/shard_map/all_to_all | solution.py:244
  101.8 14.9 %copy-start.20 = (f32[256]{0:T(256)}, f32[256]{0:T(256)S(1)}, u32[]{:S(2)}) copy-start(f32[256]{0:T(256)S(1)} %convert_element_type.140) | copy-start | bytes 3076
  114.6 7.1 %copy-start.4 = (bf16[512,256]{1,0:T(8,128)(2,1)S(1)}, bf16[512,256]{1,0:T(8,128)(2,1)}, u32[]{:S(2)}) copy-start(bf16[512,256]{1,0:T(8,128)(2,1)} %shard_map.172) | copy-start | bytes 786436
  129.4 14.5 %copy-start.8 = (f32[512,256]{0,1:T(8,128)S(1)}, f32[512,256]{0,1:T(8,128)}, u32[]{:S(2)}) copy-start(f32[512,256]{0,1:T(8,128)} %convolution_add_fusion.4) | copy-start | bytes 1572868
  143.9 4.1 %copy-start.7 = (s32[1,1,512,1024]{3,2,1,0:T(8,128)S(1)}, s32[1,1,512,1024]{3,2,1,0:T(8,128)}, u32[]{:S(2)}) copy-start(s32[1,1,512,1024]{3,2,1,0:T(8,128)} %param.15) | copy-start | bytes 6291460
  148.0 3.3 %copy-start.9 = (f32[256,256]{1,0:T(8,128)S(1)}, f32[256,256]{1,0:T(8,128)}, u32[]{:S(2)}) copy-start(f32[256,256]{1,0:T(8,128)} %fusion.66) | copy-start | bytes 786436
  148.0 3.3 %copy-start.15 = (f32[256,256]{1,0:T(8,128)S(1)}, f32[256,256]{1,0:T(8,128)}, u32[]{:S(2)}) copy-start(f32[256,256]{1,0:T(8,128)} %get-tuple-element.19) | copy-start | bytes 786436
  148.0 3.3 %copy-start.19 = (f32[256]{0:T(256)S(1)}, f32[256]{0:T(256)}, u32[]{:S(2)}) copy-start(f32[256]{0:T(256)} %get-tuple-element.23) | copy-start | bytes 3076
  181.9 6.6 %copy-start.18 = (f32[512]{0:T(512)S(1)}, f32[512]{0:T(512)}, u32[]{:S(2)}) copy-start(f32[512]{0:T(512)} %get-tuple-element.24) | copy-start | bytes 6148
  183.1 21.1 %all-to-all-start.3 = ((bf16[128,21,128]{2,1,0:T(8,128)(2,1)}), bf16[128,21,128]{2,1,0:T(8,128)(2,1)S(1)}, u32[]{:S(2)}, u32[]{:S(2)}) async-start(bf16[128,21,128]{2,1,0:T(8,128)(2,1)} %broadcast_in_dim.11), calls=%async_computation.3 | async-start | bytes 1572864 | tf_op jit(solution)/shard_map/all_to_all | solution.py:140
